TPU v7x, 32 devices: a whole 2x2x4 slice. The times are simulated.
32 devices in a mesh: dp: 8 (over z, core), rot: 4 (over y, x).
Axes of the slice: x: 2, y: 2, z: 4, core: 2. Of those that a mesh axis runs over, the one named last changes fastest.
Arguments:
- vectors: bfloat16 [2048, 4096], P('dp', 'rot'), may hold values from -100 to 100
- rotation: bfloat16 [4096, 4096], P('rot'), may hold values from -0.125 to 0.125
- codes: int32 [2048, 256], P('dp', 'rot'), may hold values from 0 to 255
Outputs:
- codebook: float32 [4096, 256], P('rot')
- new_rotation: bfloat16 [4096, 4096], P('rot', 'dp')
All inputs are finite; a program needn't handle non-finite values.
Results may differ from a plain program's by a relative error of at most 0.007.
Values may be sent and summed in bfloat16 or wider, within the bound.
No kernel may reach another device: no remote copies, remote signals or barrier semaphores. Data moves between devices by JAX's collectives and lax.ppermute only.
A program may use at most 64 MiB of HBM per device.

v0:
```python
import math

import jax
import jax.numpy as jnp
from jax import lax
from jax.sharding import PartitionSpec as P

K = 256
ITERS = 2


def body(vectors, rotation, codes):
    row_count, block_dims = vectors.shape
    width = rotation.shape[1]
    local_spaces = codes.shape[1]
    sub_dims = block_dims // local_spaces
    tile_cols = width // lax.axis_size("dp")
    col_first = lax.axis_index("dp") * tile_cols
    rotated_t = lax.psum_scatter(
        lax.dot_general(
            rotation, vectors, (((0,), (1,)), ((), ())), preferred_element_type=jnp.float32
        ),
        "rot",
        scatter_dimension=0,
        tiled=True,
    ).astype(jnp.bfloat16)
    code_ids = jnp.arange(K, dtype=jnp.int32)
    code_indicator = (codes.T[:, :, None] == code_ids[None, None, :]).astype(jnp.bfloat16)
    grouped_vectors = rotated_t.reshape(local_spaces, sub_dims, row_count)
    shard_code_sums = jnp.einsum(
        "vzo,voc->vzc", grouped_vectors, code_indicator, preferred_element_type=jnp.float32
    )
    local_counts = jnp.sum(code_indicator, axis=1, dtype=jnp.float32)
    total_sums, total_counts = lax.psum((shard_code_sums, local_counts), "dp")
    book = total_sums / jnp.maximum(total_counts, 1.0)[:, None, :]
    codebook = book.reshape(block_dims, K)
    codebook_batch = book.astype(jnp.bfloat16)
    reconstructed_transposed = jnp.einsum(
        "lyg,lxg->lyx", codebook_batch, code_indicator, preferred_element_type=jnp.float32
    )
    reconstructed_transposed = reconstructed_transposed.astype(jnp.bfloat16).reshape(
        block_dims, row_count
    )
    partial_cross = lax.dot_general(
        vectors,
        lax.all_gather(reconstructed_transposed, "rot", axis=0, tiled=True),
        (((0,), (1,)), ((), ())),
        preferred_element_type=jnp.float32,
    )
    cross_b = lax.psum(partial_cross, "dp").astype(jnp.bfloat16)

    def apply_gram(rows_b, gram_b):
        return jnp.dot(
            rows_b,
            lax.all_gather(gram_b, "rot", axis=0, tiled=True),
            preferred_element_type=jnp.float32,
        )

    rows_b = cross_b
    new_tile = None
    for iteration in range(ITERS):
        columns = lax.dynamic_slice_in_dim(rows_b, col_first, tile_cols, 1)
        gram_block = rows_b
        gram_part, columns = (
            lax.psum_scatter(
                lax.dot_general(
                    gram_block,
                    columns,
                    (((0,), (0,)), ((), ())),
                    preferred_element_type=jnp.float32,
                ),
                "rot",
                scatter_dimension=0,
                tiled=True,
            ),
            columns,
        )
        if iteration == 0:
            total = lax.psum(jnp.sum(gram_part * gram_part), ("dp", "rot"))
            factor = 1.7 / jnp.sqrt(jnp.sqrt(total))
            gram_b = (factor * factor * gram_part).astype(jnp.bfloat16)
            product = apply_gram(rows_b, gram_b)
            new_tile = factor * (1.5 * columns.astype(jnp.float32) - 0.5 * product)
        else:
            gram_b = gram_part.astype(jnp.bfloat16)
            product = apply_gram(rows_b, gram_b)
            new_tile = 1.5 * columns.astype(jnp.float32) - 0.5 * product
        if iteration + 1 < ITERS:
            rows_b = lax.all_gather(new_tile.astype(jnp.bfloat16), "dp", axis=1, tiled=True)
    new_rotation = (math.sqrt(width) * new_tile).astype(jnp.bfloat16)
    return (codebook, new_rotation)


def solution(mesh):
    return jax.shard_map(
        body,
        mesh=mesh,
        in_specs=(P("dp", "rot"), P("rot", None), P("dp", "rot")),
        out_specs=(P("rot", None), P("rot", "dp")),
        check_vma=False,
    )
```

profile of v0, /device:TPU:0, one launch (start us, length us, event | category | flops | bytes accessed | tf_op | source)
XLA Modules:
  0.0 976.6 jit_solution(6242302210182630783)
XLA Ops:
  7.2 0.0 copy-start
  7.2 0.0 reduce-scatter.4.cloned.1.call-start
  7.2 1.0 copy-done
  8.2 7.8 fusion.13
  16.0 0.0 copy-start.3
  16.0 0.0 reduce-scatter.4.cloned.1.call-update
  16.0 0.0 all-reduce.4.cloned.1.call-start
  16.1 0.8 copy-done.3
  16.8 3.4 convert_reduce_fusion
  20.3 51.3 %reduce-scatter.4.cloned.1.call-done = f32[1024,256]{1,0:T(8,128)} async-done(((f32[4096,256]{1,0:T(8,128)}), f32[1024,256]{1,0:T(8,128)}) %reduce-scatter.4.cloned.1.call-update) | async-done | bytes 1048592 | tf_op jit(solution)/shard_map/reduce_scatter | solution.py:19
  71.5 1.3 convert_element_type.36
  72.8 5.1 fusion.2
  77.9 0.0 all-reduce.4.cloned.1.call-update
  77.9 0.0 all-gather.5.cloned.1.call-start
  78.0 59.6 %all-reduce.4.cloned.1.call-done = (f32[64,16,256]{2,1,0:T(8,128)}, f32[64,256]{1,0:T(8,128)}) async-done(((f32[64,16,256]{2,1,0:T(8,128)}, f32[64,256]{1,0:T(8,128)}), (f32[64,16,256]{2,1,0:T(8,128)}, f32[64,256]{1,0:T(8,128)})) %all-reduce.4.cloned.1.call-update) | async-done | bytes 1114128 | tf_op jit(solution)/shard_map/psum | solution.py:34
  137.6 0.8 broadcast_maximum_fusion
  138.5 1.3 broadcast_divide_fusion
  139.8 0.0 copy-start.2
  139.8 5.0 fusion.5
  144.9 0.0 all-gather.5.cloned.1.call-update
  144.9 0.0 reduce-scatter.6.cloned.1.call-start
  144.9 34.3 %all-gather.5.cloned.1.call-done = bf16[4096,256]{1,0:T(8,128)(2,1)} async-done(((bf16[1024,256]{1,0:T(8,128)(2,1)}), bf16[4096,256]{1,0:T(8,128)(2,1)}) %all-gather.5.cloned.1.call-update) | async-done | bytes 2097168 | tf_op jit(solution)/shard_map/all_gather | solution.py:46
  179.2 9.7 convolution_bitcast_fusion
  188.9 0.0 copy-done.2
  188.9 330.2 %all-reduce.5 = bf16[1024,4096]{0,1:T(8,128)(2,1)} all-reduce(f32[1024,4096]{0,1:T(8,128)} %convolution_bitcast_fusion), channel_id=1, replica_groups=mesh['dp'=8,'rot'=4] {'dp'}, use_global_device_ids=true, to_apply=%region_4.0 | all-reduce | flops 4194304 | bytes 25165824 | tf_op jit(solution)/shard_map/psum | solution.py:50
  519.0 11.4 %fusion.8 = f32[4096,512]{1,0:T(8,128)} fusion(bf16[1024,4096]{0,1:T(8,128)(2,1)} %all-reduce.5, s32[]{:T(128)S(6)} %select_n.4), kind=kOutput, calls=%fused_computation.15 | convolution fusion | flops 4294967296 | bytes 17825796 | tf_op jit(solution)/shard_map/dot_general | solution.py:66
  530.4 0.0 reduce-scatter.6.cloned.1.call-update
  530.5 0.2 all-gather.7.cloned.1.call-start
  530.7 84.2 %reduce-scatter.6.cloned.1.call-done = f32[1024,512]{1,0:T(8,128)} async-done(((f32[4096,512]{1,0:T(8,128)}), f32[1024,512]{1,0:T(8,128)}) %reduce-scatter.6.cloned.1.call-update) | async-done | bytes 2097168 | tf_op jit(solution)/shard_map/reduce_scatter | solution.py:65
  614.9 2.7 multiply_reduce_fusion
  617.6 39.4 %psum.31 = f32[]{:T(128)} all-reduce(f32[]{:T(128)} %multiply_reduce_fusion), channel_id=1, replica_groups=mesh['dp'=8,'rot'=4] {'dp','rot'}, use_global_device_ids=true, to_apply=%region_7.0 | all-reduce | flops 1 | bytes 8 | tf_op jit(solution)/shard_map/psum | solution.py:79
  657.8 2.8 multiply_convert_fusion.2
  660.7 0.0 all-gather.7.cloned.1.call-update
  660.7 0.0 all-gather.9.cloned.1.call-start
  660.7 53.6 %all-gather.7.cloned.1.call-done = bf16[4096,512]{1,0:T(8,128)(2,1)} async-done(((bf16[1024,512]{1,0:T(8,128)(2,1)}), bf16[4096,512]{1,0:T(8,128)(2,1)}) %all-gather.7.cloned.1.call-update) | async-done | bytes 4194320 | tf_op jit(solution)/shard_map/all_gather | solution.py:55
  714.4 10.4 %multiply_convert_fusion.1 = bf16[1024,512]{0,1:T(8,128)(2,1)} fusion(bf16[1024,4096]{0,1:T(8,128)(2,1)} %all-reduce.5, bf16[4096,512]{1,0:T(8,128)(2,1)} %all-gather.7.cloned.1.call-done, f32[]{:T(128)S(6)} %div.13, s32[]{:T(128)S(6)} %select_n.4), kind=kOutput, calls=%fused_computation.9 | convolution fusion | flops 4298113024 | bytes 14680072 | tf_op jit(solution)/shard_map/dot_general | solution.py:53
  724.8 0.0 all-gather.9.cloned.1.call-update
  724.8 0.0 reduce-scatter.8.cloned.1.call-start
  724.9 82.1 %all-gather.9.cloned.1.call-done = bf16[1024,4096]{0,1:T(8,128)(2,1)} async-done(((bf16[1024,512]{0,1:T(8,128)(2,1)}), bf16[1024,4096]{0,1:T(8,128)(2,1)}) %all-gather.9.cloned.1.call-update) | async-done | bytes 8388624 | tf_op jit(solution)/shard_map/all_gather | solution.py:89
  807.0 11.4 %fusion.6 = f32[4096,512]{1,0:T(8,128)} fusion(bf16[1024,4096]{0,1:T(8,128)(2,1)} %all-gather.9.cloned.1.call-done, s32[]{:T(128)S(6)} %select_n.4), kind=kOutput, calls=%fused_computation.13 | convolution fusion | flops 4294967296 | bytes 17825796 | tf_op jit(solution)/shard_map/dot_general | solution.py:66
  818.4 0.0 reduce-scatter.8.cloned.1.call-update
  818.5 0.3 all-gather.11.cloned.1.call-start
  818.7 84.7 %reduce-scatter.8.cloned.1.call-done = f32[1024,512]{1,0:T(8,128)} async-done(((f32[4096,512]{1,0:T(8,128)}), f32[1024,512]{1,0:T(8,128)}) %reduce-scatter.8.cloned.1.call-update) | async-done | bytes 2097168 | tf_op jit(solution)/shard_map/reduce_scatter | solution.py:65
  903.4 2.7 convert_element_type.46
  906.1 0.0 all-gather.11.cloned.1.call-update
  906.1 52.7 %all-gather.11.cloned.1.call-done = bf16[4096,512]{1,0:T(8,128)(2,1)} async-done(((bf16[1024,512]{1,0:T(8,128)(2,1)}), bf16[4096,512]{1,0:T(8,128)(2,1)}) %all-gather.11.cloned.1.call-update) | async-done | bytes 4194320 | tf_op jit(solution)/shard_map/all_gather | solution.py:55
  958.9 0.0 copy-start.1
  958.9 9.5 multiply_convert_fusion
  968.4 1.3 copy.7
  969.7 0.0 copy-done.1
Async XLA Ops:
  7.2 1.1 copy-start
  7.2 64.4 %reduce-scatter.4.cloned.1.call-start = ((), (), s32[]{:S(2)}) async-start(), calls=%async_computation.3 | async-start | bytes 5242880 | tf_op jit(solution)/shard_map/reduce_scatter | solution.py:19
  16.0 0.8 copy-start.3
  16.0 121.6 %all-reduce.4.cloned.1.call-start = ((), (), s32[]{:S(2)}) async-start(), calls=%async_computation.10 | async-start | bytes 2228224 | tf_op jit(solution)/shard_map/psum | solution.py:34
  77.9 101.3 %all-gather.5.cloned.1.call-start = ((), (), s32[]{:S(2)}) async-start(), calls=%async_computation.4 | async-start | bytes 2621440 | tf_op jit(solution)/shard_map/all_gather | solution.py:46
  139.8 49.1 %copy-start.2 = (f32[64,16,256]{2,1,0:T(8,128)}, f32[64,16,256]{2,1,0:T(8,128)S(1)}, u32[]{:S(2)}) copy-start(f32[64,16,256]{2,1,0:T(8,128)S(1)} %broadcast_divide_fusion) | copy-start | bytes 3145732
  144.9 470.0 %reduce-scatter.6.cloned.1.call-start = ((), (), s32[]{:S(2)}) async-start(), calls=%async_computation.5 | async-start | bytes 10485760 | tf_op jit(solution)/shard_map/reduce_scatter | solution.py:65
  530.5 183.9 %all-gather.7.cloned.1.call-start = ((), (), s32[]{:S(2)}) async-start(), calls=%async_computation.6 | async-start | bytes 5242880 | tf_op jit(solution)/shard_map/all_gather | solution.py:55
  660.7 146.4 %all-gather.9.cloned.1.call-start = ((), (), s32[]{:S(2)}) async-start(), calls=%async_computation.7 | async-start | bytes 9437184 | tf_op jit(solution)/shard_map/all_gather | solution.py:89
  724.8 178.6 %reduce-scatter.8.cloned.1.call-start = ((), (), s32[]{:S(2)}) async-start(), calls=%async_computation.8 | async-start | bytes 10485760 | tf_op jit(solution)/shard_map/reduce_scatter | solution.py:65
  818.5 140.4 %all-gather.11.cloned.1.call-start = ((), (), s32[]{:S(2)}) async-start(), calls=%async_computation.9 | async-start | bytes 5242880 | tf_op jit(solution)/shard_map/all_gather | solution.py:55
  958.9 10.9 %copy-start.1 = (bf16[256,1024]{1,0:T(8,128)(2,1)S(1)}, bf16[256,1024]{1,0:T(8,128)(2,1)}, u32[]{:S(2)}) copy-start(bf16[256,1024]{1,0:T(8,128)(2,1)} %param.3) | copy-start | bytes 1572868
Sparse Core Ops, SparseCore 0:
  16.1 55.3 reduce-scatter.3
  78.1 59.5 all-reduce.3
  145.0 34.1 all-gather.4
  530.6 84.2 reduce-scatter.5
  660.8 53.5 all-gather.6
  725.0 82.0 all-gather.8
  818.6 84.7 reduce-scatter.7
  906.3 52.5 all-gather.10
where the time goes:
time: 977 us
  waiting for transfers between devices  503 us (51%)
  blocking collectives  370 us (38%)
  matrix products  70.4 us (7%)
  other arithmetic  15.1 us (2%)
  between operations  14.9 us (2%)
    psum x1, blocking collectives, body(): cross_b = lax.psum(partial_cross, 'dp').astype(jnp.bfloat16)  330 us
    reduce_scatter x2, waiting for transfers between devices, body(): lax.psum_scatter(lax.dot_general(gram_block, columns, (((0,), (0,)), ((),...  169 us
    all_gather x2, waiting for transfers between devices, apply_gram(): lax.all_gather(gram_b, 'rot', axis=0, tiled=True)  106 us
    all_gather x1, waiting for transfers between devices, body(): lax.all_gather(new_tile.astype(jnp.bfloat16), 'dp', axis=1, tiled=True)  82.1 us
    psum x1, waiting for transfers between devices, body(): total_sums, total_counts = lax.psum((shard_code_sums, local_counts), 'dp')  59.6 us
    reduce_scatter x1, waiting for transfers between devices, body(): lax.psum_scatter(lax.dot_general(rotation, vectors, (((0,), (1,)), ((), (...  51.3 us
    psum x1, blocking collectives, body(): total = lax.psum(jnp.sum(gram_part * gram_part), ('dp', 'rot'))  39.4 us
    all_gather x1, waiting for transfers between devices, body(): lax.all_gather(reconstructed_transposed, 'rot', axis=0, tiled=True)  34.3 us
  transfers between devices with their start and end apart: 8, of which 8 were waited for; matrix products, arithmetic and copies ran while one was open for 0% of the time, Pallas kernels for 0%

commit v1 on v0

v1 whole, which is shorter than its diff:
```python
import math

import jax
import jax.numpy as jnp
from jax import lax
from jax.sharding import PartitionSpec as P

K = 256
ITERS = 2


def body(vectors, rotation, codes):
    row_count, block_dims = vectors.shape
    width = rotation.shape[1]
    local_spaces = codes.shape[1]
    sub_dims = block_dims // local_spaces
    tile_cols = width // lax.axis_size("dp")
    tile_spaces = tile_cols // sub_dims
    dp_index = lax.axis_index("dp")
    code_ids = jnp.arange(K, dtype=jnp.int32)

    all_vectors = lax.all_gather(vectors, "dp", axis=0, tiled=True)
    all_codes = lax.all_gather(
        lax.all_gather(codes, "rot", axis=1, tiled=True), "dp", axis=0, tiled=True
    )
    tile_codes = lax.dynamic_slice_in_dim(all_codes, dp_index * tile_spaces, tile_spaces, 1)

    rotated_t = lax.psum_scatter(
        lax.dot_general(
            rotation, vectors, (((0,), (1,)), ((), ())), preferred_element_type=jnp.float32
        ),
        "rot",
        scatter_dimension=0,
        tiled=True,
    ).astype(jnp.bfloat16)
    code_indicator = (codes.T[:, :, None] == code_ids[None, None, :]).astype(jnp.bfloat16)
    grouped_vectors = rotated_t.reshape(local_spaces, sub_dims, row_count)
    shard_code_sums = jnp.einsum(
        "vzo,voc->vzc", grouped_vectors, code_indicator, preferred_element_type=jnp.float32
    )
    local_counts = jnp.sum(code_indicator, axis=1, dtype=jnp.float32)
    total_sums, total_counts = lax.psum((shard_code_sums, local_counts), "dp")
    book = total_sums / jnp.maximum(total_counts, 1.0)[:, None, :]
    codebook = book.reshape(block_dims, K)
    codebook_batch = lax.all_gather(book.astype(jnp.bfloat16), "rot", axis=0, tiled=True)
    tile_book = lax.dynamic_slice_in_dim(codebook_batch, dp_index * tile_spaces, tile_spaces, 0)

    tile_indicator = (tile_codes.T[:, :, None] == code_ids[None, None, :]).astype(jnp.bfloat16)
    rebuilt_t = jnp.einsum(
        "lyg,lxg->lyx", tile_book, tile_indicator, preferred_element_type=jnp.float32
    )
    rebuilt_t = rebuilt_t.astype(jnp.bfloat16).reshape(tile_cols, all_vectors.shape[0])
    cross_tile = lax.dot_general(
        all_vectors, rebuilt_t, (((0,), (1,)), ((), ())), preferred_element_type=jnp.float32
    ).astype(jnp.bfloat16)

    def apply_gram(rows_b, gram_b):
        return jnp.dot(
            rows_b,
            lax.all_gather(gram_b, "rot", axis=0, tiled=True),
            preferred_element_type=jnp.float32,
        )

    columns = cross_tile
    new_tile = None
    for iteration in range(ITERS):
        rows_b = lax.all_gather(columns, "dp", axis=1, tiled=True)
        gram_part = lax.psum_scatter(
            lax.dot_general(
                rows_b,
                columns,
                (((0,), (0,)), ((), ())),
                preferred_element_type=jnp.float32,
            ),
            "rot",
            scatter_dimension=0,
            tiled=True,
        )
        if iteration == 0:
            total = lax.psum(jnp.sum(gram_part * gram_part), ("dp", "rot"))
            factor = 1.7 / jnp.sqrt(jnp.sqrt(total))
            gram_b = (factor * factor * gram_part).astype(jnp.bfloat16)
            product = apply_gram(rows_b, gram_b)
            new_tile = factor * (1.5 * columns.astype(jnp.float32) - 0.5 * product)
        else:
            gram_b = gram_part.astype(jnp.bfloat16)
            product = apply_gram(rows_b, gram_b)
            new_tile = 1.5 * columns.astype(jnp.float32) - 0.5 * product
        columns = new_tile.astype(jnp.bfloat16)
    new_rotation = (math.sqrt(width) * new_tile).astype(jnp.bfloat16)
    return (codebook, new_rotation)


def solution(mesh):
    return jax.shard_map(
        body,
        mesh=mesh,
        in_specs=(P("dp", "rot"), P("rot", None), P("dp", "rot")),
        out_specs=(P("rot", None), P("rot", "dp")),
        check_vma=False,
    )
```

time: 977 us -> 796 us (0.81)
  blocking collectives: 370 us -> 49.1 us
  waiting for transfers between devices: 503 us -> 634 us
    psum x1 -> x0, blocking collectives: 330 us -> none  [body(): cross_b = lax.psum(partial_cross, 'dp').astype(jnp.bfloat16)]
    all_gather x2 -> x5, waiting for transfers between devices: 116 us -> 256 us  [the longest x2 163 us: body(): rows_b = lax.all_gather(columns, 'dp', axis=1, tiled=True)]
  transfers between devices with their start and end apart: 8 -> 11, of which waited for: 8 -> 11; matrix products, arithmetic and copies ran while one was open for 0% -> 3% of each run, Pallas kernels for 0% -> 0%
where the time goes in v1:
time: 796 us; the launch traced here: 795 us
  waiting for transfers between devices  634 us (80%)
  matrix products  76.7 us (10%)
  blocking collectives  49.1 us (6%)
  other arithmetic  16.4 us (2%)
  between operations  14.6 us (2%)
    reduce_scatter x2, waiting for transfers between devices, body(): lax.psum_scatter(lax.dot_general(rows_b, columns, (((0,), (0,)), ((), ())...  170 us
    all_gather x2, waiting for transfers between devices, body(): rows_b = lax.all_gather(columns, 'dp', axis=1, tiled=True)  163 us
    all_gather x2, waiting for transfers between devices, apply_gram(): lax.all_gather(gram_b, 'rot', axis=0, tiled=True)  106 us
    reduce_scatter x1, waiting for transfers between devices, body(): lax.psum_scatter(lax.dot_general(rotation, vectors, (((0,), (1,)), ((), (...  51.2 us
    psum x1, waiting for transfers between devices, body(): total_sums, total_counts = lax.psum((shard_code_sums, local_counts), 'dp')  50.1 us
    psum x1, blocking collectives, body(): total = lax.psum(jnp.sum(gram_part * gram_part), ('dp', 'rot'))  39.6 us
    all_gather x1, waiting for transfers between devices, body(): lax.all_gather(book.astype(jnp.bfloat16), 'rot', axis=0, tiled=True)  35.9 us
    all_gather x1, waiting for transfers between devices, body(): all_vectors = lax.all_gather(vectors, 'dp', axis=0, tiled=True)  31.3 us
  transfers between devices with their start and end apart: 11, of which 11 were waited for; matrix products, arithmetic and copies ran while one was open for 3% of the time, Pallas kernels for 0%

profile of v1, /device:TPU:0, one launch (start us, length us, event | category | flops | bytes accessed | tf_op | source)
XLA Modules:
  0.0 795.4 jit_solution(2216298243052583868)
XLA Ops:
  7.2 0.0 reduce-scatter.4.cloned.1.call-start
  7.2 7.9 fusion.9
  15.1 0.0 copy-start.2
  15.1 0.0 reduce-scatter.4.cloned.1.call-update
  15.1 0.0 all-reduce.3.cloned.1.call-start
  15.1 0.8 copy-done.2
  15.9 3.4 convert_reduce_fusion
  19.3 51.2 %reduce-scatter.4.cloned.1.call-done = f32[1024,256]{1,0:T(8,128)} async-done(((f32[4096,256]{1,0:T(8,128)}), f32[1024,256]{1,0:T(8,128)}) %reduce-scatter.4.cloned.1.call-update) | async-done | bytes 1048592 | tf_op jit(solution)/shard_map/reduce_scatter | solution.py:28
  70.6 1.3 convert_element_type.40
  71.8 5.1 fusion.3
  77.0 0.0 all-reduce.3.cloned.1.call-update
  77.0 0.0 all-gather.10.cloned.1.call-start
  77.0 9.6 %all_gather.25 = s32[256,256]{0,1:T(8,128)} all-gather(s32[256,64]{0,1:T(8,128)S(1)} %copy-done.2), channel_id=1, replica_groups=mesh['dp'=8,'rot'=4] {'rot'}, dimensions={1}, use_global_device_ids=true | all-gather | bytes 327680 | tf_op jit(solution)/shard_map/all_gather | solution.py:24
  86.6 0.0 all-gather.10.cloned.1.call-update
  86.6 0.0 all-gather.8.cloned.1.call-start
  86.7 50.1 %all-reduce.3.cloned.1.call-done = (f32[64,16,256]{2,1,0:T(8,128)}, f32[64,256]{1,0:T(8,128)}) async-done(((f32[64,16,256]{2,1,0:T(8,128)}, f32[64,256]{1,0:T(8,128)}), (f32[64,16,256]{2,1,0:T(8,128)}, f32[64,256]{1,0:T(8,128)})) %all-reduce.3.cloned.1.call-update) | async-done | bytes 1114128 | tf_op jit(solution)/shard_map/psum | solution.py:42
  136.7 0.8 broadcast_maximum_fusion
  137.6 2.5 fusion.8
  140.1 0.0 all-gather.8.cloned.1.call-update
  140.1 0.0 all-gather.12.cloned.1.call-start
  140.2 0.5 all-gather.12.cloned.1.call-update
  140.7 0.0 all-gather.14.cloned.1.call-start
  140.8 25.8 %all-gather.10.cloned.1.call-done = s32[2048,256]{0,1:T(8,128)} async-done(((s32[256,256]{0,1:T(8,128)}), s32[2048,256]{0,1:T(8,128)}) %all-gather.10.cloned.1.call-update) | async-done | bytes 2097168 | tf_op jit(solution)/shard_map/all_gather | solution.py:23
  166.5 1.0 dynamic-slice_bitcast_fusion
  167.5 35.9 %all-gather.8.cloned.1.call-done = bf16[256,16,256]{2,1,0:T(8,128)(2,1)} async-done(((bf16[64,16,256]{2,1,0:T(8,128)(2,1)}), bf16[256,16,256]{2,1,0:T(8,128)(2,1)}) %all-gather.8.cloned.1.call-update) | async-done | bytes 2097168 | tf_op jit(solution)/shard_map/all_gather | solution.py:45
  203.4 1.0 fusion.28
  204.4 16.1 %fusion.5 = bf16[32,16,2048]{2,1,0:T(8,128)(2,1)S(1)} fusion(s32[32,2048]{1,0:T(8,128)S(1)} %dynamic-slice_bitcast_fusion, bf16[32,16,256]{2,1,0:T(8,128)(2,1)S(1)} %fusion.28), kind=kOutput, calls=%fused_computation.8 | convolution fusion | flops 554696704 | bytes 2621440 | tf_op jit(solution)/shard_map/lyg,lxg->lyx/dot_general | solution.py:49
  220.5 31.3 %all-gather.12.cloned.1.call-done = bf16[2048,1024]{1,0:T(8,128)(2,1)} async-done(((bf16[256,1024]{1,0:T(8,128)(2,1)}), bf16[2048,1024]{1,0:T(8,128)(2,1)}) %all-gather.12.cloned.1.call-update) | async-done | bytes 4194320 | tf_op jit(solution)/shard_map/all_gather | solution.py:22
  251.8 5.5 convolution_convert_fusion
  257.2 0.0 all-gather.14.cloned.1.call-update
  257.3 0.0 reduce-scatter.6.cloned.1.call-start
  257.3 81.0 %all-gather.14.cloned.1.call-done = bf16[1024,4096]{0,1:T(8,128)(2,1)} async-done(((bf16[1024,512]{0,1:T(8,128)(2,1)}), bf16[1024,4096]{0,1:T(8,128)(2,1)}) %all-gather.14.cloned.1.call-update) | async-done | bytes 8388624 | tf_op jit(solution)/shard_map/all_gather | solution.py:67
  338.3 11.4 %fusion.10 = f32[4096,512]{1,0:T(8,128)} fusion(bf16[1024,4096]{0,1:T(8,128)(2,1)} %all-gather.14.cloned.1.call-done, bf16[512,1024]{1,0:T(8,128)(2,1)} %convolution_convert_fusion), kind=kOutput, calls=%fused_computation.21 | convolution fusion | flops 4294967296 | bytes 17825792 | tf_op jit(solution)/shard_map/dot_general | solution.py:69
  349.7 0.0 reduce-scatter.6.cloned.1.call-update
  349.7 0.0 copy-start
  349.7 0.0 all-gather.16.cloned.1.call-start
  349.8 84.9 %reduce-scatter.6.cloned.1.call-done = f32[1024,512]{1,0:T(8,128)} async-done(((f32[4096,512]{1,0:T(8,128)}), f32[1024,512]{1,0:T(8,128)}) %reduce-scatter.6.cloned.1.call-update) | async-done | bytes 2097168 | tf_op jit(solution)/shard_map/reduce_scatter | solution.py:68
  434.7 2.7 multiply_reduce_fusion
  437.4 39.6 %psum.23 = f32[]{:T(128)} all-reduce(f32[]{:T(128)} %multiply_reduce_fusion), channel_id=1, replica_groups=mesh['dp'=8,'rot'=4] {'dp','rot'}, use_global_device_ids=true, to_apply=%region_6.0 | all-reduce | flops 1 | bytes 8 | tf_op jit(solution)/shard_map/psum | solution.py:80
  477.6 2.9 multiply_convert_fusion.2
  480.5 0.0 all-gather.16.cloned.1.call-update
  480.5 0.0 all-gather.18.cloned.1.call-start
  480.6 53.6 %all-gather.16.cloned.1.call-done = bf16[4096,512]{1,0:T(8,128)(2,1)} async-done(((bf16[1024,512]{1,0:T(8,128)(2,1)}), bf16[4096,512]{1,0:T(8,128)(2,1)}) %all-gather.16.cloned.1.call-update) | async-done | bytes 4194320 | tf_op jit(solution)/shard_map/all_gather | solution.py:60
  534.1 0.0 copy-done
  534.1 10.1 %multiply_convert_fusion.1 = bf16[1024,512]{0,1:T(8,128)(2,1)} fusion(bf16[1024,4096]{0,1:T(8,128)(2,1)} %all-gather.14.cloned.1.call-done, bf16[4096,512]{1,0:T(8,128)(2,1)} %all-gather.16.cloned.1.call-done, f32[]{:T(128)S(6)} %div.13, bf16[512,1024]{1,0:T(8,128)(2,1)S(1)} %copy-done), kind=kOutput, calls=%fused_computation.10 | convolution fusion | flops 4298113024 | bytes 14680068 | tf_op jit(solution)/shard_map/dot_general | solution.py:58
  544.3 0.0 all-gather.18.cloned.1.call-update
  544.3 0.0 reduce-scatter.8.cloned.1.call-start
  544.4 82.1 %all-gather.18.cloned.1.call-done = bf16[1024,4096]{0,1:T(8,128)(2,1)} async-done(((bf16[1024,512]{0,1:T(8,128)(2,1)}), bf16[1024,4096]{0,1:T(8,128)(2,1)}) %all-gather.18.cloned.1.call-update) | async-done | bytes 8388624 | tf_op jit(solution)/shard_map/all_gather | solution.py:67
  626.5 11.4 %fusion.11 = f32[4096,512]{1,0:T(8,128)} fusion(bf16[1024,4096]{0,1:T(8,128)(2,1)} %all-gather.18.cloned.1.call-done, bf16[1024,512]{0,1:T(8,128)(2,1)} %multiply_convert_fusion.1), kind=kOutput, calls=%fused_computation.22 | convolution fusion | flops 4294967296 | bytes 17825792 | tf_op jit(solution)/shard_map/dot_general | solution.py:69
  637.9 0.0 reduce-scatter.8.cloned.1.call-update
  637.9 0.0 copy-start.1
  637.9 0.3 all-gather.20.cloned.1.call-start
  638.2 84.7 %reduce-scatter.8.cloned.1.call-done = f32[1024,512]{1,0:T(8,128)} async-done(((f32[4096,512]{1,0:T(8,128)}), f32[1024,512]{1,0:T(8,128)}) %reduce-scatter.8.cloned.1.call-update) | async-done | bytes 2097168 | tf_op jit(solution)/shard_map/reduce_scatter | solution.py:68
  722.9 2.8 convert_element_type.51
  725.7 0.0 all-gather.20.cloned.1.call-update
  725.7 52.7 %all-gather.20.cloned.1.call-done = bf16[4096,512]{1,0:T(8,128)(2,1)} async-done(((bf16[1024,512]{1,0:T(8,128)(2,1)}), bf16[4096,512]{1,0:T(8,128)(2,1)}) %all-gather.20.cloned.1.call-update) | async-done | bytes 4194320 | tf_op jit(solution)/shard_map/all_gather | solution.py:60
  778.4 0.0 copy-done.1
  778.4 9.2 %multiply_convert_fusion = bf16[1024,512]{0,1:T(8,128)(2,1)S(1)} fusion(bf16[1024,512]{0,1:T(8,128)(2,1)S(1)} %copy-done.1, bf16[1024,4096]{0,1:T(8,128)(2,1)} %all-gather.18.cloned.1.call-done, bf16[4096,512]{1,0:T(8,128)(2,1)} %all-gather.20.cloned.1.call-done), kind=kOutput, calls=%fused_computation.9 | convolution fusion | flops 4298113024 | bytes 14680064 | tf_op jit(solution)/shard_map/dot_general | solution.py:58
  787.6 1.3 copy.10
Async XLA Ops:
  7.2 63.4 %reduce-scatter.4.cloned.1.call-start = ((), (), s32[]{:S(2)}) async-start(), calls=%async_computation.3 | async-start | bytes 5242880 | tf_op jit(solution)/shard_map/reduce_scatter | solution.py:28
  15.1 0.8 copy-start.2
  15.1 121.6 %all-reduce.3.cloned.1.call-start = ((), (), s32[]{:S(2)}) async-start(), calls=%async_computation.13 | async-start | bytes 2228224 | tf_op jit(solution)/shard_map/psum | solution.py:42
  77.0 89.6 %all-gather.10.cloned.1.call-start = ((), (), s32[]{:S(2)}) async-start(), calls=%async_computation.5 | async-start | bytes 2359296 | tf_op jit(solution)/shard_map/all_gather | solution.py:23
  86.6 116.8 %all-gather.8.cloned.1.call-start = ((), (), s32[]{:S(2)}) async-start(), calls=%async_computation.4 | async-start | bytes 2621440 | tf_op jit(solution)/shard_map/all_gather | solution.py:45
  140.1 111.6 %all-gather.12.cloned.1.call-start = ((), (), s32[]{:S(2)}) async-start(), calls=%async_computation.6 | async-start | bytes 4718592 | tf_op jit(solution)/shard_map/all_gather | solution.py:22
  140.7 197.6 %all-gather.14.cloned.1.call-start = ((), (), s32[]{:S(2)}) async-start(), calls=%async_computation.7 | async-start | bytes 9437184 | tf_op jit(solution)/shard_map/all_gather | solution.py:67
  257.3 177.4 %reduce-scatter.6.cloned.1.call-start = ((), (), s32[]{:S(2)}) async-start(), calls=%async_computation.8 | async-start | bytes 10485760 | tf_op jit(solution)/shard_map/reduce_scatter | solution.py:68
  349.7 184.4 %copy-start = (bf16[512,1024]{1,0:T(8,128)(2,1)S(1)}, bf16[512,1024]{1,0:T(8,128)(2,1)}, u32[]{:S(2)}) copy-start(bf16[512,1024]{1,0:T(8,128)(2,1)} %convolution_convert_fusion) | copy-start | bytes 3145732
  349.7 184.4 %all-gather.16.cloned.1.call-start = ((), (), s32[]{:S(2)}) async-start(), calls=%async_computation.9 | async-start | bytes 5242880 | tf_op jit(solution)/shard_map/all_gather | solution.py:60
  480.5 146.0 %all-gather.18.cloned.1.call-start = ((), (), s32[]{:S(2)}) async-start(), calls=%async_computation.10 | async-start | bytes 9437184 | tf_op jit(solution)/shard_map/all_gather | solution.py:67
  544.3 178.6 %reduce-scatter.8.cloned.1.call-start = ((), (), s32[]{:S(2)}) async-start(), calls=%async_computation.11 | async-start | bytes 10485760 | tf_op jit(solution)/shard_map/reduce_scatter | solution.py:68
  637.9 140.5 %copy-start.1 = (bf16[1024,512]{0,1:T(8,128)(2,1)S(1)}, bf16[1024,512]{0,1:T(8,128)(2,1)}, u32[]{:S(2)}) copy-start(bf16[1024,512]{0,1:T(8,128)(2,1)} %multiply_convert_fusion.1) | copy-start | bytes 3145732
  637.9 140.4 %all-gather.20.cloned.1.call-start = ((), (), s32[]{:S(2)}) async-start(), calls=%async_computation.12 | async-start | bytes 5242880 | tf_op jit(solution)/shard_map/all_gather | solution.py:60
Sparse Core Ops, SparseCore 0:
  15.2 55.3 reduce-scatter.3
  77.1 59.5 all-reduce.2
  138.3 28.1 all-gather.9
  168.8 34.5 all-gather.7
  204.9 46.8 all-gather.11
  257.4 80.8 all-gather.13
  349.8 84.7 reduce-scatter.5
  480.6 53.4 all-gather.15
  544.4 82.0 all-gather.17
  638.1 84.7 reduce-scatter.7
  725.8 52.5 all-gather.19

commit v2 on v1

--- a/solution.py
+++ b/solution.py
@@ -19,11 +19,23 @@
     dp_index = lax.axis_index("dp")
     code_ids = jnp.arange(K, dtype=jnp.int32)
 
-    all_vectors = lax.all_gather(vectors, "dp", axis=0, tiled=True)
-    all_codes = lax.all_gather(
-        lax.all_gather(codes, "rot", axis=1, tiled=True), "dp", axis=0, tiled=True
-    )
-    tile_codes = lax.dynamic_slice_in_dim(all_codes, dp_index * tile_spaces, tile_spaces, 1)
+    dp_size = lax.axis_size("dp")
+    row_codes = lax.all_gather(codes, "rot", axis=1, tiled=True)
+    vector_parts = [vectors]
+    code_parts = [lax.dynamic_slice_in_dim(row_codes, dp_index * tile_spaces, tile_spaces, 1)]
+    for shift in range(1, dp_size):
+        pairs = [(i, (i + shift) % dp_size) for i in range(dp_size)]
+        target = (dp_index + shift) % dp_size
+        vector_parts.append(lax.ppermute(vectors, "dp", pairs))
+        code_parts.append(
+            lax.ppermute(
+                lax.dynamic_slice_in_dim(row_codes, target * tile_spaces, tile_spaces, 1),
+                "dp",
+                pairs,
+            )
+        )
+    all_vectors = jnp.concatenate(vector_parts, axis=0)
+    tile_codes = jnp.concatenate(code_parts, axis=0)
 
     rotated_t = lax.psum_scatter(
         lax.dot_general(
@@ -79,9 +91,10 @@
         if iteration == 0:
             total = lax.psum(jnp.sum(gram_part * gram_part), ("dp", "rot"))
             factor = 1.7 / jnp.sqrt(jnp.sqrt(total))
-            gram_b = (factor * factor * gram_part).astype(jnp.bfloat16)
-            product = apply_gram(rows_b, gram_b)
-            new_tile = factor * (1.5 * columns.astype(jnp.float32) - 0.5 * product)
+            product = apply_gram(rows_b, gram_part.astype(jnp.bfloat16))
+            new_tile = factor * (
+                1.5 * columns.astype(jnp.float32) - 0.5 * (factor * factor) * product
+            )
         else:
             gram_b = gram_part.astype(jnp.bfloat16)
             product = apply_gram(rows_b, gram_b)

time: 796 us -> 783 us (0.984)
  waiting for transfers between devices: 634 us -> 582 us
  starting transfers between devices: 0.67 us -> 32.4 us
    ppermute x0 -> x14, waiting for transfers between devices: none -> 64.3 us  [the longest x7 42.2 us: body(): lax.ppermute(lax.dynamic_slice_in_dim(row_codes, target * tile_spaces, ti...]
    all_gather x2 -> x0, waiting for transfers between devices: 57.1 us -> none  [the longest x1 31.3 us: body(): all_vectors = lax.all_gather(vectors, 'dp', axis=0, tiled=True)]
    all_gather x2, waiting for transfers between devices: 106 us -> 65 us  [apply_gram(): lax.all_gather(gram_b, 'rot', axis=0, tiled=True)]
    all_gather x1, waiting for transfers between devices: 35.9 us -> 0.01 us  [body(): lax.all_gather(book.astype(jnp.bfloat16), 'rot', axis=0, tiled=True)]
    ppermute x0 -> x14, starting transfers between devices: none -> 31.7 us  [the longest x7 23.1 us: body(): lax.ppermute(lax.dynamic_slice_in_dim(row_codes, target * tile_spaces, ti...]
    psum x1, waiting for transfers between devices: 50.1 us -> 59.7 us  [body(): total_sums, total_counts = lax.psum((shard_code_sums, local_counts), 'dp')]
    all_gather x2, waiting for transfers between devices: 163 us -> 172 us  [body(): rows_b = lax.all_gather(columns, 'dp', axis=1, tiled=True)]
  transfers between devices with their start and end apart: 11 -> 23, of which waited for: 11 -> 18; matrix products, arithmetic and copies ran while one was open for 3% -> 1% of each run, Pallas kernels for 0% -> 0%
where the time goes in v2:
time: 783 us; the launch traced here: 782 us
  waiting for transfers between devices  582 us (74%)
  matrix products  77.6 us (10%)
  blocking collectives  51.5 us (7%)
  starting transfers between devices  32.4 us (4%)
  other arithmetic  15.2 us (2%)
  between operations  14.6 us (2%)
  local copies, waits for them, and re-layouts  8.48 us (1%)
    all_gather x2, waiting for transfers between devices, body(): rows_b = lax.all_gather(columns, 'dp', axis=1, tiled=True)  172 us
    reduce_scatter x2, waiting for transfers between devices, body(): lax.psum_scatter(lax.dot_general(rows_b, columns, (((0,), (0,)), ((), ())...  170 us
    all_gather x2, waiting for transfers between devices, apply_gram(): lax.all_gather(gram_b, 'rot', axis=0, tiled=True)  65 us
    psum x1, waiting for transfers between devices, body(): total_sums, total_counts = lax.psum((shard_code_sums, local_counts), 'dp')  59.7 us
    reduce_scatter x1, waiting for transfers between devices, body(): lax.psum_scatter(lax.dot_general(rotation, vectors, (((0,), (1,)), ((), (...  51.2 us
    ppermute x7, waiting for transfers between devices, body(): lax.ppermute(lax.dynamic_slice_in_dim(row_codes, target * tile_spaces, ti...  42.2 us
    psum x1, blocking collectives, body(): total = lax.psum(jnp.sum(gram_part * gram_part), ('dp', 'rot'))  40.5 us
    ppermute x7, starting transfers between devices, body(): lax.ppermute(lax.dynamic_slice_in_dim(row_codes, target * tile_spaces, ti...  23.1 us
  transfers between devices with their start and end apart: 23, of which 18 were waited for; matrix products, arithmetic and copies ran while one was open for 1% of the time, Pallas kernels for 0%

profile of v2, /device:TPU:0, one launch (start us, length us, event | category | flops | bytes accessed | tf_op | source)
XLA Modules:
  0.0 782.1 jit_solution(17895046792326193594)
XLA Ops:
  7.2 0.0 reduce-scatter.4.cloned.1.call-start
  7.2 7.9 %fusion.9 = f32[4096,256]{1,0:T(8,128)} fusion(bf16[1024,4096]{1,0:T(8,128)(2,1)} %param.4, bf16[256,1024]{1,0:T(8,128)(2,1)} %param.3), kind=kOutput, calls=%fused_computation.41 | convolution fusion | flops 2147483648 | bytes 13107200 | tf_op jit(solution)/shard_map/dot_general | solution.py:41
  15.1 0.0 all-reduce.3.cloned.1.call-start
  15.1 0.8 copy-done.3
  15.9 3.4 convert_reduce_fusion
  19.3 51.2 %reduce-scatter.4.cloned.1.call-done = f32[1024,256]{1,0:T(8,128)} async-done(((f32[4096,256]{1,0:T(8,128)}), f32[1024,256]{1,0:T(8,128)}) %reduce-scatter.4.cloned.1.call-update) | async-done | bytes 1048592 | tf_op jit(solution)/shard_map/reduce_scatter | solution.py:40
  70.6 1.3 convert_element_type.37
  71.9 5.1 fusion.3
  77.0 0.0 all-reduce.3.cloned.1.call-update
  77.0 0.0 all-gather.6.cloned.1.call-start
  77.0 59.7 %all-reduce.3.cloned.1.call-done = (f32[64,16,256]{2,1,0:T(8,128)}, f32[64,256]{1,0:T(8,128)}) async-done(((f32[64,16,256]{2,1,0:T(8,128)}, f32[64,256]{1,0:T(8,128)}), (f32[64,16,256]{2,1,0:T(8,128)}, f32[64,256]{1,0:T(8,128)})) %all-reduce.3.cloned.1.call-update) | async-done | bytes 1114128 | tf_op jit(solution)/shard_map/psum | solution.py:54
  136.7 0.8 broadcast_maximum_fusion
  137.6 2.5 fusion.8
  140.1 0.0 all-gather.8.cloned.1.call-start
  140.2 1.5 collective-permute-start.3
  141.7 0.4 collective-permute-start.1
  142.2 1.5 collective-permute-start
  143.7 11.0 %all_gather.19 = s32[256,256]{0,1:T(8,128)S(1)} all-gather(s32[256,64]{0,1:T(8,128)S(1)} %copy-done.3), channel_id=1, replica_groups=mesh['dp'=8,'rot'=4] {'rot'}, dimensions={1}, use_global_device_ids=true | all-gather | bytes 327680 | tf_op jit(solution)/shard_map/all_gather | solution.py:23
  154.7 0.1 collective-permute-start.7
  154.8 0.8 constant_dynamic-update-slice_fusion.7
  155.7 26.4 %collective-permute-done.7 = s32[256,32]{0,1:T(8,128)S(1)} collective-permute-done((s32[256,32]{0,1:T(8,128)S(1)}, s32[256,32]{0,1:T(8,128)S(1)}, u32[]{:S(2)}, u32[]{:S(2)}) %collective-permute-start.7) | collective-permute-done | bytes 32800 | tf_op jit(solution)/shard_map/ppermute | solution.py:31
  182.0 5.8 collective-permute-done.8
  187.8 12.3 %collective-permute-start.9 = (s32[256,32]{0,1:T(8,128)S(1)}, s32[256,32]{0,1:T(8,128)S(1)}, u32[]{:S(2)}, u32[]{:S(2)}) collective-permute-start(s32[256,32]{0,1:T(8,128)S(1)} %get-tuple-element.12), channel_id=1, source_target_pairs={{0,12},{4,16},{8,20},{12,24},{16,28},{20,0},{24,4},{28,8},{1,13},{... | collective-permute-start | bytes 98312 | tf_op jit(solution)/shard_map/ppermute | solution.py:31
  200.1 1.6 collective-permute-done.9
  201.7 6.0 collective-permute-start.10
  207.7 1.9 collective-permute-done.10
  209.6 3.3 collective-permute-done.11
  212.9 4.2 collective-permute-start.12
  217.1 1.6 collective-permute-done.12
  218.7 0.6 collective-permute-start.13
  219.3 1.6 collective-permute-done.13
  220.9 3.8 collective-permute-start.4
  224.7 0.8 constant_dynamic-update-slice_fusion.6
  225.6 1.2 collective-permute-start.6
  226.8 0.8 constant_dynamic-update-slice_fusion.5
  227.7 0.8 constant_dynamic-update-slice_fusion.4
  228.5 0.8 constant_dynamic-update-slice_fusion.3
  229.3 7.7 collective-permute-done.4
  237.1 0.8 constant_dynamic-update-slice_fusion.2
  237.9 9.6 %collective-permute-done.5 = bf16[256,1024]{1,0:T(8,128)(2,1)S(1)} collective-permute-done((bf16[256,1024]{1,0:T(8,128)(2,1)S(1)}, bf16[256,1024]{1,0:T(8,128)(2,1)S(1)}, u32[]{:S(2)}, u32[]{:S(2)}) %collective-permute-start.5) | collective-permute-done | bytes 524320 | tf_op jit(solution)/shard_map/ppermute | solution.py:29
  247.5 0.8 constant_dynamic-update-slice_fusion.1
  248.3 4.8 collective-permute-done.6
  253.1 0.8 constant_dynamic-update-slice_fusion
  253.9 1.0 fusion.28
  254.9 16.1 %fusion.5 = bf16[32,16,2048]{2,1,0:T(8,128)(2,1)S(1)} fusion(s32[32,2048]{1,0:T(8,128)S(1)} %bitcast.23, bf16[32,16,256]{2,1,0:T(8,128)(2,1)S(1)} %fusion.28), kind=kOutput, calls=%fused_computation.8 | convolution fusion | flops 554696704 | bytes 2621440 | tf_op jit(solution)/shard_map/lyg,lxg->lyx/dot_general | solution.py:61
  271.0 5.6 convolution_convert_fusion
  276.6 0.2 reduce-scatter.6.cloned.1.call-start
  276.8 90.2 %all-gather.8.cloned.1.call-done = bf16[1024,4096]{1,0:T(8,128)(2,1)} async-done(((bf16[1024,512]{1,0:T(8,128)(2,1)}), bf16[1024,4096]{1,0:T(8,128)(2,1)}) %all-gather.8.cloned.1.call-update) | async-done | bytes 8388624 | tf_op jit(solution)/shard_map/all_gather | solution.py:79
  367.0 11.4 %fusion.10 = f32[4096,512]{1,0:T(8,128)} fusion(bf16[1024,4096]{1,0:T(8,128)(2,1)} %all-gather.8.cloned.1.call-done, bf16[1024,512]{1,0:T(8,128)(2,1)} %convolution_convert_fusion), kind=kOutput, calls=%fused_computation.42 | convolution fusion | flops 4294967296 | bytes 17825792 | tf_op jit(solution)/shard_map/dot_general | solution.py:81
  378.4 0.0 all-gather.10.cloned.1.call-start
  378.5 84.9 %reduce-scatter.6.cloned.1.call-done = f32[1024,512]{1,0:T(8,128)} async-done(((f32[4096,512]{1,0:T(8,128)}), f32[1024,512]{1,0:T(8,128)}) %reduce-scatter.6.cloned.1.call-update) | async-done | bytes 2097168 | tf_op jit(solution)/shard_map/reduce_scatter | solution.py:80
  463.4 4.4 multiply_reduce_fusion
  467.8 0.0 all-gather.12.cloned.1.call-start
  467.8 40.5 %psum.23 = f32[]{:T(128)} all-reduce(f32[]{:T(128)} %get-tuple-element.6), channel_id=1, replica_groups=mesh['dp'=8,'rot'=4] {'dp','rot'}, use_global_device_ids=true, to_apply=%region_6.7 | all-reduce | flops 1 | bytes 8 | tf_op jit(solution)/shard_map/psum | solution.py:92
  509.0 12.3 %all-gather.10.cloned.1.call-done = bf16[4096,512]{1,0:T(8,128)(2,1)} async-done(((bf16[1024,512]{1,0:T(8,128)(2,1)}), bf16[4096,512]{1,0:T(8,128)(2,1)}) %all-gather.10.cloned.1.call-update) | async-done | bytes 4194320 | tf_op jit(solution)/shard_map/all_gather | solution.py:72
  521.3 10.1 %multiply_convert_fusion.1 = bf16[1024,512]{1,0:T(8,128)(2,1)} fusion(bf16[1024,512]{1,0:T(8,128)(2,1)S(1)} %copy-done, bf16[1024,4096]{1,0:T(8,128)(2,1)} %all-gather.8.cloned.1.call-done, bf16[4096,512]{1,0:T(8,128)(2,1)} %all-gather.10.cloned.1.call-done, f32[]{:T(128)S(6)} %mul.76, f32[]{:T(128)S(6)} %div.13), kind=kOutput, calls=%fused_computation.10 | convolution fusion | flops 4298113024 | bytes 14680072 | tf_op jit(solution)/shard_map/dot_general | solution.py:70
  531.4 0.3 reduce-scatter.8.cloned.1.call-start
  531.7 81.9 %all-gather.12.cloned.1.call-done = bf16[1024,4096]{1,0:T(8,128)(2,1)} async-done(((bf16[1024,512]{1,0:T(8,128)(2,1)}), bf16[1024,4096]{1,0:T(8,128)(2,1)}) %all-gather.12.cloned.1.call-update) | async-done | bytes 8388624 | tf_op jit(solution)/shard_map/all_gather | solution.py:79
  613.6 11.4 %fusion.11 = f32[4096,512]{1,0:T(8,128)} fusion(bf16[1024,4096]{1,0:T(8,128)(2,1)} %all-gather.12.cloned.1.call-done, bf16[1024,512]{1,0:T(8,128)(2,1)} %multiply_convert_fusion.1), kind=kOutput, calls=%fused_computation.43 | convolution fusion | flops 4294967296 | bytes 17825792 | tf_op jit(solution)/shard_map/dot_general | solution.py:81
  625.0 0.0 all-gather.14.cloned.1.call-start
  625.1 84.9 %reduce-scatter.8.cloned.1.call-done = f32[1024,512]{1,0:T(8,128)} async-done(((f32[4096,512]{1,0:T(8,128)}), f32[1024,512]{1,0:T(8,128)}) %reduce-scatter.8.cloned.1.call-update) | async-done | bytes 2097168 | tf_op jit(solution)/shard_map/reduce_scatter | solution.py:80
  710.0 2.7 convert_element_type.47
  712.7 52.7 %all-gather.14.cloned.1.call-done = bf16[4096,512]{1,0:T(8,128)(2,1)} async-done(((bf16[1024,512]{1,0:T(8,128)(2,1)}), bf16[4096,512]{1,0:T(8,128)(2,1)}) %all-gather.14.cloned.1.call-update) | async-done | bytes 4194320 | tf_op jit(solution)/shard_map/all_gather | solution.py:72
  765.5 10.1 %multiply_convert_fusion = bf16[1024,512]{1,0:T(8,128)(2,1)} fusion(bf16[1024,512]{1,0:T(8,128)(2,1)S(1)} %copy-done.1, bf16[1024,4096]{1,0:T(8,128)(2,1)} %all-gather.12.cloned.1.call-done, bf16[4096,512]{1,0:T(8,128)(2,1)} %all-gather.14.cloned.1.call-done), kind=kOutput, calls=%fused_computation.9 | convolution fusion | flops 4298113024 | bytes 14680064 | tf_op jit(solution)/shard_map/dot_general | solution.py:70
  (32 shorter events, 0.2 us)
Async XLA Ops:
  7.2 63.4 %reduce-scatter.4.cloned.1.call-start = ((), (), s32[]{:S(2)}) async-start(), calls=%async_computation.3 | async-start | bytes 5242880 | tf_op jit(solution)/shard_map/reduce_scatter | solution.py:40
  15.1 0.8 copy-start.3
  15.1 121.7 %all-reduce.3.cloned.1.call-start = ((), (), s32[]{:S(2)}) async-start(), calls=%async_computation.11 | async-start | bytes 2228224 | tf_op jit(solution)/shard_map/psum | solution.py:54
  71.8 68.3 %copy-start.2 = (bf16[256,1024]{1,0:T(8,128)(2,1)S(1)}, bf16[256,1024]{1,0:T(8,128)(2,1)}, u32[]{:S(2)}) copy-start(bf16[256,1024]{1,0:T(8,128)(2,1)} %param.3) | copy-start | bytes 1572868
  77.0 176.9 %all-gather.6.cloned.1.call-start = ((), (), s32[]{:S(2)}) async-start(), calls=%async_computation.4 | async-start | bytes 2621440 | tf_op jit(solution)/shard_map/all_gather | solution.py:57
  140.1 226.9 %all-gather.8.cloned.1.call-start = ((), (), s32[]{:S(2)}) async-start(), calls=%async_computation.5 | async-start | bytes 9437184 | tf_op jit(solution)/shard_map/all_gather | solution.py:79
  140.2 88.3 %collective-permute-start.3 = (bf16[256,1024]{1,0:T(8,128)(2,1)S(1)}, bf16[256,1024]{1,0:T(8,128)(2,1)S(1)}, u32[]{:S(2)}, u32[]{:S(2)}) collective-permute-start(bf16[256,1024]{1,0:T(8,128)(2,1)S(1)} %copy-done.2), channel_id=1, source_target_pairs={{0,16},{4,20},{8,24},{12,28},{16,0},{20,4},{24,8},{28,12},{1,17},{... | collective-permute-start | bytes 1572872 | tf_op jit(solution)/shard_map/ppermute | solution.py:29
  141.7 86.0 %collective-permute-start.2 = (bf16[256,1024]{1,0:T(8,128)(2,1)S(1)}, bf16[256,1024]{1,0:T(8,128)(2,1)S(1)}, u32[]{:S(2)}, u32[]{:S(2)}) collective-permute-start(bf16[256,1024]{1,0:T(8,128)(2,1)S(1)} %copy-done.2), channel_id=1, source_target_pairs={{0,12},{4,16},{8,20},{12,24},{16,28},{20,0},{24,4},{28,8},{1,13},{... | collective-permute-start | bytes 1572872 | tf_op jit(solution)/shard_map/ppermute | solution.py:29
  141.7 83.9 %collective-permute-start.1 = (bf16[256,1024]{1,0:T(8,128)(2,1)S(1)}, bf16[256,1024]{1,0:T(8,128)(2,1)S(1)}, u32[]{:S(2)}, u32[]{:S(2)}) collective-permute-start(bf16[256,1024]{1,0:T(8,128)(2,1)S(1)} %copy-done.2), channel_id=1, source_target_pairs={{0,8},{4,12},{8,16},{12,20},{16,24},{20,28},{24,0},{28,4},{1,9},{5... | collective-permute-start | bytes 1572872 | tf_op jit(solution)/shard_map/ppermute | solution.py:29
  142.2 82.6 %collective-permute-start = (bf16[256,1024]{1,0:T(8,128)(2,1)S(1)}, bf16[256,1024]{1,0:T(8,128)(2,1)S(1)}, u32[]{:S(2)}, u32[]{:S(2)}) collective-permute-start(bf16[256,1024]{1,0:T(8,128)(2,1)S(1)} %copy-done.2), channel_id=1, source_target_pairs={{0,4},{4,8},{8,12},{12,16},{16,20},{20,24},{24,28},{28,0},{1,5},{5... | collective-permute-start | bytes 1572872 | tf_op jit(solution)/shard_map/ppermute | solution.py:29
  154.7 27.3 %collective-permute-start.7 = (s32[256,32]{0,1:T(8,128)S(1)}, s32[256,32]{0,1:T(8,128)S(1)}, u32[]{:S(2)}, u32[]{:S(2)}) collective-permute-start(s32[256,32]{0,1:T(8,128)S(1)} %get-tuple-element.14), channel_id=1, source_target_pairs={{0,4},{4,8},{8,12},{12,16},{16,20},{20,24},{24,28},{28,0},{1,5},{5... | collective-permute-start | bytes 98312 | tf_op jit(solution)/shard_map/ppermute | solution.py:31
  182.0 5.8 collective-permute-start.8
  187.8 13.9 %collective-permute-start.9 = (s32[256,32]{0,1:T(8,128)S(1)}, s32[256,32]{0,1:T(8,128)S(1)}, u32[]{:S(2)}, u32[]{:S(2)}) collective-permute-start(s32[256,32]{0,1:T(8,128)S(1)} %get-tuple-element.12), channel_id=1, source_target_pairs={{0,12},{4,16},{8,20},{12,24},{16,28},{20,0},{24,4},{28,8},{1,13},{... | collective-permute-start | bytes 98312 | tf_op jit(solution)/shard_map/ppermute | solution.py:31
  201.7 7.9 %collective-permute-start.10 = (s32[256,32]{0,1:T(8,128)S(1)}, s32[256,32]{0,1:T(8,128)S(1)}, u32[]{:S(2)}, u32[]{:S(2)}) collective-permute-start(s32[256,32]{0,1:T(8,128)S(1)} %get-tuple-element.11), channel_id=1, source_target_pairs={{0,16},{4,20},{8,24},{12,28},{16,0},{20,4},{24,8},{28,12},{1,17},{... | collective-permute-start | bytes 98312 | tf_op jit(solution)/shard_map/ppermute | solution.py:31
  209.6 3.3 collective-permute-start.11
  212.9 5.8 collective-permute-start.12
  218.7 2.2 collective-permute-start.13
  220.9 16.2 %collective-permute-start.4 = (bf16[256,1024]{1,0:T(8,128)(2,1)S(1)}, bf16[256,1024]{1,0:T(8,128)(2,1)S(1)}, u32[]{:S(2)}, u32[]{:S(2)}) collective-permute-start(bf16[256,1024]{1,0:T(8,128)(2,1)S(1)} %copy-done.2), channel_id=1, source_target_pairs={{0,20},{4,24},{8,28},{12,0},{16,4},{20,8},{24,12},{28,16},{1,21},{... | collective-permute-start | bytes 1572872 | tf_op jit(solution)/shard_map/ppermute | solution.py:29
  224.7 22.7 %collective-permute-start.5 = (bf16[256,1024]{1,0:T(8,128)(2,1)S(1)}, bf16[256,1024]{1,0:T(8,128)(2,1)S(1)}, u32[]{:S(2)}, u32[]{:S(2)}) collective-permute-start(bf16[256,1024]{1,0:T(8,128)(2,1)S(1)} %copy-done.2), channel_id=1, source_target_pairs={{0,24},{4,28},{8,0},{12,4},{16,8},{20,12},{24,16},{28,20},{1,25},{... | collective-permute-start | bytes 1572872 | tf_op jit(solution)/shard_map/ppermute | solution.py:29
  225.6 27.5 %collective-permute-start.6 = (bf16[256,1024]{1,0:T(8,128)(2,1)S(1)}, bf16[256,1024]{1,0:T(8,128)(2,1)S(1)}, u32[]{:S(2)}, u32[]{:S(2)}) collective-permute-start(bf16[256,1024]{1,0:T(8,128)(2,1)S(1)} %copy-done.2), channel_id=1, source_target_pairs={{0,28},{4,0},{8,4},{12,8},{16,12},{20,16},{24,20},{28,24},{1,29},{... | collective-permute-start | bytes 1572872 | tf_op jit(solution)/shard_map/ppermute | solution.py:29
  276.6 186.8 %reduce-scatter.6.cloned.1.call-start = ((), (), s32[]{:S(2)}) async-start(), calls=%async_computation.6 | async-start | bytes 10485760 | tf_op jit(solution)/shard_map/reduce_scatter | solution.py:80
  378.4 142.9 %copy-start = (bf16[1024,512]{1,0:T(8,128)(2,1)S(1)}, bf16[1024,512]{1,0:T(8,128)(2,1)}, u32[]{:S(2)}) copy-start(bf16[1024,512]{1,0:T(8,128)(2,1)} %convolution_convert_fusion) | copy-start | bytes 3145732
  378.4 142.8 %all-gather.10.cloned.1.call-start = ((), (), s32[]{:S(2)}) async-start(), calls=%async_computation.7 | async-start | bytes 5242880 | tf_op jit(solution)/shard_map/all_gather | solution.py:72
  467.8 145.8 %all-gather.12.cloned.1.call-start = ((), (), s32[]{:S(2)}) async-start(), calls=%async_computation.8 | async-start | bytes 9437184 | tf_op jit(solution)/shard_map/all_gather | solution.py:79
  531.4 178.6 %reduce-scatter.8.cloned.1.call-start = ((), (), s32[]{:S(2)}) async-start(), calls=%async_computation.9 | async-start | bytes 10485760 | tf_op jit(solution)/shard_map/reduce_scatter | solution.py:80
  625.0 140.4 %copy-start.1 = (bf16[1024,512]{1,0:T(8,128)(2,1)S(1)}, bf16[1024,512]{1,0:T(8,128)(2,1)}, u32[]{:S(2)}) copy-start(bf16[1024,512]{1,0:T(8,128)(2,1)} %multiply_convert_fusion.1) | copy-start | bytes 3145732
  625.0 140.4 %all-gather.14.cloned.1.call-start = ((), (), s32[]{:S(2)}) async-start(), calls=%async_computation.10 | async-start | bytes 5242880 | tf_op jit(solution)/shard_map/all_gather | solution.py:72
Sparse Core Ops, SparseCore 0:
  15.2 55.3 reduce-scatter.3
  77.1 59.5 all-reduce.2
  140.2 35.5 all-gather.5
  276.7 90.2 all-gather.7
  378.5 84.7 reduce-scatter.5
  467.9 53.3 all-gather.9
  531.5 82.0 all-gather.11
  625.1 84.7 reduce-scatter.7
  712.9 52.5 all-gather.13

commit v3 on v2

--- a/solution.py
+++ b/solution.py
@@ -45,6 +45,9 @@
         scatter_dimension=0,
         tiled=True,
     ).astype(jnp.bfloat16)
+    rotated_t, all_vectors, tile_codes = lax.optimization_barrier(
+        (rotated_t, all_vectors, tile_codes)
+    )
     code_indicator = (codes.T[:, :, None] == code_ids[None, None, :]).astype(jnp.bfloat16)
     grouped_vectors = rotated_t.reshape(local_spaces, sub_dims, row_count)
     shard_code_sums = jnp.einsum(

time: 783 us -> 767 us (0.980)
  waiting for transfers between devices: 582 us -> 563 us
    reduce_scatter x1, waiting for transfers between devices: 51.2 us -> 0.01 us  [body(): lax.psum_scatter(lax.dot_general(rotation, vectors, (((0,), (1,)), ((), (...]
    all_gather x1, waiting for transfers between devices: 0.01 us -> 34.3 us  [body(): lax.all_gather(book.astype(jnp.bfloat16), 'rot', axis=0, tiled=True)]
    psum x1, waiting for transfers between devices: 59.7 us -> 68.1 us  [body(): total_sums, total_counts = lax.psum((shard_code_sums, local_counts), 'dp')]
    all_gather x2, waiting for transfers between devices: 172 us -> 164 us  [body(): rows_b = lax.all_gather(columns, 'dp', axis=1, tiled=True)]
where the time goes in v3:
time: 767 us
  waiting for transfers between devices  563 us (73%)
  matrix products  77.6 us (10%)
  blocking collectives  51.8 us (7%)
  starting transfers between devices  36.2 us (5%)
  other arithmetic  15.2 us (2%)
  between operations  14.6 us (2%)
  local copies, waits for them, and re-layouts  8.76 us (1%)
    reduce_scatter x2, waiting for transfers between devices, body(): lax.psum_scatter(lax.dot_general(rows_b, columns, (((0,), (0,)), ((), ())...  170 us
    all_gather x2, waiting for transfers between devices, body(): rows_b = lax.all_gather(columns, 'dp', axis=1, tiled=True)  164 us
    psum x1, waiting for transfers between devices, body(): total_sums, total_counts = lax.psum((shard_code_sums, local_counts), 'dp')  68.1 us
    all_gather x2, waiting for transfers between devices, apply_gram(): lax.all_gather(gram_b, 'rot', axis=0, tiled=True)  65 us
    psum x1, blocking collectives, body(): total = lax.psum(jnp.sum(gram_part * gram_part), ('dp', 'rot'))  40.5 us
    ppermute x7, waiting for transfers between devices, body(): lax.ppermute(lax.dynamic_slice_in_dim(row_codes, target * tile_spaces, ti...  39.3 us
    all_gather x1, waiting for transfers between devices, body(): lax.all_gather(book.astype(jnp.bfloat16), 'rot', axis=0, tiled=True)  34.3 us
    ppermute x7, starting transfers between devices, body(): lax.ppermute(lax.dynamic_slice_in_dim(row_codes, target * tile_spaces, ti...  24.5 us
  transfers between devices with their start and end apart: 23, of which 18 were waited for; matrix products, arithmetic and copies ran while one was open for 1% of the time, Pallas kernels for 0%

profile of v3, /device:TPU:0, one launch (start us, length us, event | category | flops | bytes accessed | tf_op | source)
XLA Modules:
  0.0 766.7 jit_solution(3703915921396216914)
XLA Ops:
  7.2 7.9 %fusion.9 = f32[4096,256]{1,0:T(8,128)} fusion(bf16[1024,4096]{1,0:T(8,128)(2,1)} %param.4, bf16[256,1024]{1,0:T(8,128)(2,1)} %param.3), kind=kOutput, calls=%fused_computation.41 | convolution fusion | flops 2147483648 | bytes 13107200 | tf_op jit(solution)/shard_map/dot_general | solution.py:41
  15.1 0.0 all-reduce.3.cloned.1.call-start
  15.1 1.0 copy-done.2
  16.1 4.1 collective-permute-start.3
  20.2 0.7 collective-permute-start.2
  20.9 0.8 collective-permute-start.1
  21.7 0.2 collective-permute-start
  21.9 11.3 %all_gather.18 = s32[256,256]{0,1:T(8,128)S(1)} all-gather(s32[256,64]{0,1:T(8,128)S(1)} %copy-done.3), channel_id=1, replica_groups=mesh['dp'=8,'rot'=4] {'rot'}, dimensions={1}, use_global_device_ids=true | all-gather | bytes 327680 | tf_op jit(solution)/shard_map/all_gather | solution.py:23
  33.2 0.1 collective-permute-start.7
  33.3 3.4 convert_reduce_fusion
  36.7 0.8 constant_dynamic-update-slice_fusion.7
  37.6 24.1 %collective-permute-done.7 = s32[256,32]{0,1:T(8,128)S(1)} collective-permute-done((s32[256,32]{0,1:T(8,128)S(1)}, s32[256,32]{0,1:T(8,128)S(1)}, u32[]{:S(2)}, u32[]{:S(2)}) %collective-permute-start.7) | collective-permute-done | bytes 32800 | tf_op jit(solution)/shard_map/ppermute | solution.py:31
  61.7 0.6 collective-permute-start.8
  62.3 5.2 collective-permute-done.8
  67.5 13.1 %collective-permute-start.9 = (s32[256,32]{0,1:T(8,128)S(1)}, s32[256,32]{0,1:T(8,128)S(1)}, u32[]{:S(2)}, u32[]{:S(2)}) collective-permute-start(s32[256,32]{0,1:T(8,128)S(1)} %get-tuple-element.18), channel_id=1, source_target_pairs={{0,12},{4,16},{8,20},{12,24},{16,28},{20,0},{24,4},{28,8},{1,13},{... | collective-permute-start | bytes 98312 | tf_op jit(solution)/shard_map/ppermute | solution.py:31
  80.6 1.6 collective-permute-done.9
  82.2 6.0 collective-permute-start.10
  88.2 1.9 collective-permute-done.10
  90.1 3.3 collective-permute-done.11
  93.5 4.2 collective-permute-start.12
  97.7 1.6 collective-permute-done.12
  99.2 0.6 collective-permute-start.13
  99.8 1.6 collective-permute-done.13
  101.4 3.8 collective-permute-start.4
  105.3 0.8 constant_dynamic-update-slice_fusion.6
  106.1 1.2 collective-permute-start.6
  107.3 0.8 constant_dynamic-update-slice_fusion.5
  108.2 0.8 constant_dynamic-update-slice_fusion.4
  109.0 0.8 constant_dynamic-update-slice_fusion.3
  109.9 7.7 %collective-permute-done.4 = bf16[256,1024]{1,0:T(8,128)(2,1)S(1)} collective-permute-done((bf16[256,1024]{1,0:T(8,128)(2,1)S(1)}, bf16[256,1024]{1,0:T(8,128)(2,1)S(1)}, u32[]{:S(2)}, u32[]{:S(2)}) %collective-permute-start.4) | collective-permute-done | bytes 524320 | tf_op jit(solution)/shard_map/ppermute | solution.py:29
  117.6 0.8 constant_dynamic-update-slice_fusion.2
  118.4 9.6 %collective-permute-done.5 = bf16[256,1024]{1,0:T(8,128)(2,1)S(1)} collective-permute-done((bf16[256,1024]{1,0:T(8,128)(2,1)S(1)}, bf16[256,1024]{1,0:T(8,128)(2,1)S(1)}, u32[]{:S(2)}, u32[]{:S(2)}) %collective-permute-start.5) | collective-permute-done | bytes 524320 | tf_op jit(solution)/shard_map/ppermute | solution.py:29
  128.0 0.8 constant_dynamic-update-slice_fusion.1
  128.8 4.8 collective-permute-done.6
  133.6 0.9 constant_dynamic-update-slice_fusion
  134.5 1.3 convert_element_type.37
  135.8 5.1 fusion.3
  140.9 0.0 all-gather.6.cloned.1.call-start
  141.0 68.1 %all-reduce.3.cloned.1.call-done = (f32[64,16,256]{2,1,0:T(8,128)}, f32[64,256]{1,0:T(8,128)}) async-done(((f32[64,16,256]{2,1,0:T(8,128)}, f32[64,256]{1,0:T(8,128)}), (f32[64,16,256]{2,1,0:T(8,128)}, f32[64,256]{1,0:T(8,128)})) %all-reduce.3.cloned.1.call-update) | async-done | bytes 1114128 | tf_op jit(solution)/shard_map/psum | solution.py:57
  209.0 0.8 broadcast_maximum_fusion
  209.9 2.5 fusion.8
  212.4 0.0 all-gather.8.cloned.1.call-start
  212.5 34.3 %all-gather.6.cloned.1.call-done = bf16[256,16,256]{2,1,0:T(8,128)(2,1)} async-done(((bf16[64,16,256]{2,1,0:T(8,128)(2,1)}), bf16[256,16,256]{2,1,0:T(8,128)(2,1)}) %all-gather.6.cloned.1.call-update) | async-done | bytes 2097168 | tf_op jit(solution)/shard_map/all_gather | solution.py:60
  246.7 1.0 fusion.28
  247.7 16.1 %fusion.5 = bf16[32,16,2048]{2,1,0:T(8,128)(2,1)S(1)} fusion(s32[32,2048]{1,0:T(8,128)S(1)} %bitcast.23, bf16[32,16,256]{2,1,0:T(8,128)(2,1)S(1)} %fusion.28), kind=kOutput, calls=%fused_computation.8 | convolution fusion | flops 554696704 | bytes 2621440 | tf_op jit(solution)/shard_map/lyg,lxg->lyx/dot_general | solution.py:64
  263.8 5.6 convolution_convert_fusion
  269.4 0.2 reduce-scatter.6.cloned.1.call-start
  269.6 82.0 %all-gather.8.cloned.1.call-done = bf16[1024,4096]{1,0:T(8,128)(2,1)} async-done(((bf16[1024,512]{1,0:T(8,128)(2,1)}), bf16[1024,4096]{1,0:T(8,128)(2,1)}) %all-gather.8.cloned.1.call-update) | async-done | bytes 8388624 | tf_op jit(solution)/shard_map/all_gather | solution.py:82
  351.6 11.4 %fusion.10 = f32[4096,512]{1,0:T(8,128)} fusion(bf16[1024,4096]{1,0:T(8,128)(2,1)} %all-gather.8.cloned.1.call-done, bf16[1024,512]{1,0:T(8,128)(2,1)} %convolution_convert_fusion), kind=kOutput, calls=%fused_computation.42 | convolution fusion | flops 4294967296 | bytes 17825792 | tf_op jit(solution)/shard_map/dot_general | solution.py:84
  363.0 0.0 all-gather.10.cloned.1.call-start
  363.1 84.9 %reduce-scatter.6.cloned.1.call-done = f32[1024,512]{1,0:T(8,128)} async-done(((f32[4096,512]{1,0:T(8,128)}), f32[1024,512]{1,0:T(8,128)}) %reduce-scatter.6.cloned.1.call-update) | async-done | bytes 2097168 | tf_op jit(solution)/shard_map/reduce_scatter | solution.py:83
  448.0 4.4 multiply_reduce_fusion
  452.4 0.0 all-gather.12.cloned.1.call-start
  452.4 40.5 %psum.23 = f32[]{:T(128)} all-reduce(f32[]{:T(128)} %get-tuple-element.12), channel_id=1, replica_groups=mesh['dp'=8,'rot'=4] {'dp','rot'}, use_global_device_ids=true, to_apply=%region_6.7 | all-reduce | flops 1 | bytes 8 | tf_op jit(solution)/shard_map/psum | solution.py:95
  493.5 12.3 %all-gather.10.cloned.1.call-done = bf16[4096,512]{1,0:T(8,128)(2,1)} async-done(((bf16[1024,512]{1,0:T(8,128)(2,1)}), bf16[4096,512]{1,0:T(8,128)(2,1)}) %all-gather.10.cloned.1.call-update) | async-done | bytes 4194320 | tf_op jit(solution)/shard_map/all_gather | solution.py:75
  505.9 10.1 %multiply_convert_fusion.1 = bf16[1024,512]{1,0:T(8,128)(2,1)} fusion(bf16[1024,512]{1,0:T(8,128)(2,1)S(1)} %copy-done, bf16[1024,4096]{1,0:T(8,128)(2,1)} %all-gather.8.cloned.1.call-done, bf16[4096,512]{1,0:T(8,128)(2,1)} %all-gather.10.cloned.1.call-done, f32[]{:T(128)S(6)} %mul.76, f32[]{:T(128)S(6)} %div.13), kind=kOutput, calls=%fused_computation.10 | convolution fusion | flops 4298113024 | bytes 14680072 | tf_op jit(solution)/shard_map/dot_general | solution.py:73
  516.0 0.3 reduce-scatter.8.cloned.1.call-start
  516.3 81.9 %all-gather.12.cloned.1.call-done = bf16[1024,4096]{1,0:T(8,128)(2,1)} async-done(((bf16[1024,512]{1,0:T(8,128)(2,1)}), bf16[1024,4096]{1,0:T(8,128)(2,1)}) %all-gather.12.cloned.1.call-update) | async-done | bytes 8388624 | tf_op jit(solution)/shard_map/all_gather | solution.py:82
  598.2 11.4 %fusion.11 = f32[4096,512]{1,0:T(8,128)} fusion(bf16[1024,4096]{1,0:T(8,128)(2,1)} %all-gather.12.cloned.1.call-done, bf16[1024,512]{1,0:T(8,128)(2,1)} %multiply_convert_fusion.1), kind=kOutput, calls=%fused_computation.43 | convolution fusion | flops 4294967296 | bytes 17825792 | tf_op jit(solution)/shard_map/dot_general | solution.py:84
  609.6 0.0 all-gather.14.cloned.1.call-start
  609.7 84.9 %reduce-scatter.8.cloned.1.call-done = f32[1024,512]{1,0:T(8,128)} async-done(((f32[4096,512]{1,0:T(8,128)}), f32[1024,512]{1,0:T(8,128)}) %reduce-scatter.8.cloned.1.call-update) | async-done | bytes 2097168 | tf_op jit(solution)/shard_map/reduce_scatter | solution.py:83
  694.6 2.7 convert_element_type.47
  697.3 52.7 %all-gather.14.cloned.1.call-done = bf16[4096,512]{1,0:T(8,128)(2,1)} async-done(((bf16[1024,512]{1,0:T(8,128)(2,1)}), bf16[4096,512]{1,0:T(8,128)(2,1)}) %all-gather.14.cloned.1.call-update) | async-done | bytes 4194320 | tf_op jit(solution)/shard_map/all_gather | solution.py:75
  750.1 10.1 %multiply_convert_fusion = bf16[1024,512]{1,0:T(8,128)(2,1)} fusion(bf16[1024,512]{1,0:T(8,128)(2,1)S(1)} %copy-done.1, bf16[1024,4096]{1,0:T(8,128)(2,1)} %all-gather.12.cloned.1.call-done, bf16[4096,512]{1,0:T(8,128)(2,1)} %all-gather.14.cloned.1.call-done), kind=kOutput, calls=%fused_computation.9 | convolution fusion | flops 4298113024 | bytes 14680064 | tf_op jit(solution)/shard_map/dot_general | solution.py:73
  (32 shorter events, 0.3 us)
Async XLA Ops:
  7.2 127.3 %reduce-scatter.4.cloned.1.call-start = ((), (), s32[]{:S(2)}) async-start(), calls=%async_computation.3 | async-start | bytes 5242880 | tf_op jit(solution)/shard_map/reduce_scatter | solution.py:40
  15.1 1.0 copy-start.2
  15.1 6.9 copy-start.3
  15.1 193.9 %all-reduce.3.cloned.1.call-start = ((), (), s32[]{:S(2)}) async-start(), calls=%async_computation.11 | async-start | bytes 2228224 | tf_op jit(solution)/shard_map/psum | solution.py:57
  16.1 92.9 %collective-permute-start.3 = (bf16[256,1024]{1,0:T(8,128)(2,1)S(1)}, bf16[256,1024]{1,0:T(8,128)(2,1)S(1)}, u32[]{:S(2)}, u32[]{:S(2)}) collective-permute-start(bf16[256,1024]{1,0:T(8,128)(2,1)S(1)} %copy-done.2), channel_id=1, source_target_pairs={{0,16},{4,20},{8,24},{12,28},{16,0},{20,4},{24,8},{28,12},{1,17},{... | collective-permute-start | bytes 1572872 | tf_op jit(solution)/shard_map/ppermute | solution.py:29
  20.2 88.0 %collective-permute-start.2 = (bf16[256,1024]{1,0:T(8,128)(2,1)S(1)}, bf16[256,1024]{1,0:T(8,128)(2,1)S(1)}, u32[]{:S(2)}, u32[]{:S(2)}) collective-permute-start(bf16[256,1024]{1,0:T(8,128)(2,1)S(1)} %copy-done.2), channel_id=1, source_target_pairs={{0,12},{4,16},{8,20},{12,24},{16,28},{20,0},{24,4},{28,8},{1,13},{... | collective-permute-start | bytes 1572872 | tf_op jit(solution)/shard_map/ppermute | solution.py:29
  20.9 85.2 %collective-permute-start.1 = (bf16[256,1024]{1,0:T(8,128)(2,1)S(1)}, bf16[256,1024]{1,0:T(8,128)(2,1)S(1)}, u32[]{:S(2)}, u32[]{:S(2)}) collective-permute-start(bf16[256,1024]{1,0:T(8,128)(2,1)S(1)} %copy-done.2), channel_id=1, source_target_pairs={{0,8},{4,12},{8,16},{12,20},{16,24},{20,28},{24,0},{28,4},{1,9},{5... | collective-permute-start | bytes 1572872 | tf_op jit(solution)/shard_map/ppermute | solution.py:29
  21.7 83.5 %collective-permute-start = (bf16[256,1024]{1,0:T(8,128)(2,1)S(1)}, bf16[256,1024]{1,0:T(8,128)(2,1)S(1)}, u32[]{:S(2)}, u32[]{:S(2)}) collective-permute-start(bf16[256,1024]{1,0:T(8,128)(2,1)S(1)} %copy-done.2), channel_id=1, source_target_pairs={{0,4},{4,8},{8,12},{12,16},{16,20},{20,24},{24,28},{28,0},{1,5},{5... | collective-permute-start | bytes 1572872 | tf_op jit(solution)/shard_map/ppermute | solution.py:29
  33.2 28.5 %collective-permute-start.7 = (s32[256,32]{0,1:T(8,128)S(1)}, s32[256,32]{0,1:T(8,128)S(1)}, u32[]{:S(2)}, u32[]{:S(2)}) collective-permute-start(s32[256,32]{0,1:T(8,128)S(1)} %get-tuple-element.20), channel_id=1, source_target_pairs={{0,4},{4,8},{8,12},{12,16},{16,20},{20,24},{24,28},{28,0},{1,5},{5... | collective-permute-start | bytes 98312 | tf_op jit(solution)/shard_map/ppermute | solution.py:31
  61.7 5.8 collective-permute-start.8
  67.5 14.7 %collective-permute-start.9 = (s32[256,32]{0,1:T(8,128)S(1)}, s32[256,32]{0,1:T(8,128)S(1)}, u32[]{:S(2)}, u32[]{:S(2)}) collective-permute-start(s32[256,32]{0,1:T(8,128)S(1)} %get-tuple-element.18), channel_id=1, source_target_pairs={{0,12},{4,16},{8,20},{12,24},{16,28},{20,0},{24,4},{28,8},{1,13},{... | collective-permute-start | bytes 98312 | tf_op jit(solution)/shard_map/ppermute | solution.py:31
  82.2 7.9 %collective-permute-start.10 = (s32[256,32]{0,1:T(8,128)S(1)}, s32[256,32]{0,1:T(8,128)S(1)}, u32[]{:S(2)}, u32[]{:S(2)}) collective-permute-start(s32[256,32]{0,1:T(8,128)S(1)} %get-tuple-element.17), channel_id=1, source_target_pairs={{0,16},{4,20},{8,24},{12,28},{16,0},{20,4},{24,8},{28,12},{1,17},{... | collective-permute-start | bytes 98312 | tf_op jit(solution)/shard_map/ppermute | solution.py:31
  90.1 3.3 collective-permute-start.11
  93.5 5.8 collective-permute-start.12
  99.2 2.2 collective-permute-start.13
  101.4 16.2 %collective-permute-start.4 = (bf16[256,1024]{1,0:T(8,128)(2,1)S(1)}, bf16[256,1024]{1,0:T(8,128)(2,1)S(1)}, u32[]{:S(2)}, u32[]{:S(2)}) collective-permute-start(bf16[256,1024]{1,0:T(8,128)(2,1)S(1)} %copy-done.2), channel_id=1, source_target_pairs={{0,20},{4,24},{8,28},{12,0},{16,4},{20,8},{24,12},{28,16},{1,21},{... | collective-permute-start | bytes 1572872 | tf_op jit(solution)/shard_map/ppermute | solution.py:29
  105.2 22.7 %collective-permute-start.5 = (bf16[256,1024]{1,0:T(8,128)(2,1)S(1)}, bf16[256,1024]{1,0:T(8,128)(2,1)S(1)}, u32[]{:S(2)}, u32[]{:S(2)}) collective-permute-start(bf16[256,1024]{1,0:T(8,128)(2,1)S(1)} %copy-done.2), channel_id=1, source_target_pairs={{0,24},{4,28},{8,0},{12,4},{16,8},{20,12},{24,16},{28,20},{1,25},{... | collective-permute-start | bytes 1572872 | tf_op jit(solution)/shard_map/ppermute | solution.py:29
  106.1 27.5 %collective-permute-start.6 = (bf16[256,1024]{1,0:T(8,128)(2,1)S(1)}, bf16[256,1024]{1,0:T(8,128)(2,1)S(1)}, u32[]{:S(2)}, u32[]{:S(2)}) collective-permute-start(bf16[256,1024]{1,0:T(8,128)(2,1)S(1)} %copy-done.2), channel_id=1, source_target_pairs={{0,28},{4,0},{8,4},{12,8},{16,12},{20,16},{24,20},{28,24},{1,29},{... | collective-permute-start | bytes 1572872 | tf_op jit(solution)/shard_map/ppermute | solution.py:29
  140.9 105.8 %all-gather.6.cloned.1.call-start = ((), (), s32[]{:S(2)}) async-start(), calls=%async_computation.4 | async-start | bytes 2621440 | tf_op jit(solution)/shard_map/all_gather | solution.py:60
  212.4 139.2 %all-gather.8.cloned.1.call-start = ((), (), s32[]{:S(2)}) async-start(), calls=%async_computation.5 | async-start | bytes 9437184 | tf_op jit(solution)/shard_map/all_gather | solution.py:82
  269.4 178.6 %reduce-scatter.6.cloned.1.call-start = ((), (), s32[]{:S(2)}) async-start(), calls=%async_computation.6 | async-start | bytes 10485760 | tf_op jit(solution)/shard_map/reduce_scatter | solution.py:83
  363.0 142.9 %copy-start = (bf16[1024,512]{1,0:T(8,128)(2,1)S(1)}, bf16[1024,512]{1,0:T(8,128)(2,1)}, u32[]{:S(2)}) copy-start(bf16[1024,512]{1,0:T(8,128)(2,1)} %convolution_convert_fusion) | copy-start | bytes 3145732
  363.0 142.8 %all-gather.10.cloned.1.call-start = ((), (), s32[]{:S(2)}) async-start(), calls=%async_computation.7 | async-start | bytes 5242880 | tf_op jit(solution)/shard_map/all_gather | solution.py:75
  452.4 145.8 %all-gather.12.cloned.1.call-start = ((), (), s32[]{:S(2)}) async-start(), calls=%async_computation.8 | async-start | bytes 9437184 | tf_op jit(solution)/shard_map/all_gather | solution.py:82
  516.0 178.6 %reduce-scatter.8.cloned.1.call-start = ((), (), s32[]{:S(2)}) async-start(), calls=%async_computation.9 | async-start | bytes 10485760 | tf_op jit(solution)/shard_map/reduce_scatter | solution.py:83
  609.6 140.4 %copy-start.1 = (bf16[1024,512]{1,0:T(8,128)(2,1)S(1)}, bf16[1024,512]{1,0:T(8,128)(2,1)}, u32[]{:S(2)}) copy-start(bf16[1024,512]{1,0:T(8,128)(2,1)} %multiply_convert_fusion.1) | copy-start | bytes 3145732
  609.6 140.4 %all-gather.14.cloned.1.call-start = ((), (), s32[]{:S(2)}) async-start(), calls=%async_computation.10 | async-start | bytes 5242880 | tf_op jit(solution)/shard_map/all_gather | solution.py:75
Sparse Core Ops, SparseCore 0:
  15.2 57.4 reduce-scatter.3
  141.0 67.9 all-reduce.2
  212.5 34.1 all-gather.5
  269.5 82.0 all-gather.7
  363.1 84.7 reduce-scatter.5
  452.5 53.3 all-gather.9
  516.1 82.0 all-gather.11
  609.7 84.7 reduce-scatter.7
  697.5 52.5 all-gather.13

commit v4 on v2

--- a/solution.py
+++ b/solution.py
@@ -21,21 +21,18 @@
 
     dp_size = lax.axis_size("dp")
     row_codes = lax.all_gather(codes, "rot", axis=1, tiled=True)
-    vector_parts = [vectors]
-    code_parts = [lax.dynamic_slice_in_dim(row_codes, dp_index * tile_spaces, tile_spaces, 1)]
+
+    def tile_part(block):
+        block_codes = lax.dynamic_slice_in_dim(row_codes, block * tile_spaces, tile_spaces, 1)
+        return jnp.concatenate([vectors, block_codes.astype(jnp.bfloat16)], axis=1)
+
+    parts = [tile_part(dp_index)]
     for shift in range(1, dp_size):
         pairs = [(i, (i + shift) % dp_size) for i in range(dp_size)]
-        target = (dp_index + shift) % dp_size
-        vector_parts.append(lax.ppermute(vectors, "dp", pairs))
-        code_parts.append(
-            lax.ppermute(
-                lax.dynamic_slice_in_dim(row_codes, target * tile_spaces, tile_spaces, 1),
-                "dp",
-                pairs,
-            )
-        )
-    all_vectors = jnp.concatenate(vector_parts, axis=0)
-    tile_codes = jnp.concatenate(code_parts, axis=0)
+        parts.append(lax.ppermute(tile_part((dp_index + shift) % dp_size), "dp", pairs))
+    joined = jnp.concatenate(parts, axis=0)
+    all_vectors = joined[:, :block_dims]
+    tile_codes = joined[:, block_dims:].astype(jnp.int32)
 
     rotated_t = lax.psum_scatter(
         lax.dot_general(
@@ -52,6 +49,9 @@
     )
     local_counts = jnp.sum(code_indicator, axis=1, dtype=jnp.float32)
     total_sums, total_counts = lax.psum((shard_code_sums, local_counts), "dp")
+    total_sums, total_counts, all_vectors, tile_codes = lax.optimization_barrier(
+        (total_sums, total_counts, all_vectors, tile_codes)
+    )
     book = total_sums / jnp.maximum(total_counts, 1.0)[:, None, :]
     codebook = book.reshape(block_dims, K)
     codebook_batch = lax.all_gather(book.astype(jnp.bfloat16), "rot", axis=0, tiled=True)

time: 783 us -> 748 us (0.955)
  waiting for transfers between devices: 582 us -> 562 us
  starting transfers between devices: 32.4 us -> 13.8 us
    reduce_scatter x1, waiting for transfers between devices: 51.2 us -> 0.01 us  [body(): lax.psum_scatter(lax.dot_general(rotation, vectors, (((0,), (1,)), ((), (...]
    all_gather x1, waiting for transfers between devices: 0.01 us -> 34.3 us  [body(): lax.all_gather(book.astype(jnp.bfloat16), 'rot', axis=0, tiled=True)]
    ppermute x14 -> x7, starting transfers between devices: 31.7 us -> 13 us  [body(): lax.ppermute(tile_part((dp_index + shift) % dp_size), 'dp', pairs)]
    psum x1, waiting for transfers between devices: 59.7 us -> 73.9 us  [body(): total_sums, total_counts = lax.psum((shard_code_sums, local_counts), 'dp')]
    ppermute x14 -> x7, waiting for transfers between devices: 64.3 us -> 55.1 us  [body(): lax.ppermute(tile_part((dp_index + shift) % dp_size), 'dp', pairs)]
    all_gather x2, waiting for transfers between devices: 172 us -> 164 us  [body(): rows_b = lax.all_gather(columns, 'dp', axis=1, tiled=True)]
  transfers between devices with their start and end apart: 23 -> 16, of which waited for: 18 -> 12; matrix products, arithmetic and copies ran while one was open for 1% -> 3% of each run, Pallas kernels for 0% -> 0%
where the time goes in v4:
time: 748 us
  waiting for transfers between devices  562 us (75%)
  matrix products  75.4 us (10%)
  blocking collectives  51.5 us (7%)
  other arithmetic  17.3 us (2%)
  between operations  14.7 us (2%)
  starting transfers between devices  13.8 us (2%)
  local copies, waits for them, and re-layouts  13 us (2%)
    reduce_scatter x2, waiting for transfers between devices, body(): lax.psum_scatter(lax.dot_general(rows_b, columns, (((0,), (0,)), ((), ())...  170 us
    all_gather x2, waiting for transfers between devices, body(): rows_b = lax.all_gather(columns, 'dp', axis=1, tiled=True)  164 us
    psum x1, waiting for transfers between devices, body(): total_sums, total_counts = lax.psum((shard_code_sums, local_counts), 'dp')  73.9 us
    all_gather x2, waiting for transfers between devices, apply_gram(): lax.all_gather(gram_b, 'rot', axis=0, tiled=True)  65 us
    ppermute x7, waiting for transfers between devices, body(): lax.ppermute(tile_part((dp_index + shift) % dp_size), 'dp', pairs)  55.1 us
    psum x1, blocking collectives, body(): total = lax.psum(jnp.sum(gram_part * gram_part), ('dp', 'rot'))  40.5 us
    all_gather x1, waiting for transfers between devices, body(): lax.all_gather(book.astype(jnp.bfloat16), 'rot', axis=0, tiled=True)  34.3 us
    dot_general x2, matrix products, body(): lax.dot_general(rows_b, columns, (((0,), (0,)), ((), ())), preferred_elem...  22.8 us
  transfers between devices with their start and end apart: 16, of which 12 were waited for; matrix products, arithmetic and copies ran while one was open for 3% of the time, Pallas kernels for 0%

profile of v4, /device:TPU:0, one launch (start us, length us, event | category | flops | bytes accessed | tf_op | source)
XLA Modules:
  0.0 748.0 jit_solution(4359585762277740183)
XLA Ops:
  7.2 0.0 reduce-scatter.4.cloned.1.call-start
  7.2 7.9 %fusion.9 = f32[4096,256]{1,0:T(8,128)} fusion(bf16[1024,4096]{1,0:T(8,128)(2,1)} %param.4, bf16[256,1024]{1,0:T(8,128)(2,1)} %param.3), kind=kOutput, calls=%fused_computation.42 | convolution fusion | flops 2147483648 | bytes 13107200 | tf_op jit(solution)/shard_map/dot_general | solution.py:38
  15.1 0.0 reduce-scatter.4.cloned.1.call-update
  15.1 0.0 all-reduce.3.cloned.1.call-start
  15.3 0.9 copy-done.3
  16.2 0.2 copy.14
  16.4 11.0 %all_gather.18 = s32[256,256]{0,1:T(8,128)S(1)} all-gather(s32[256,64]{0,1:T(8,128)S(1)} %copy-done.4), channel_id=1, replica_groups=mesh['dp'=8,'rot'=4] {'rot'}, dimensions={1}, use_global_device_ids=true | all-gather | bytes 327680 | tf_op jit(solution)/shard_map/all_gather | solution.py:23
  27.5 1.1 pad_maximum_fusion.6
  28.6 3.5 collective-permute-start.6
  32.2 1.2 collective-permute-start.2
  33.3 1.7 collective-permute-start.3
  35.1 3.4 convert_reduce_fusion
  38.5 3.8 collective-permute-done
  42.3 6.6 collective-permute-start.4
  48.9 0.9 constant_dynamic-update-slice_fusion.6
  49.8 9.4 %collective-permute-done.1 = bf16[256,1056]{0,1:T(8,128)(2,1)S(1)} collective-permute-done((bf16[256,1056]{0,1:T(8,128)(2,1)S(1)}, bf16[256,1056]{0,1:T(8,128)(2,1)S(1)}, u32[]{:S(2)}, u32[]{:S(2)}) %collective-permute-start.1) | collective-permute-done | bytes 540704 | tf_op jit(solution)/shard_map/ppermute | solution.py:32
  59.2 0.9 constant_dynamic-update-slice_fusion.5
  60.1 28.8 %collective-permute-done.2 = bf16[256,1056]{0,1:T(8,128)(2,1)S(1)} collective-permute-done((bf16[256,1056]{0,1:T(8,128)(2,1)S(1)}, bf16[256,1056]{0,1:T(8,128)(2,1)S(1)}, u32[]{:S(2)}, u32[]{:S(2)}) %collective-permute-start.2) | collective-permute-done | bytes 540704 | tf_op jit(solution)/shard_map/ppermute | solution.py:32
  88.9 0.9 constant_dynamic-update-slice_fusion.4
  89.7 13.1 %collective-permute-done.3 = bf16[256,1056]{0,1:T(8,128)(2,1)S(1)} collective-permute-done((bf16[256,1056]{0,1:T(8,128)(2,1)S(1)}, bf16[256,1056]{0,1:T(8,128)(2,1)S(1)}, u32[]{:S(2)}, u32[]{:S(2)}) %collective-permute-start.3) | collective-permute-done | bytes 540704 | tf_op jit(solution)/shard_map/ppermute | solution.py:32
  102.8 0.9 constant_dynamic-update-slice_fusion.3
  103.7 0.9 constant_dynamic-update-slice_fusion.2
  104.6 0.9 constant_dynamic-update-slice_fusion.1
  105.5 1.3 convert_element_type.64
  106.8 5.1 fusion.3
  111.9 0.0 all-reduce.3.cloned.1.call-update
  111.9 0.0 all-gather.6.cloned.1.call-start
  112.0 0.9 constant_dynamic-update-slice_fusion
  112.8 4.8 slice.8
  117.6 0.9 slice_convert_fusion
  118.6 73.9 %all-reduce.3.cloned.1.call-done = (f32[64,16,256]{2,1,0:T(8,128)}, f32[64,256]{1,0:T(8,128)}) async-done(((f32[64,16,256]{2,1,0:T(8,128)}, f32[64,256]{1,0:T(8,128)}), (f32[64,16,256]{2,1,0:T(8,128)}, f32[64,256]{1,0:T(8,128)})) %all-reduce.3.cloned.1.call-update) | async-done | bytes 1114128 | tf_op jit(solution)/shard_map/psum | solution.py:51
  192.5 0.8 broadcast_maximum_fusion
  193.4 2.5 fusion.8
  195.9 0.0 all-gather.6.cloned.1.call-update
  195.9 0.0 all-gather.8.cloned.1.call-start
  195.9 34.3 %all-gather.6.cloned.1.call-done = bf16[256,16,256]{2,1,0:T(8,128)(2,1)} async-done(((bf16[64,16,256]{2,1,0:T(8,128)(2,1)}), bf16[256,16,256]{2,1,0:T(8,128)(2,1)}) %all-gather.6.cloned.1.call-update) | async-done | bytes 2097168 | tf_op jit(solution)/shard_map/all_gather | solution.py:57
  230.2 1.0 fusion.28
  231.2 16.1 %fusion.5 = bf16[32,16,2048]{2,1,0:T(8,128)(2,1)S(1)} fusion(s32[32,2048]{1,0:T(8,128)S(1)} %bitcast.23, bf16[32,16,256]{2,1,0:T(8,128)(2,1)S(1)} %fusion.28), kind=kOutput, calls=%fused_computation.8 | convolution fusion | flops 554696704 | bytes 2621440 | tf_op jit(solution)/shard_map/lyg,lxg->lyx/dot_general | solution.py:61
  247.3 3.3 convolution_convert_fusion
  250.6 0.0 all-gather.8.cloned.1.call-update
  250.7 0.2 reduce-scatter.6.cloned.1.call-start
  250.9 82.0 %all-gather.8.cloned.1.call-done = bf16[1024,4096]{1,0:T(8,128)(2,1)} async-done(((bf16[1024,512]{1,0:T(8,128)(2,1)}), bf16[1024,4096]{1,0:T(8,128)(2,1)}) %all-gather.8.cloned.1.call-update) | async-done | bytes 8388624 | tf_op jit(solution)/shard_map/all_gather | solution.py:79
  332.9 11.4 %fusion.10 = f32[4096,512]{1,0:T(8,128)} fusion(bf16[1024,4096]{1,0:T(8,128)(2,1)} %all-gather.8.cloned.1.call-done, bf16[1024,512]{1,0:T(8,128)(2,1)} %convolution_convert_fusion), kind=kOutput, calls=%fused_computation.43 | convolution fusion | flops 4294967296 | bytes 17825792 | tf_op jit(solution)/shard_map/dot_general | solution.py:81
  344.3 0.0 reduce-scatter.6.cloned.1.call-update
  344.3 0.0 all-gather.10.cloned.1.call-start
  344.3 84.9 %reduce-scatter.6.cloned.1.call-done = f32[1024,512]{1,0:T(8,128)} async-done(((f32[4096,512]{1,0:T(8,128)}), f32[1024,512]{1,0:T(8,128)}) %reduce-scatter.6.cloned.1.call-update) | async-done | bytes 2097168 | tf_op jit(solution)/shard_map/reduce_scatter | solution.py:80
  429.2 4.4 multiply_reduce_fusion
  433.6 0.0 all-gather.10.cloned.1.call-update
  433.7 0.0 all-gather.12.cloned.1.call-start
  433.7 40.5 %psum.23 = f32[]{:T(128)} all-reduce(f32[]{:T(128)} %get-tuple-element.14), channel_id=1, replica_groups=mesh['dp'=8,'rot'=4] {'dp','rot'}, use_global_device_ids=true, to_apply=%region_6.7 | all-reduce | flops 1 | bytes 8 | tf_op jit(solution)/shard_map/psum | solution.py:92
  474.9 12.3 %all-gather.10.cloned.1.call-done = bf16[4096,512]{1,0:T(8,128)(2,1)} async-done(((bf16[1024,512]{1,0:T(8,128)(2,1)}), bf16[4096,512]{1,0:T(8,128)(2,1)}) %all-gather.10.cloned.1.call-update) | async-done | bytes 4194320 | tf_op jit(solution)/shard_map/all_gather | solution.py:72
  487.2 10.1 %multiply_convert_fusion.1 = bf16[1024,512]{1,0:T(8,128)(2,1)} fusion(bf16[1024,512]{1,0:T(8,128)(2,1)S(1)} %copy-done.1, bf16[1024,4096]{1,0:T(8,128)(2,1)} %all-gather.8.cloned.1.call-done, bf16[4096,512]{1,0:T(8,128)(2,1)} %all-gather.10.cloned.1.call-done, f32[]{:T(128)S(6)} %mul.76, f32[]{:T(128)S(6)} %div.13), kind=kOutput, calls=%fused_computation.10 | convolution fusion | flops 4298113024 | bytes 14680072 | tf_op jit(solution)/shard_map/dot_general | solution.py:70
  497.3 0.0 all-gather.12.cloned.1.call-update
  497.3 0.3 reduce-scatter.8.cloned.1.call-start
  497.6 81.9 %all-gather.12.cloned.1.call-done = bf16[1024,4096]{1,0:T(8,128)(2,1)} async-done(((bf16[1024,512]{1,0:T(8,128)(2,1)}), bf16[1024,4096]{1,0:T(8,128)(2,1)}) %all-gather.12.cloned.1.call-update) | async-done | bytes 8388624 | tf_op jit(solution)/shard_map/all_gather | solution.py:79
  579.5 11.4 %fusion.11 = f32[4096,512]{1,0:T(8,128)} fusion(bf16[1024,4096]{1,0:T(8,128)(2,1)} %all-gather.12.cloned.1.call-done, bf16[1024,512]{1,0:T(8,128)(2,1)} %multiply_convert_fusion.1), kind=kOutput, calls=%fused_computation.44 | convolution fusion | flops 4294967296 | bytes 17825792 | tf_op jit(solution)/shard_map/dot_general | solution.py:81
  590.9 0.0 reduce-scatter.8.cloned.1.call-update
  590.9 0.0 copy-start.2
  590.9 0.0 all-gather.14.cloned.1.call-start
  591.0 84.9 %reduce-scatter.8.cloned.1.call-done = f32[1024,512]{1,0:T(8,128)} async-done(((f32[4096,512]{1,0:T(8,128)}), f32[1024,512]{1,0:T(8,128)}) %reduce-scatter.8.cloned.1.call-update) | async-done | bytes 2097168 | tf_op jit(solution)/shard_map/reduce_scatter | solution.py:80
  675.9 2.8 convert_element_type.83
  678.6 0.0 all-gather.14.cloned.1.call-update
  678.7 52.7 %all-gather.14.cloned.1.call-done = bf16[4096,512]{1,0:T(8,128)(2,1)} async-done(((bf16[1024,512]{1,0:T(8,128)(2,1)}), bf16[4096,512]{1,0:T(8,128)(2,1)}) %all-gather.14.cloned.1.call-update) | async-done | bytes 4194320 | tf_op jit(solution)/shard_map/all_gather | solution.py:72
  731.4 10.1 %multiply_convert_fusion = bf16[1024,512]{1,0:T(8,128)(2,1)} fusion(bf16[1024,512]{1,0:T(8,128)(2,1)S(1)} %copy-done.2, bf16[1024,4096]{1,0:T(8,128)(2,1)} %all-gather.12.cloned.1.call-done, bf16[4096,512]{1,0:T(8,128)(2,1)} %all-gather.14.cloned.1.call-done), kind=kOutput, calls=%fused_computation.9 | convolution fusion | flops 4298113024 | bytes 14680064 | tf_op jit(solution)/shard_map/dot_general | solution.py:70
  (16 shorter events, 0.1 us)
Async XLA Ops:
  7.2 98.3 %reduce-scatter.4.cloned.1.call-start = ((), (), s32[]{:S(2)}) async-start(), calls=%async_computation.3 | async-start | bytes 5242880 | tf_op jit(solution)/shard_map/reduce_scatter | solution.py:37
  15.1 1.0 copy-start.3
  15.1 1.3 copy-start.4
  15.1 177.4 %all-reduce.3.cloned.1.call-start = ((), (), s32[]{:S(2)}) async-start(), calls=%async_computation.11 | async-start | bytes 2228224 | tf_op jit(solution)/shard_map/psum | solution.py:51
  28.6 13.7 %collective-permute-start = (bf16[256,1056]{0,1:T(8,128)(2,1)S(1)}, bf16[256,1056]{0,1:T(8,128)(2,1)S(1)}, u32[]{:S(2)}, u32[]{:S(2)}) collective-permute-start(bf16[256,1056]{0,1:T(8,128)(2,1)S(1)} %get-tuple-element.17), channel_id=1, source_target_pairs={{0,4},{4,8},{8,12},{12,16},{16,20},{20,24},{24,28},{28,0},{1,5},{5... | collective-permute-start | bytes 1622024 | tf_op jit(solution)/shard_map/ppermute | solution.py:32
  28.6 83.3 %collective-permute-start.6 = (bf16[256,1056]{0,1:T(8,128)(2,1)S(1)}, bf16[256,1056]{0,1:T(8,128)(2,1)S(1)}, u32[]{:S(2)}, u32[]{:S(2)}) collective-permute-start(bf16[256,1056]{0,1:T(8,128)(2,1)S(1)} %get-tuple-element.16), channel_id=1, source_target_pairs={{0,28},{4,0},{8,4},{12,8},{16,12},{20,16},{24,20},{28,24},{1,29},{... | collective-permute-start | bytes 1622024 | tf_op jit(solution)/shard_map/ppermute | solution.py:32
  32.2 27.1 %collective-permute-start.1 = (bf16[256,1056]{0,1:T(8,128)(2,1)S(1)}, bf16[256,1056]{0,1:T(8,128)(2,1)S(1)}, u32[]{:S(2)}, u32[]{:S(2)}) collective-permute-start(bf16[256,1056]{0,1:T(8,128)(2,1)S(1)} %get-tuple-element.18), channel_id=1, source_target_pairs={{0,8},{4,12},{8,16},{12,20},{16,24},{20,28},{24,0},{28,4},{1,9},{5... | collective-permute-start | bytes 1622024 | tf_op jit(solution)/shard_map/ppermute | solution.py:32
  32.2 56.7 %collective-permute-start.2 = (bf16[256,1056]{0,1:T(8,128)(2,1)S(1)}, bf16[256,1056]{0,1:T(8,128)(2,1)S(1)}, u32[]{:S(2)}, u32[]{:S(2)}) collective-permute-start(bf16[256,1056]{0,1:T(8,128)(2,1)S(1)} %get-tuple-element.19), channel_id=1, source_target_pairs={{0,12},{4,16},{8,20},{12,24},{16,28},{20,0},{24,4},{28,8},{1,13},{... | collective-permute-start | bytes 1622024 | tf_op jit(solution)/shard_map/ppermute | solution.py:32
  33.3 69.5 %collective-permute-start.3 = (bf16[256,1056]{0,1:T(8,128)(2,1)S(1)}, bf16[256,1056]{0,1:T(8,128)(2,1)S(1)}, u32[]{:S(2)}, u32[]{:S(2)}) collective-permute-start(bf16[256,1056]{0,1:T(8,128)(2,1)S(1)} %get-tuple-element.20), channel_id=1, source_target_pairs={{0,16},{4,20},{8,24},{12,28},{16,0},{20,4},{24,8},{28,12},{1,17},{... | collective-permute-start | bytes 1622024 | tf_op jit(solution)/shard_map/ppermute | solution.py:32
  42.3 61.4 %collective-permute-start.4 = (bf16[256,1056]{0,1:T(8,128)(2,1)S(1)}, bf16[256,1056]{0,1:T(8,128)(2,1)S(1)}, u32[]{:S(2)}, u32[]{:S(2)}) collective-permute-start(bf16[256,1056]{0,1:T(8,128)(2,1)S(1)} %get-tuple-element.21), channel_id=1, source_target_pairs={{0,20},{4,24},{8,28},{12,0},{16,4},{20,8},{24,12},{28,16},{1,21},{... | collective-permute-start | bytes 1622024 | tf_op jit(solution)/shard_map/ppermute | solution.py:32
  59.2 45.4 %collective-permute-start.5 = (bf16[256,1056]{0,1:T(8,128)(2,1)S(1)}, bf16[256,1056]{0,1:T(8,128)(2,1)S(1)}, u32[]{:S(2)}, u32[]{:S(2)}) collective-permute-start(bf16[256,1056]{0,1:T(8,128)(2,1)S(1)} %get-tuple-element.22), channel_id=1, source_target_pairs={{0,24},{4,28},{8,0},{12,4},{16,8},{20,12},{24,16},{28,20},{1,25},{... | collective-permute-start | bytes 1622024 | tf_op jit(solution)/shard_map/ppermute | solution.py:32
  111.9 118.3 %all-gather.6.cloned.1.call-start = ((), (), s32[]{:S(2)}) async-start(), calls=%async_computation.4 | async-start | bytes 2621440 | tf_op jit(solution)/shard_map/all_gather | solution.py:57
  195.9 137.0 %all-gather.8.cloned.1.call-start = ((), (), s32[]{:S(2)}) async-start(), calls=%async_computation.5 | async-start | bytes 9437184 | tf_op jit(solution)/shard_map/all_gather | solution.py:79
  231.2 16.1 %copy-start = (bf16[2048,1024]{0,1:T(8,128)(2,1)S(1)}, bf16[2048,1024]{0,1:T(8,128)(2,1)}, u32[]{:S(2)}) copy-start(bf16[2048,1024]{0,1:T(8,128)(2,1)} %slice.8) | copy-start | bytes 12582916
  250.7 178.6 %reduce-scatter.6.cloned.1.call-start = ((), (), s32[]{:S(2)}) async-start(), calls=%async_computation.6 | async-start | bytes 10485760 | tf_op jit(solution)/shard_map/reduce_scatter | solution.py:80
  344.3 142.9 %copy-start.1 = (bf16[1024,512]{1,0:T(8,128)(2,1)S(1)}, bf16[1024,512]{1,0:T(8,128)(2,1)}, u32[]{:S(2)}) copy-start(bf16[1024,512]{1,0:T(8,128)(2,1)} %convolution_convert_fusion) | copy-start | bytes 3145732
  344.3 142.9 %all-gather.10.cloned.1.call-start = ((), (), s32[]{:S(2)}) async-start(), calls=%async_computation.7 | async-start | bytes 5242880 | tf_op jit(solution)/shard_map/all_gather | solution.py:72
  433.7 145.8 %all-gather.12.cloned.1.call-start = ((), (), s32[]{:S(2)}) async-start(), calls=%async_computation.8 | async-start | bytes 9437184 | tf_op jit(solution)/shard_map/all_gather | solution.py:79
  497.3 178.6 %reduce-scatter.8.cloned.1.call-start = ((), (), s32[]{:S(2)}) async-start(), calls=%async_computation.9 | async-start | bytes 10485760 | tf_op jit(solution)/shard_map/reduce_scatter | solution.py:80
  590.9 140.5 %copy-start.2 = (bf16[1024,512]{1,0:T(8,128)(2,1)S(1)}, bf16[1024,512]{1,0:T(8,128)(2,1)}, u32[]{:S(2)}) copy-start(bf16[1024,512]{1,0:T(8,128)(2,1)} %multiply_convert_fusion.1) | copy-start | bytes 3145732
  590.9 140.5 %all-gather.14.cloned.1.call-start = ((), (), s32[]{:S(2)}) async-start(), calls=%async_computation.10 | async-start | bytes 5242880 | tf_op jit(solution)/shard_map/all_gather | solution.py:72
Sparse Core Ops, SparseCore 0:
  15.3 55.9 reduce-scatter.3
  112.0 80.4 all-reduce.2
  196.0 34.1 all-gather.5
  250.8 82.0 all-gather.7
  344.4 84.7 reduce-scatter.5
  433.8 53.3 all-gather.9
  497.4 82.0 all-gather.11
  591.0 84.7 reduce-scatter.7
  678.8 52.5 all-gather.13

commit v5 on v4

--- a/solution.py
+++ b/solution.py
@@ -66,39 +66,39 @@
         all_vectors, rebuilt_t, (((0,), (1,)), ((), ())), preferred_element_type=jnp.float32
     ).astype(jnp.bfloat16)
 
-    def apply_gram(rows_b, gram_b):
-        return jnp.dot(
-            rows_b,
-            lax.all_gather(gram_b, "rot", axis=0, tiled=True),
-            preferred_element_type=jnp.float32,
-        )
+    def gram_step(tile, first):
+        parts = [tile]
+        for shift in range(1, dp_size):
+            pairs = [(i, (i + shift) % dp_size) for i in range(dp_size)]
+            parts.append(lax.ppermute(tile, "dp", pairs))
+        half = dp_size // 2
+        panels = [jnp.concatenate(parts[:half], axis=1), jnp.concatenate(parts[half:], axis=1)]
+        pieces = [
+            lax.psum_scatter(
+                lax.dot_general(
+                    panel, tile, (((0,), (0,)), ((), ())), preferred_element_type=jnp.float32
+                ),
+                "rot",
+                scatter_dimension=0,
+                tiled=True,
+            )
+            for panel in panels
+        ]
+        product = None
+        for panel, piece in zip(panels, pieces):
+            gathered = lax.all_gather(piece.astype(jnp.bfloat16), "rot", axis=0, tiled=True)
+            term = jnp.dot(panel, gathered, preferred_element_type=jnp.float32)
+            product = term if product is None else product + term
+        if first:
+            squares = sum(jnp.sum(piece * piece) for piece in pieces)
+            factor = 1.7 / jnp.sqrt(jnp.sqrt(lax.psum(squares, ("dp", "rot"))))
+            return factor * (1.5 * tile.astype(jnp.float32) - 0.5 * (factor * factor) * product)
+        return 1.5 * tile.astype(jnp.float32) - 0.5 * product
 
+    new_tile = None
     columns = cross_tile
-    new_tile = None
     for iteration in range(ITERS):
-        rows_b = lax.all_gather(columns, "dp", axis=1, tiled=True)
-        gram_part = lax.psum_scatter(
-            lax.dot_general(
-                rows_b,
-                columns,
-                (((0,), (0,)), ((), ())),
-                preferred_element_type=jnp.float32,
-            ),
-            "rot",
-            scatter_dimension=0,
-            tiled=True,
-        )
-        if iteration == 0:
-            total = lax.psum(jnp.sum(gram_part * gram_part), ("dp", "rot"))
-            factor = 1.7 / jnp.sqrt(jnp.sqrt(total))
-            product = apply_gram(rows_b, gram_part.astype(jnp.bfloat16))
-            new_tile = factor * (
-                1.5 * columns.astype(jnp.float32) - 0.5 * (factor * factor) * product
-            )
-        else:
-            gram_b = gram_part.astype(jnp.bfloat16)
-            product = apply_gram(rows_b, gram_b)
-            new_tile = 1.5 * columns.astype(jnp.float32) - 0.5 * product
+        new_tile = gram_step(columns, iteration == 0)
         columns = new_tile.astype(jnp.bfloat16)
     new_rotation = (math.sqrt(width) * new_tile).astype(jnp.bfloat16)
     return (codebook, new_rotation)

time: 748 us -> 951 us (1.27)
  starting transfers between devices: 13.8 us -> 158 us
  waiting for transfers between devices: 562 us -> 603 us
    ppermute x0 -> x14, waiting for transfers between devices: none -> 240 us  [gram_step(): parts.append(lax.ppermute(tile, 'dp', pairs))]
    all_gather x4, waiting for transfers between devices: 229 us -> 87.8 us  [gram_step(): lax.all_gather(piece.astype(jnp.bfloat16), 'rot', axis=0, tiled=True)]
    ppermute x0 -> x14, starting transfers between devices: none -> 137 us  [gram_step(): parts.append(lax.ppermute(tile, 'dp', pairs))]
    reduce_scatter x2 -> x4, waiting for transfers between devices: 170 us -> 118 us  [gram_step(): lax.psum_scatter(lax.dot_general(panel, tile, (((0,), (0,)), ((), ())), p...]
    ppermute x7, waiting for transfers between devices: 55.1 us -> 37.8 us  [body(): lax.ppermute(tile_part((dp_index + shift) % dp_size), 'dp', pairs)]
    psum x1, waiting for transfers between devices: 73.9 us -> 84.8 us  [body(): total_sums, total_counts = lax.psum((shard_code_sums, local_counts), 'dp')]
    dot_general x4 -> x8, matrix products: 43 us -> 48.6 us  [the longest x4 24.4 us: gram_step(): term = jnp.dot(panel, gathered, preferred_element_type=jnp.float32)]
  transfers between devices with their start and end apart: 16 -> 32, of which waited for: 12 -> 19; matrix products, arithmetic and copies ran while one was open for 3% -> 7% of each run, Pallas kernels for 0% -> 0%
where the time goes in v5:
time: 951 us; the launch traced here: 950 us
  waiting for transfers between devices  603 us (63%)
  starting transfers between devices  158 us (17%)
  matrix products  80.1 us (8%)
  blocking collectives  50.5 us (5%)
  local copies, waits for them, and re-layouts  21.7 us (2%)
  other arithmetic  20.8 us (2%)
  between operations  16.1 us (2%)
    ppermute x14, waiting for transfers between devices, gram_step(): parts.append(lax.ppermute(tile, 'dp', pairs))  240 us
    ppermute x14, starting transfers between devices, gram_step(): parts.append(lax.ppermute(tile, 'dp', pairs))  137 us
    reduce_scatter x4, waiting for transfers between devices, gram_step(): lax.psum_scatter(lax.dot_general(panel, tile, (((0,), (0,)), ((), ())), p...  118 us
    all_gather x4, waiting for transfers between devices, gram_step(): lax.all_gather(piece.astype(jnp.bfloat16), 'rot', axis=0, tiled=True)  87.8 us
    psum x1, waiting for transfers between devices, body(): total_sums, total_counts = lax.psum((shard_code_sums, local_counts), 'dp')  84.8 us
    psum x1, blocking collectives, gram_step(): factor = 1.7 / jnp.sqrt(jnp.sqrt(lax.psum(squares, ('dp', 'rot'))))  39.5 us
    ppermute x7, waiting for transfers between devices, body(): lax.ppermute(tile_part((dp_index + shift) % dp_size), 'dp', pairs)  37.8 us
    all_gather x1, waiting for transfers between devices, body(): lax.all_gather(book.astype(jnp.bfloat16), 'rot', axis=0, tiled=True)  34.3 us
  transfers between devices with their start and end apart: 32, of which 19 were waited for; matrix products, arithmetic and copies ran while one was open for 7% of the time, Pallas kernels for 0%

profile of v5, /device:TPU:0, one launch (start us, length us, event | category | flops | bytes accessed | tf_op | source)
XLA Modules:
  0.0 950.3 jit_solution(7759961061396925088)
XLA Ops:
  7.2 7.9 fusion.15
  16.4 11.0 %all_gather.18 = s32[256,256]{0,1:T(8,128)S(1)} all-gather(s32[256,64]{0,1:T(8,128)S(1)} %copy-done.2), channel_id=1, replica_groups=mesh['dp'=8,'rot'=4] {'rot'}, dimensions={1}, use_global_device_ids=true | all-gather | bytes 327680 | tf_op jit(solution)/shard_map/all_gather | solution.py:23
  27.5 1.2 pad_maximum_fusion.12
  28.6 1.8 collective-permute-start.1
  30.4 3.0 collective-permute-start.2
  34.2 1.5 collective-permute-start.4
  35.7 3.4 convert_reduce_fusion
  39.1 5.1 collective-permute-done
  44.3 2.5 collective-permute-start.5
  47.6 10.1 %collective-permute-start.6 = (bf16[256,1056]{0,1:T(8,128)(2,1)S(1)}, bf16[256,1056]{0,1:T(8,128)(2,1)S(1)}, u32[]{:S(2)}, u32[]{:S(2)}) collective-permute-start(bf16[256,1056]{0,1:T(8,128)(2,1)S(1)} %get-tuple-element.22), channel_id=1, source_target_pairs={{0,28},{4,0},{8,4},{12,8},{16,12},{20,16},{24,20},{28,24},{1,29},{... | collective-permute-start | bytes 1622024 | tf_op jit(solution)/shard_map/ppermute | solution.py:32
  58.6 32.6 %collective-permute-done.2 = bf16[256,1056]{0,1:T(8,128)(2,1)S(1)} collective-permute-done((bf16[256,1056]{0,1:T(8,128)(2,1)S(1)}, bf16[256,1056]{0,1:T(8,128)(2,1)S(1)}, u32[]{:S(2)}, u32[]{:S(2)}) %collective-permute-start.2) | collective-permute-done | bytes 540704 | tf_op jit(solution)/shard_map/ppermute | solution.py:32
  93.1 0.9 constant_dynamic-update-slice_fusion.2
  94.8 1.3 convert_element_type.70
  96.1 5.1 fusion.3
  102.2 4.8 slice.8
  107.0 0.9 slice_convert_fusion
  107.9 84.8 %all-reduce.3.cloned.1.call-done = (f32[64,16,256]{2,1,0:T(8,128)}, f32[64,256]{1,0:T(8,128)}) async-done(((f32[64,16,256]{2,1,0:T(8,128)}, f32[64,256]{1,0:T(8,128)}), (f32[64,16,256]{2,1,0:T(8,128)}, f32[64,256]{1,0:T(8,128)})) %all-reduce.3.cloned.1.call-update) | async-done | bytes 1114128 | tf_op jit(solution)/shard_map/psum | solution.py:51
  193.5 2.5 fusion.14
  196.1 34.3 %all-gather.6.cloned.1.call-done = bf16[256,16,256]{2,1,0:T(8,128)(2,1)} async-done(((bf16[64,16,256]{2,1,0:T(8,128)(2,1)}), bf16[256,16,256]{2,1,0:T(8,128)(2,1)}) %all-gather.6.cloned.1.call-update) | async-done | bytes 2097168 | tf_op jit(solution)/shard_map/all_gather | solution.py:57
  230.4 1.0 fusion.40
  231.4 16.1 %fusion.5 = bf16[32,16,2048]{2,1,0:T(8,128)(2,1)S(1)} fusion(s32[32,2048]{1,0:T(8,128)S(1)} %bitcast.27, bf16[32,16,256]{2,1,0:T(8,128)(2,1)S(1)} %fusion.40), kind=kOutput, calls=%fused_computation.10 | convolution fusion | flops 554696704 | bytes 2621440 | tf_op jit(solution)/shard_map/lyg,lxg->lyx/dot_general | solution.py:61
  247.5 2.4 convolution_convert_fusion
  249.9 2.5 collective-permute-start.10
  252.4 2.8 collective-permute-start.12
  255.2 1.0 collective-permute-start.13
  256.2 54.1 %collective-permute-done.10 = bf16[1024,512]{0,1:T(8,128)(2,1)S(1)} collective-permute-done((bf16[1024,512]{0,1:T(8,128)(2,1)S(1)}, bf16[1024,512]{0,1:T(8,128)(2,1)S(1)}, u32[]{:S(2)}, u32[]{:S(2)}) %collective-permute-start.10) | collective-permute-done | bytes 1048608 | tf_op jit(solution)/shard_map/ppermute | solution.py:73
  310.5 9.1 collective-permute-done.12
  319.7 11.2 %collective-permute-done.13 = bf16[1024,512]{0,1:T(8,128)(2,1)S(1)} collective-permute-done((bf16[1024,512]{0,1:T(8,128)(2,1)S(1)}, bf16[1024,512]{0,1:T(8,128)(2,1)S(1)}, u32[]{:S(2)}, u32[]{:S(2)}) %collective-permute-start.13) | collective-permute-done | bytes 1048608 | tf_op jit(solution)/shard_map/ppermute | solution.py:73
  330.9 2.0 copy-done.3
  332.9 4.4 fusion.16
  337.4 62.2 %collective-permute-start.9 = (bf16[1024,512]{0,1:T(8,128)(2,1)S(1)}, bf16[1024,512]{0,1:T(8,128)(2,1)S(1)}, u32[]{:S(2)}, u32[]{:S(2)}) collective-permute-start(bf16[1024,512]{0,1:T(8,128)(2,1)S(1)} %convolution_convert_fusion), channel_id=1, source_target_pairs={{0,12},{4,16},{8,20},{12,24},{16,28},{20,0},{24,4},{28,8},{1,13},{... | collective-permute-start | bytes 3145736 | tf_op jit(solution)/shard_map/ppermute | solution.py:73
  399.8 23.4 %collective-permute-done.9 = bf16[1024,512]{0,1:T(8,128)(2,1)S(1)} collective-permute-done((bf16[1024,512]{0,1:T(8,128)(2,1)S(1)}, bf16[1024,512]{0,1:T(8,128)(2,1)S(1)}, u32[]{:S(2)}, u32[]{:S(2)}) %collective-permute-start.9) | collective-permute-done | bytes 1048608 | tf_op jit(solution)/shard_map/ppermute | solution.py:73
  423.2 22.5 %collective-permute-done.8 = bf16[1024,512]{0,1:T(8,128)(2,1)S(1)} collective-permute-done((bf16[1024,512]{0,1:T(8,128)(2,1)S(1)}, bf16[1024,512]{0,1:T(8,128)(2,1)S(1)}, u32[]{:S(2)}, u32[]{:S(2)}) %collective-permute-start.8) | collective-permute-done | bytes 1048608 | tf_op jit(solution)/shard_map/ppermute | solution.py:73
  445.7 1.0 copy-done.6
  446.6 7.7 fusion.7
  454.4 3.1 multiply_reduce_fusion
  457.6 59.0 %reduce-scatter.8.cloned.1.call-done = f32[512,512]{1,0:T(8,128)} async-done(((f32[2048,512]{1,0:T(8,128)}), f32[512,512]{1,0:T(8,128)}) %reduce-scatter.8.cloned.1.call-update) | async-done | bytes 1048592 | tf_op jit(solution)/shard_map/reduce_scatter | solution.py:77
  516.6 3.3 multiply_reduce_fusion.1
  521.2 39.5 %psum.23 = f32[]{:T(128)} all-reduce(f32[]{:T(128)S(6)} %add.115), channel_id=1, replica_groups=mesh['dp'=8,'rot'=4] {'dp','rot'}, use_global_device_ids=true, to_apply=%region_8.9 | all-reduce | flops 1 | bytes 8 | tf_op jit(solution)/shard_map/psum | solution.py:94
  561.3 7.0 fusion.17
  568.3 22.6 %all-gather.8.cloned.1.call-done = bf16[2048,512]{1,0:T(8,128)(2,1)} async-done(((bf16[512,512]{1,0:T(8,128)(2,1)}), bf16[2048,512]{1,0:T(8,128)(2,1)}) %all-gather.8.cloned.1.call-update) | async-done | bytes 2097168 | tf_op jit(solution)/shard_map/all_gather | solution.py:89
  590.9 5.4 multiply_convert_fusion.1
  596.3 2.5 collective-permute-start.17
  598.8 2.8 collective-permute-start.19
  601.6 1.0 collective-permute-start.20
  602.6 54.1 %collective-permute-done.17 = bf16[1024,512]{0,1:T(8,128)(2,1)S(1)} collective-permute-done((bf16[1024,512]{0,1:T(8,128)(2,1)S(1)}, bf16[1024,512]{0,1:T(8,128)(2,1)S(1)}, u32[]{:S(2)}, u32[]{:S(2)}) %collective-permute-start.17) | collective-permute-done | bytes 1048608 | tf_op jit(solution)/shard_map/ppermute | solution.py:73
  656.9 9.1 collective-permute-done.19
  666.1 11.2 %collective-permute-done.20 = bf16[1024,512]{0,1:T(8,128)(2,1)S(1)} collective-permute-done((bf16[1024,512]{0,1:T(8,128)(2,1)S(1)}, bf16[1024,512]{0,1:T(8,128)(2,1)S(1)}, u32[]{:S(2)}, u32[]{:S(2)}) %collective-permute-start.20) | collective-permute-done | bytes 1048608 | tf_op jit(solution)/shard_map/ppermute | solution.py:73
  677.3 2.0 copy-done.4
  679.3 4.4 fusion.18
  683.8 62.2 %collective-permute-start.16 = (bf16[1024,512]{0,1:T(8,128)(2,1)S(1)}, bf16[1024,512]{0,1:T(8,128)(2,1)S(1)}, u32[]{:S(2)}, u32[]{:S(2)}) collective-permute-start(bf16[1024,512]{0,1:T(8,128)(2,1)S(1)} %multiply_convert_fusion.1), channel_id=1, source_target_pairs={{0,12},{4,16},{8,20},{12,24},{16,28},{20,0},{24,4},{28,8},{1,13},{... | collective-permute-start | bytes 3145736 | tf_op jit(solution)/shard_map/ppermute | solution.py:73
  746.2 23.4 %collective-permute-done.16 = bf16[1024,512]{0,1:T(8,128)(2,1)S(1)} collective-permute-done((bf16[1024,512]{0,1:T(8,128)(2,1)S(1)}, bf16[1024,512]{0,1:T(8,128)(2,1)S(1)}, u32[]{:S(2)}, u32[]{:S(2)}) %collective-permute-start.16) | collective-permute-done | bytes 1048608 | tf_op jit(solution)/shard_map/ppermute | solution.py:73
  769.6 22.5 %collective-permute-done.15 = bf16[1024,512]{0,1:T(8,128)(2,1)S(1)} collective-permute-done((bf16[1024,512]{0,1:T(8,128)(2,1)S(1)}, bf16[1024,512]{0,1:T(8,128)(2,1)S(1)}, u32[]{:S(2)}, u32[]{:S(2)}) %collective-permute-start.15) | collective-permute-done | bytes 1048608 | tf_op jit(solution)/shard_map/ppermute | solution.py:73
  792.1 1.0 copy-done.7
  793.0 1.0 copy-done.8
  794.0 7.7 fusion.6
  801.8 2.1 convert_element_type.91
  804.0 59.1 %reduce-scatter.12.cloned.1.call-done = f32[512,512]{1,0:T(8,128)} async-done(((f32[2048,512]{1,0:T(8,128)}), f32[512,512]{1,0:T(8,128)}) %reduce-scatter.12.cloned.1.call-update) | async-done | bytes 1048592 | tf_op jit(solution)/shard_map/reduce_scatter | solution.py:77
  863.1 2.1 convert_element_type.90
  865.2 34.8 %all-gather.14.cloned.1.call-done = bf16[2048,512]{1,0:T(8,128)(2,1)} async-done(((bf16[512,512]{1,0:T(8,128)(2,1)}), bf16[2048,512]{1,0:T(8,128)(2,1)}) %all-gather.14.cloned.1.call-update) | async-done | bytes 2097168 | tf_op jit(solution)/shard_map/all_gather | solution.py:89
  900.0 6.6 fusion.19
  906.6 30.4 %all-gather.12.cloned.1.call-done = bf16[2048,512]{1,0:T(8,128)(2,1)} async-done(((bf16[512,512]{1,0:T(8,128)(2,1)}), bf16[2048,512]{1,0:T(8,128)(2,1)}) %all-gather.12.cloned.1.call-update) | async-done | bytes 2097168 | tf_op jit(solution)/shard_map/all_gather | solution.py:89
  937.0 5.4 multiply_convert_fusion
  942.4 1.3 copy.27
  (73 shorter events, 9.7 us)
Async XLA Ops:
  7.2 87.7 %reduce-scatter.6.cloned.1.call-start = ((), (), s32[]{:S(2)}) async-start(), calls=%async_computation.5 | async-start | bytes 5242880 | tf_op jit(solution)/shard_map/reduce_scatter | solution.py:37
  15.1 1.0 copy-start.1
  15.1 1.3 copy-start.2
  15.2 177.5 %all-reduce.3.cloned.1.call-start = ((), (), s32[]{:S(2)}) async-start(), calls=%async_computation.15 | async-start | bytes 2228224 | tf_op jit(solution)/shard_map/psum | solution.py:51
  28.6 15.7 %collective-permute-start = (bf16[256,1056]{0,1:T(8,128)(2,1)S(1)}, bf16[256,1056]{0,1:T(8,128)(2,1)S(1)}, u32[]{:S(2)}, u32[]{:S(2)}) collective-permute-start(bf16[256,1056]{0,1:T(8,128)(2,1)S(1)} %get-tuple-element.23), channel_id=1, source_target_pairs={{0,4},{4,8},{8,12},{12,16},{16,20},{20,24},{24,28},{28,0},{1,5},{5... | collective-permute-start | bytes 1622024 | tf_op jit(solution)/shard_map/ppermute | solution.py:32
  28.6 19.0 %collective-permute-start.1 = (bf16[256,1056]{0,1:T(8,128)(2,1)S(1)}, bf16[256,1056]{0,1:T(8,128)(2,1)S(1)}, u32[]{:S(2)}, u32[]{:S(2)}) collective-permute-start(bf16[256,1056]{0,1:T(8,128)(2,1)S(1)} %get-tuple-element.24), channel_id=1, source_target_pairs={{0,8},{4,12},{8,16},{12,20},{16,24},{20,28},{24,0},{28,4},{1,9},{5... | collective-permute-start | bytes 1622024 | tf_op jit(solution)/shard_map/ppermute | solution.py:32
  30.4 60.9 %collective-permute-start.2 = (bf16[256,1056]{0,1:T(8,128)(2,1)S(1)}, bf16[256,1056]{0,1:T(8,128)(2,1)S(1)}, u32[]{:S(2)}, u32[]{:S(2)}) collective-permute-start(bf16[256,1056]{0,1:T(8,128)(2,1)S(1)} %get-tuple-element.25), channel_id=1, source_target_pairs={{0,12},{4,16},{8,20},{12,24},{16,28},{20,0},{24,4},{28,8},{1,13},{... | collective-permute-start | bytes 1622024 | tf_op jit(solution)/shard_map/ppermute | solution.py:32
  33.3 58.8 %collective-permute-start.3 = (bf16[256,1056]{0,1:T(8,128)(2,1)S(1)}, bf16[256,1056]{0,1:T(8,128)(2,1)S(1)}, u32[]{:S(2)}, u32[]{:S(2)}) collective-permute-start(bf16[256,1056]{0,1:T(8,128)(2,1)S(1)} %get-tuple-element.26), channel_id=1, source_target_pairs={{0,16},{4,20},{8,24},{12,28},{16,0},{20,4},{24,8},{28,12},{1,17},{... | collective-permute-start | bytes 1622024 | tf_op jit(solution)/shard_map/ppermute | solution.py:32
  34.2 58.8 %collective-permute-start.4 = (bf16[256,1056]{0,1:T(8,128)(2,1)S(1)}, bf16[256,1056]{0,1:T(8,128)(2,1)S(1)}, u32[]{:S(2)}, u32[]{:S(2)}) collective-permute-start(bf16[256,1056]{0,1:T(8,128)(2,1)S(1)} %get-tuple-element.27), channel_id=1, source_target_pairs={{0,20},{4,24},{8,28},{12,0},{16,4},{20,8},{24,12},{28,16},{1,21},{... | collective-permute-start | bytes 1622024 | tf_op jit(solution)/shard_map/ppermute | solution.py:32
  44.3 49.7 %collective-permute-start.5 = (bf16[256,1056]{0,1:T(8,128)(2,1)S(1)}, bf16[256,1056]{0,1:T(8,128)(2,1)S(1)}, u32[]{:S(2)}, u32[]{:S(2)}) collective-permute-start(bf16[256,1056]{0,1:T(8,128)(2,1)S(1)} %get-tuple-element.28), channel_id=1, source_target_pairs={{0,24},{4,28},{8,0},{12,4},{16,8},{20,12},{24,16},{28,20},{1,25},{... | collective-permute-start | bytes 1622024 | tf_op jit(solution)/shard_map/ppermute | solution.py:32
  47.6 53.6 %collective-permute-start.6 = (bf16[256,1056]{0,1:T(8,128)(2,1)S(1)}, bf16[256,1056]{0,1:T(8,128)(2,1)S(1)}, u32[]{:S(2)}, u32[]{:S(2)}) collective-permute-start(bf16[256,1056]{0,1:T(8,128)(2,1)S(1)} %get-tuple-element.22), channel_id=1, source_target_pairs={{0,28},{4,0},{8,4},{12,8},{16,12},{20,16},{24,20},{28,24},{1,29},{... | collective-permute-start | bytes 1622024 | tf_op jit(solution)/shard_map/ppermute | solution.py:32
  101.2 129.2 %all-gather.6.cloned.1.call-start = ((), (), s32[]{:S(2)}) async-start(), calls=%async_computation.6 | async-start | bytes 2621440 | tf_op jit(solution)/shard_map/all_gather | solution.py:57
  196.1 258.3 %reduce-scatter.10.cloned.1.call-start = ((), (), s32[]{:S(2)}) async-start(), calls=%async_computation.8 | async-start | bytes 5242880 | tf_op jit(solution)/shard_map/reduce_scatter | solution.py:77
  231.4 16.1 %copy-start = (bf16[2048,1024]{0,1:T(8,128)(2,1)S(1)}, bf16[2048,1024]{0,1:T(8,128)(2,1)}, u32[]{:S(2)}) copy-start(bf16[2048,1024]{0,1:T(8,128)(2,1)} %slice.8) | copy-start | bytes 12582916
  249.9 60.5 %collective-permute-start.10 = (bf16[1024,512]{0,1:T(8,128)(2,1)S(1)}, bf16[1024,512]{0,1:T(8,128)(2,1)S(1)}, u32[]{:S(2)}, u32[]{:S(2)}) collective-permute-start(bf16[1024,512]{0,1:T(8,128)(2,1)S(1)} %convolution_convert_fusion), channel_id=1, source_target_pairs={{0,16},{4,20},{8,24},{12,28},{16,0},{20,4},{24,8},{28,12},{1,17},{... | collective-permute-start | bytes 3145736 | tf_op jit(solution)/shard_map/ppermute | solution.py:73
  252.4 58.1 %collective-permute-start.11 = (bf16[1024,512]{0,1:T(8,128)(2,1)S(1)}, bf16[1024,512]{0,1:T(8,128)(2,1)S(1)}, u32[]{:S(2)}, u32[]{:S(2)}) collective-permute-start(bf16[1024,512]{0,1:T(8,128)(2,1)S(1)} %convolution_convert_fusion), channel_id=1, source_target_pairs={{0,20},{4,24},{8,28},{12,0},{16,4},{20,8},{24,12},{28,16},{1,21},{... | collective-permute-start | bytes 3145736 | tf_op jit(solution)/shard_map/ppermute | solution.py:73
  252.4 67.2 %collective-permute-start.12 = (bf16[1024,512]{0,1:T(8,128)(2,1)S(1)}, bf16[1024,512]{0,1:T(8,128)(2,1)S(1)}, u32[]{:S(2)}, u32[]{:S(2)}) collective-permute-start(bf16[1024,512]{0,1:T(8,128)(2,1)S(1)} %convolution_convert_fusion), channel_id=1, source_target_pairs={{0,24},{4,28},{8,0},{12,4},{16,8},{20,12},{24,16},{28,20},{1,25},{... | collective-permute-start | bytes 3145736 | tf_op jit(solution)/shard_map/ppermute | solution.py:73
  255.2 75.6 %collective-permute-start.13 = (bf16[1024,512]{0,1:T(8,128)(2,1)S(1)}, bf16[1024,512]{0,1:T(8,128)(2,1)S(1)}, u32[]{:S(2)}, u32[]{:S(2)}) collective-permute-start(bf16[1024,512]{0,1:T(8,128)(2,1)S(1)} %convolution_convert_fusion), channel_id=1, source_target_pairs={{0,28},{4,0},{8,4},{12,8},{16,12},{20,16},{24,20},{28,24},{1,29},{... | collective-permute-start | bytes 3145736 | tf_op jit(solution)/shard_map/ppermute | solution.py:73
  330.9 2.0 copy-start.3
  337.3 179.3 %reduce-scatter.8.cloned.1.call-start = ((), (), s32[]{:S(2)}) async-start(), calls=%async_computation.7 | async-start | bytes 5242880 | tf_op jit(solution)/shard_map/reduce_scatter | solution.py:77
  337.4 85.8 %collective-permute-start.9 = (bf16[1024,512]{0,1:T(8,128)(2,1)S(1)}, bf16[1024,512]{0,1:T(8,128)(2,1)S(1)}, u32[]{:S(2)}, u32[]{:S(2)}) collective-permute-start(bf16[1024,512]{0,1:T(8,128)(2,1)S(1)} %convolution_convert_fusion), channel_id=1, source_target_pairs={{0,12},{4,16},{8,20},{12,24},{16,28},{20,0},{24,4},{28,8},{1,13},{... | collective-permute-start | bytes 3145736 | tf_op jit(solution)/shard_map/ppermute | solution.py:73
  399.6 46.0 %collective-permute-start.8 = (bf16[1024,512]{0,1:T(8,128)(2,1)S(1)}, bf16[1024,512]{0,1:T(8,128)(2,1)S(1)}, u32[]{:S(2)}, u32[]{:S(2)}) collective-permute-start(bf16[1024,512]{0,1:T(8,128)(2,1)S(1)} %convolution_convert_fusion), channel_id=1, source_target_pairs={{0,8},{4,12},{8,16},{12,20},{16,24},{20,28},{24,0},{28,4},{1,9},{5... | collective-permute-start | bytes 3145736 | tf_op jit(solution)/shard_map/ppermute | solution.py:73
  399.6 46.0 %collective-permute-start.7 = (bf16[1024,512]{0,1:T(8,128)(2,1)S(1)}, bf16[1024,512]{0,1:T(8,128)(2,1)S(1)}, u32[]{:S(2)}, u32[]{:S(2)}) collective-permute-start(bf16[1024,512]{0,1:T(8,128)(2,1)S(1)} %convolution_convert_fusion), channel_id=1, source_target_pairs={{0,4},{4,8},{8,12},{12,16},{16,20},{20,24},{24,28},{28,0},{1,5},{5... | collective-permute-start | bytes 3145736 | tf_op jit(solution)/shard_map/ppermute | solution.py:73
  445.6 8.7 copy-start.5
  445.7 1.0 copy-start.6
  454.3 107.0 %all-gather.10.cloned.1.call-start = ((), (), s32[]{:S(2)}) async-start(), calls=%async_computation.10 | async-start | bytes 2621440 | tf_op jit(solution)/shard_map/all_gather | solution.py:89
  457.6 133.3 %all-gather.8.cloned.1.call-start = ((), (), s32[]{:S(2)}) async-start(), calls=%async_computation.9 | async-start | bytes 2621440 | tf_op jit(solution)/shard_map/all_gather | solution.py:89
  519.9 281.9 %reduce-scatter.14.cloned.1.call-start = ((), (), s32[]{:S(2)}) async-start(), calls=%async_computation.13 | async-start | bytes 5242880 | tf_op jit(solution)/shard_map/reduce_scatter | solution.py:77
  596.3 60.5 %collective-permute-start.17 = (bf16[1024,512]{0,1:T(8,128)(2,1)S(1)}, bf16[1024,512]{0,1:T(8,128)(2,1)S(1)}, u32[]{:S(2)}, u32[]{:S(2)}) collective-permute-start(bf16[1024,512]{0,1:T(8,128)(2,1)S(1)} %multiply_convert_fusion.1), channel_id=1, source_target_pairs={{0,16},{4,20},{8,24},{12,28},{16,0},{20,4},{24,8},{28,12},{1,17},{... | collective-permute-start | bytes 3145736 | tf_op jit(solution)/shard_map/ppermute | solution.py:73
  598.8 58.1 %collective-permute-start.18 = (bf16[1024,512]{0,1:T(8,128)(2,1)S(1)}, bf16[1024,512]{0,1:T(8,128)(2,1)S(1)}, u32[]{:S(2)}, u32[]{:S(2)}) collective-permute-start(bf16[1024,512]{0,1:T(8,128)(2,1)S(1)} %multiply_convert_fusion.1), channel_id=1, source_target_pairs={{0,20},{4,24},{8,28},{12,0},{16,4},{20,8},{24,12},{28,16},{1,21},{... | collective-permute-start | bytes 3145736 | tf_op jit(solution)/shard_map/ppermute | solution.py:73
  598.8 67.2 %collective-permute-start.19 = (bf16[1024,512]{0,1:T(8,128)(2,1)S(1)}, bf16[1024,512]{0,1:T(8,128)(2,1)S(1)}, u32[]{:S(2)}, u32[]{:S(2)}) collective-permute-start(bf16[1024,512]{0,1:T(8,128)(2,1)S(1)} %multiply_convert_fusion.1), channel_id=1, source_target_pairs={{0,24},{4,28},{8,0},{12,4},{16,8},{20,12},{24,16},{28,20},{1,25},{... | collective-permute-start | bytes 3145736 | tf_op jit(solution)/shard_map/ppermute | solution.py:73
  601.6 75.6 %collective-permute-start.20 = (bf16[1024,512]{0,1:T(8,128)(2,1)S(1)}, bf16[1024,512]{0,1:T(8,128)(2,1)S(1)}, u32[]{:S(2)}, u32[]{:S(2)}) collective-permute-start(bf16[1024,512]{0,1:T(8,128)(2,1)S(1)} %multiply_convert_fusion.1), channel_id=1, source_target_pairs={{0,28},{4,0},{8,4},{12,8},{16,12},{20,16},{24,20},{28,24},{1,29},{... | collective-permute-start | bytes 3145736 | tf_op jit(solution)/shard_map/ppermute | solution.py:73
  677.3 2.0 copy-start.4
  683.8 179.3 %reduce-scatter.12.cloned.1.call-start = ((), (), s32[]{:S(2)}) async-start(), calls=%async_computation.11 | async-start | bytes 5242880 | tf_op jit(solution)/shard_map/reduce_scatter | solution.py:77
  683.8 85.8 %collective-permute-start.16 = (bf16[1024,512]{0,1:T(8,128)(2,1)S(1)}, bf16[1024,512]{0,1:T(8,128)(2,1)S(1)}, u32[]{:S(2)}, u32[]{:S(2)}) collective-permute-start(bf16[1024,512]{0,1:T(8,128)(2,1)S(1)} %multiply_convert_fusion.1), channel_id=1, source_target_pairs={{0,12},{4,16},{8,20},{12,24},{16,28},{20,0},{24,4},{28,8},{1,13},{... | collective-permute-start | bytes 3145736 | tf_op jit(solution)/shard_map/ppermute | solution.py:73
  746.1 46.0 %collective-permute-start.15 = (bf16[1024,512]{0,1:T(8,128)(2,1)S(1)}, bf16[1024,512]{0,1:T(8,128)(2,1)S(1)}, u32[]{:S(2)}, u32[]{:S(2)}) collective-permute-start(bf16[1024,512]{0,1:T(8,128)(2,1)S(1)} %multiply_convert_fusion.1), channel_id=1, source_target_pairs={{0,8},{4,12},{8,16},{12,20},{16,24},{20,28},{24,0},{28,4},{1,9},{5... | collective-permute-start | bytes 3145736 | tf_op jit(solution)/shard_map/ppermute | solution.py:73
  746.1 46.0 %collective-permute-start.14 = (bf16[1024,512]{0,1:T(8,128)(2,1)S(1)}, bf16[1024,512]{0,1:T(8,128)(2,1)S(1)}, u32[]{:S(2)}, u32[]{:S(2)}) collective-permute-start(bf16[1024,512]{0,1:T(8,128)(2,1)S(1)} %multiply_convert_fusion.1), channel_id=1, source_target_pairs={{0,4},{4,8},{8,12},{12,16},{16,20},{20,24},{24,28},{28,0},{1,5},{5... | collective-permute-start | bytes 3145736 | tf_op jit(solution)/shard_map/ppermute | solution.py:73
  792.1 1.0 copy-start.7
  793.0 1.0 copy-start.8
  801.7 98.2 %all-gather.14.cloned.1.call-start = ((), (), s32[]{:S(2)}) async-start(), calls=%async_computation.14 | async-start | bytes 2621440 | tf_op jit(solution)/shard_map/all_gather | solution.py:89
  803.9 133.1 %all-gather.12.cloned.1.call-start = ((), (), s32[]{:S(2)}) async-start(), calls=%async_computation.12 | async-start | bytes 2621440 | tf_op jit(solution)/shard_map/all_gather | solution.py:89
Sparse Core Ops, SparseCore 0:
  15.3 55.9 reduce-scatter.5
  101.4 91.2 all-reduce.2
  196.2 34.1 all-gather.5
  337.5 111.4 reduce-scatter.9
  454.5 62.1 reduce-scatter.7
  518.3 35.4 all-gather.9
  555.7 35.1 all-gather.7
  683.9 111.4 reduce-scatter.13
  801.8 61.1 reduce-scatter.11
  864.7 35.1 all-gather.13
  901.8 35.1 all-gather.11

commit v6 on v4

--- a/solution.py
+++ b/solution.py
@@ -83,21 +83,21 @@
                 columns,
                 (((0,), (0,)), ((), ())),
                 preferred_element_type=jnp.float32,
-            ),
+            ).astype(jnp.bfloat16),
             "rot",
             scatter_dimension=0,
             tiled=True,
         )
         if iteration == 0:
-            total = lax.psum(jnp.sum(gram_part * gram_part), ("dp", "rot"))
+            gram_f = gram_part.astype(jnp.float32)
+            total = lax.psum(jnp.sum(gram_f * gram_f), ("dp", "rot"))
             factor = 1.7 / jnp.sqrt(jnp.sqrt(total))
-            product = apply_gram(rows_b, gram_part.astype(jnp.bfloat16))
+            product = apply_gram(rows_b, gram_part)
             new_tile = factor * (
                 1.5 * columns.astype(jnp.float32) - 0.5 * (factor * factor) * product
             )
         else:
-            gram_b = gram_part.astype(jnp.bfloat16)
-            product = apply_gram(rows_b, gram_b)
+            product = apply_gram(rows_b, gram_part)
             new_tile = 1.5 * columns.astype(jnp.float32) - 0.5 * product
         columns = new_tile.astype(jnp.bfloat16)
     new_rotation = (math.sqrt(width) * new_tile).astype(jnp.bfloat16)

time: 748 us -> 675 us (0.902)
  waiting for transfers between devices: 562 us -> 489 us
    reduce_scatter x2, waiting for transfers between devices: 170 us -> 102 us  [body(): lax.psum_scatter(lax.dot_general(rows_b, columns, (((0,), (0,)), ((), ())...]
    ppermute x7, waiting for transfers between devices: 55.1 us -> 37.8 us  [body(): lax.ppermute(tile_part((dp_index + shift) % dp_size), 'dp', pairs)]
    psum x1, waiting for transfers between devices: 73.9 us -> 85 us  [body(): total_sums, total_counts = lax.psum((shard_code_sums, local_counts), 'dp')]
  transfers between devices with their start and end apart: 16 -> 16, of which waited for: 12 -> 10; matrix products, arithmetic and copies ran while one was open for 3% -> 4% of each run, Pallas kernels for 0% -> 0%
where the time goes in v6:
time: 675 us
  waiting for transfers between devices  489 us (72%)
  matrix products  73 us (11%)
  blocking collectives  51.4 us (8%)
  starting transfers between devices  20.5 us (3%)
  between operations  14.8 us (2%)
  local copies, waits for them, and re-layouts  13 us (2%)
  other arithmetic  12.6 us (2%)
    all_gather x2, waiting for transfers between devices, body(): rows_b = lax.all_gather(columns, 'dp', axis=1, tiled=True)  164 us
    reduce_scatter x2, waiting for transfers between devices, body(): lax.psum_scatter(lax.dot_general(rows_b, columns, (((0,), (0,)), ((), ())...  102 us
    psum x1, waiting for transfers between devices, body(): total_sums, total_counts = lax.psum((shard_code_sums, local_counts), 'dp')  85 us
    all_gather x2, waiting for transfers between devices, apply_gram(): lax.all_gather(gram_b, 'rot', axis=0, tiled=True)  66 us
    psum x1, blocking collectives, body(): total = lax.psum(jnp.sum(gram_f * gram_f), ('dp', 'rot'))  40.3 us
    ppermute x7, waiting for transfers between devices, body(): lax.ppermute(tile_part((dp_index + shift) % dp_size), 'dp', pairs)  37.8 us
    all_gather x1, waiting for transfers between devices, body(): lax.all_gather(book.astype(jnp.bfloat16), 'rot', axis=0, tiled=True)  34.3 us
    dot_general x2, matrix products, body(): lax.dot_general(rows_b, columns, (((0,), (0,)), ((), ())), preferred_elem...  20.3 us
  transfers between devices with their start and end apart: 16, of which 10 were waited for; matrix products, arithmetic and copies ran while one was open for 4% of the time, Pallas kernels for 0%

profile of v6, /device:TPU:0, one launch (start us, length us, event | category | flops | bytes accessed | tf_op | source)
XLA Modules:
  0.0 674.6 jit_solution(4834777221851214295)
XLA Ops:
  7.2 0.0 reduce-scatter.4.cloned.1.call-start
  7.2 7.9 %fusion.9 = f32[4096,256]{1,0:T(8,128)} fusion(bf16[1024,4096]{1,0:T(8,128)(2,1)} %param.4, bf16[256,1024]{1,0:T(8,128)(2,1)} %param.3), kind=kOutput, calls=%fused_computation.44 | convolution fusion | flops 2147483648 | bytes 13107200 | tf_op jit(solution)/shard_map/dot_general | solution.py:38
  15.1 0.0 reduce-scatter.4.cloned.1.call-update
  15.1 0.0 all-reduce.3.cloned.1.call-start
  15.3 0.9 copy-done.3
  16.2 0.2 copy.14
  16.4 11.0 %all_gather.18 = s32[256,256]{0,1:T(8,128)S(1)} all-gather(s32[256,64]{0,1:T(8,128)S(1)} %copy-done.4), channel_id=1, replica_groups=mesh['dp'=8,'rot'=4] {'rot'}, dimensions={1}, use_global_device_ids=true | all-gather | bytes 327680 | tf_op jit(solution)/shard_map/all_gather | solution.py:23
  27.5 1.2 pad_maximum_fusion.6
  28.7 0.0 collective-permute-start
  28.7 1.8 collective-permute-start.1
  30.4 3.0 collective-permute-start.2
  33.4 0.9 collective-permute-start.3
  34.2 1.5 collective-permute-start.4
  35.7 3.4 convert_reduce_fusion
  39.2 5.1 collective-permute-done
  44.3 2.5 collective-permute-start.5
  46.8 0.9 constant_dynamic-update-slice_fusion.6
  47.7 0.0 collective-permute-done.1
  47.7 10.1 %collective-permute-start.6 = (bf16[256,1056]{0,1:T(8,128)(2,1)S(1)}, bf16[256,1056]{0,1:T(8,128)(2,1)S(1)}, u32[]{:S(2)}, u32[]{:S(2)}) collective-permute-start(bf16[256,1056]{0,1:T(8,128)(2,1)S(1)} %get-tuple-element.14), channel_id=1, source_target_pairs={{0,28},{4,0},{8,4},{12,8},{16,12},{20,16},{24,20},{28,24},{1,29},{... | collective-permute-start | bytes 1622024 | tf_op jit(solution)/shard_map/ppermute | solution.py:32
  57.8 0.9 constant_dynamic-update-slice_fusion.5
  58.7 32.6 %collective-permute-done.2 = bf16[256,1056]{0,1:T(8,128)(2,1)S(1)} collective-permute-done((bf16[256,1056]{0,1:T(8,128)(2,1)S(1)}, bf16[256,1056]{0,1:T(8,128)(2,1)S(1)}, u32[]{:S(2)}, u32[]{:S(2)}) %collective-permute-start.2) | collective-permute-done | bytes 540704 | tf_op jit(solution)/shard_map/ppermute | solution.py:32
  91.3 0.9 constant_dynamic-update-slice_fusion.4
  92.2 0.9 constant_dynamic-update-slice_fusion.3
  93.1 0.9 constant_dynamic-update-slice_fusion.2
  94.0 0.9 constant_dynamic-update-slice_fusion.1
  94.8 1.3 convert_element_type.67
  96.1 5.1 fusion.3
  101.2 0.0 all-reduce.3.cloned.1.call-update
  101.2 0.0 all-gather.6.cloned.1.call-start
  101.3 0.9 constant_dynamic-update-slice_fusion
  102.2 4.8 slice.8
  107.0 0.9 slice_convert_fusion
  107.9 85.0 %all-reduce.3.cloned.1.call-done = (f32[64,16,256]{2,1,0:T(8,128)}, f32[64,256]{1,0:T(8,128)}) async-done(((f32[64,16,256]{2,1,0:T(8,128)}, f32[64,256]{1,0:T(8,128)}), (f32[64,16,256]{2,1,0:T(8,128)}, f32[64,256]{1,0:T(8,128)})) %all-reduce.3.cloned.1.call-update) | async-done | bytes 1114128 | tf_op jit(solution)/shard_map/psum | solution.py:51
  192.9 0.8 broadcast_maximum_fusion
  193.7 2.5 fusion.8
  196.2 0.0 all-gather.6.cloned.1.call-update
  196.3 0.0 all-gather.8.cloned.1.call-start
  196.3 34.3 %all-gather.6.cloned.1.call-done = bf16[256,16,256]{2,1,0:T(8,128)(2,1)} async-done(((bf16[64,16,256]{2,1,0:T(8,128)(2,1)}), bf16[256,16,256]{2,1,0:T(8,128)(2,1)}) %all-gather.6.cloned.1.call-update) | async-done | bytes 2097168 | tf_op jit(solution)/shard_map/all_gather | solution.py:57
  230.6 1.0 fusion.26
  231.6 16.1 %fusion.5 = bf16[32,16,2048]{2,1,0:T(8,128)(2,1)S(1)} fusion(s32[32,2048]{1,0:T(8,128)S(1)} %bitcast.23, bf16[32,16,256]{2,1,0:T(8,128)(2,1)S(1)} %fusion.26), kind=kOutput, calls=%fused_computation.10 | convolution fusion | flops 554696704 | bytes 2621440 | tf_op jit(solution)/shard_map/lyg,lxg->lyx/dot_general | solution.py:61
  247.7 3.3 convolution_convert_fusion.2
  251.0 0.0 all-gather.8.cloned.1.call-update
  251.0 0.2 reduce-scatter.6.cloned.1.call-start
  251.3 82.0 %all-gather.8.cloned.1.call-done = bf16[1024,4096]{1,0:T(8,128)(2,1)} async-done(((bf16[1024,512]{1,0:T(8,128)(2,1)}), bf16[1024,4096]{1,0:T(8,128)(2,1)}) %all-gather.8.cloned.1.call-update) | async-done | bytes 8388624 | tf_op jit(solution)/shard_map/all_gather | solution.py:79
  333.2 10.2 %convolution_convert_fusion.1 = bf16[4096,512]{1,0:T(8,128)(2,1)} fusion(bf16[1024,4096]{1,0:T(8,128)(2,1)} %all-gather.8.cloned.1.call-done, bf16[1024,512]{1,0:T(8,128)(2,1)} %convolution_convert_fusion.2), kind=kOutput, calls=%fused_computation.9 | convolution fusion | flops 4297064448 | bytes 13631488 | tf_op jit(solution)/shard_map/dot_general | solution.py:81
  343.4 0.0 reduce-scatter.6.cloned.1.call-update
  343.4 0.0 all-gather.10.cloned.1.call-start
  343.5 51.2 %reduce-scatter.6.cloned.1.call-done = bf16[1024,512]{1,0:T(8,128)(2,1)} async-done(((bf16[4096,512]{1,0:T(8,128)(2,1)}), bf16[1024,512]{1,0:T(8,128)(2,1)}) %reduce-scatter.6.cloned.1.call-update) | async-done | bytes 1048592 | tf_op jit(solution)/shard_map/reduce_scatter | solution.py:80
  394.7 0.0 all-gather.10.cloned.1.call-update
  394.7 0.0 all-gather.12.cloned.1.call-start
  394.7 2.4 multiply_reduce_fusion
  397.2 40.3 %psum.23 = f32[]{:T(128)} all-reduce(f32[]{:T(128)} %multiply_reduce_fusion), channel_id=1, replica_groups=mesh['dp'=8,'rot'=4] {'dp','rot'}, use_global_device_ids=true, to_apply=%region_6.7 | all-reduce | flops 1 | bytes 8 | tf_op jit(solution)/shard_map/psum | solution.py:93
  438.2 11.5 %all-gather.10.cloned.1.call-done = bf16[4096,512]{1,0:T(8,128)(2,1)} async-done(((bf16[1024,512]{1,0:T(8,128)(2,1)}), bf16[4096,512]{1,0:T(8,128)(2,1)}) %all-gather.10.cloned.1.call-update) | async-done | bytes 4194320 | tf_op jit(solution)/shard_map/all_gather | solution.py:72
  449.8 10.1 %multiply_convert_fusion.1 = bf16[1024,512]{1,0:T(8,128)(2,1)} fusion(bf16[1024,512]{1,0:T(8,128)(2,1)S(1)} %copy-done.1, bf16[1024,4096]{1,0:T(8,128)(2,1)} %all-gather.8.cloned.1.call-done, bf16[4096,512]{1,0:T(8,128)(2,1)} %all-gather.10.cloned.1.call-done, f32[]{:T(128)S(6)} %mul.76, f32[]{:T(128)S(6)} %div.13), kind=kOutput, calls=%fused_computation.12 | convolution fusion | flops 4298113024 | bytes 14680072 | tf_op jit(solution)/shard_map/dot_general | solution.py:70
  459.9 0.0 all-gather.12.cloned.1.call-update
  459.9 0.3 reduce-scatter.8.cloned.1.call-start
  460.2 81.9 %all-gather.12.cloned.1.call-done = bf16[1024,4096]{1,0:T(8,128)(2,1)} async-done(((bf16[1024,512]{1,0:T(8,128)(2,1)}), bf16[1024,4096]{1,0:T(8,128)(2,1)}) %all-gather.12.cloned.1.call-update) | async-done | bytes 8388624 | tf_op jit(solution)/shard_map/all_gather | solution.py:79
  542.1 10.2 %convolution_convert_fusion = bf16[4096,512]{1,0:T(8,128)(2,1)} fusion(bf16[1024,4096]{1,0:T(8,128)(2,1)} %all-gather.12.cloned.1.call-done, bf16[1024,512]{1,0:T(8,128)(2,1)} %multiply_convert_fusion.1), kind=kOutput, calls=%fused_computation.8 | convolution fusion | flops 4297064448 | bytes 13631488 | tf_op jit(solution)/shard_map/dot_general | solution.py:81
  552.3 0.0 reduce-scatter.8.cloned.1.call-update
  552.3 0.0 all-gather.14.cloned.1.call-start
  552.3 51.2 %reduce-scatter.8.cloned.1.call-done = bf16[1024,512]{1,0:T(8,128)(2,1)} async-done(((bf16[4096,512]{1,0:T(8,128)(2,1)}), bf16[1024,512]{1,0:T(8,128)(2,1)}) %reduce-scatter.8.cloned.1.call-update) | async-done | bytes 1048592 | tf_op jit(solution)/shard_map/reduce_scatter | solution.py:80
  603.5 0.0 all-gather.14.cloned.1.call-update
  603.6 54.4 %all-gather.14.cloned.1.call-done = bf16[4096,512]{1,0:T(8,128)(2,1)} async-done(((bf16[1024,512]{1,0:T(8,128)(2,1)}), bf16[4096,512]{1,0:T(8,128)(2,1)}) %all-gather.14.cloned.1.call-update) | async-done | bytes 4194320 | tf_op jit(solution)/shard_map/all_gather | solution.py:72
  658.0 10.1 %multiply_convert_fusion = bf16[1024,512]{1,0:T(8,128)(2,1)} fusion(bf16[1024,512]{1,0:T(8,128)(2,1)S(1)} %copy-done.2, bf16[1024,4096]{1,0:T(8,128)(2,1)} %all-gather.12.cloned.1.call-done, bf16[4096,512]{1,0:T(8,128)(2,1)} %all-gather.14.cloned.1.call-done), kind=kOutput, calls=%fused_computation.11 | convolution fusion | flops 4298113024 | bytes 14680064 | tf_op jit(solution)/shard_map/dot_general | solution.py:70
  (15 shorter events, 0.0 us)
Async XLA Ops:
  7.2 87.7 %reduce-scatter.4.cloned.1.call-start = ((), (), s32[]{:S(2)}) async-start(), calls=%async_computation.3 | async-start | bytes 5242880 | tf_op jit(solution)/shard_map/reduce_scatter | solution.py:37
  15.1 1.0 copy-start.3
  15.1 1.3 copy-start.4
  15.1 177.7 %all-reduce.3.cloned.1.call-start = ((), (), s32[]{:S(2)}) async-start(), calls=%async_computation.11 | async-start | bytes 2228224 | tf_op jit(solution)/shard_map/psum | solution.py:51
  28.7 15.7 %collective-permute-start = (bf16[256,1056]{0,1:T(8,128)(2,1)S(1)}, bf16[256,1056]{0,1:T(8,128)(2,1)S(1)}, u32[]{:S(2)}, u32[]{:S(2)}) collective-permute-start(bf16[256,1056]{0,1:T(8,128)(2,1)S(1)} %get-tuple-element.15), channel_id=1, source_target_pairs={{0,4},{4,8},{8,12},{12,16},{16,20},{20,24},{24,28},{28,0},{1,5},{5... | collective-permute-start | bytes 1622024 | tf_op jit(solution)/shard_map/ppermute | solution.py:32
  28.7 19.0 %collective-permute-start.1 = (bf16[256,1056]{0,1:T(8,128)(2,1)S(1)}, bf16[256,1056]{0,1:T(8,128)(2,1)S(1)}, u32[]{:S(2)}, u32[]{:S(2)}) collective-permute-start(bf16[256,1056]{0,1:T(8,128)(2,1)S(1)} %get-tuple-element.16), channel_id=1, source_target_pairs={{0,8},{4,12},{8,16},{12,20},{16,24},{20,28},{24,0},{28,4},{1,9},{5... | collective-permute-start | bytes 1622024 | tf_op jit(solution)/shard_map/ppermute | solution.py:32
  30.4 60.9 %collective-permute-start.2 = (bf16[256,1056]{0,1:T(8,128)(2,1)S(1)}, bf16[256,1056]{0,1:T(8,128)(2,1)S(1)}, u32[]{:S(2)}, u32[]{:S(2)}) collective-permute-start(bf16[256,1056]{0,1:T(8,128)(2,1)S(1)} %get-tuple-element.17), channel_id=1, source_target_pairs={{0,12},{4,16},{8,20},{12,24},{16,28},{20,0},{24,4},{28,8},{1,13},{... | collective-permute-start | bytes 1622024 | tf_op jit(solution)/shard_map/ppermute | solution.py:32
  33.4 58.8 %collective-permute-start.3 = (bf16[256,1056]{0,1:T(8,128)(2,1)S(1)}, bf16[256,1056]{0,1:T(8,128)(2,1)S(1)}, u32[]{:S(2)}, u32[]{:S(2)}) collective-permute-start(bf16[256,1056]{0,1:T(8,128)(2,1)S(1)} %get-tuple-element.18), channel_id=1, source_target_pairs={{0,16},{4,20},{8,24},{12,28},{16,0},{20,4},{24,8},{28,12},{1,17},{... | collective-permute-start | bytes 1622024 | tf_op jit(solution)/shard_map/ppermute | solution.py:32
  34.2 58.8 %collective-permute-start.4 = (bf16[256,1056]{0,1:T(8,128)(2,1)S(1)}, bf16[256,1056]{0,1:T(8,128)(2,1)S(1)}, u32[]{:S(2)}, u32[]{:S(2)}) collective-permute-start(bf16[256,1056]{0,1:T(8,128)(2,1)S(1)} %get-tuple-element.19), channel_id=1, source_target_pairs={{0,20},{4,24},{8,28},{12,0},{16,4},{20,8},{24,12},{28,16},{1,21},{... | collective-permute-start | bytes 1622024 | tf_op jit(solution)/shard_map/ppermute | solution.py:32
  44.3 49.6 %collective-permute-start.5 = (bf16[256,1056]{0,1:T(8,128)(2,1)S(1)}, bf16[256,1056]{0,1:T(8,128)(2,1)S(1)}, u32[]{:S(2)}, u32[]{:S(2)}) collective-permute-start(bf16[256,1056]{0,1:T(8,128)(2,1)S(1)} %get-tuple-element.20), channel_id=1, source_target_pairs={{0,24},{4,28},{8,0},{12,4},{16,8},{20,12},{24,16},{28,20},{1,25},{... | collective-permute-start | bytes 1622024 | tf_op jit(solution)/shard_map/ppermute | solution.py:32
  47.7 53.6 %collective-permute-start.6 = (bf16[256,1056]{0,1:T(8,128)(2,1)S(1)}, bf16[256,1056]{0,1:T(8,128)(2,1)S(1)}, u32[]{:S(2)}, u32[]{:S(2)}) collective-permute-start(bf16[256,1056]{0,1:T(8,128)(2,1)S(1)} %get-tuple-element.14), channel_id=1, source_target_pairs={{0,28},{4,0},{8,4},{12,8},{16,12},{20,16},{24,20},{28,24},{1,29},{... | collective-permute-start | bytes 1622024 | tf_op jit(solution)/shard_map/ppermute | solution.py:32
  101.2 129.4 %all-gather.6.cloned.1.call-start = ((), (), s32[]{:S(2)}) async-start(), calls=%async_computation.4 | async-start | bytes 2621440 | tf_op jit(solution)/shard_map/all_gather | solution.py:57
  196.3 137.0 %all-gather.8.cloned.1.call-start = ((), (), s32[]{:S(2)}) async-start(), calls=%async_computation.5 | async-start | bytes 9437184 | tf_op jit(solution)/shard_map/all_gather | solution.py:79
  231.6 16.1 %copy-start = (bf16[2048,1024]{0,1:T(8,128)(2,1)S(1)}, bf16[2048,1024]{0,1:T(8,128)(2,1)}, u32[]{:S(2)}) copy-start(bf16[2048,1024]{0,1:T(8,128)(2,1)} %slice.8) | copy-start | bytes 12582916
  251.0 143.6 %reduce-scatter.6.cloned.1.call-start = ((), (), s32[]{:S(2)}) async-start(), calls=%async_computation.6 | async-start | bytes 5242880 | tf_op jit(solution)/shard_map/reduce_scatter | solution.py:80
  343.4 106.4 %copy-start.1 = (bf16[1024,512]{1,0:T(8,128)(2,1)S(1)}, bf16[1024,512]{1,0:T(8,128)(2,1)}, u32[]{:S(2)}) copy-start(bf16[1024,512]{1,0:T(8,128)(2,1)} %convolution_convert_fusion.2) | copy-start | bytes 3145732
  343.4 106.4 %all-gather.10.cloned.1.call-start = ((), (), s32[]{:S(2)}) async-start(), calls=%async_computation.7 | async-start | bytes 5242880 | tf_op jit(solution)/shard_map/all_gather | solution.py:72
  394.7 147.4 %all-gather.12.cloned.1.call-start = ((), (), s32[]{:S(2)}) async-start(), calls=%async_computation.8 | async-start | bytes 9437184 | tf_op jit(solution)/shard_map/all_gather | solution.py:79
  459.9 143.6 %reduce-scatter.8.cloned.1.call-start = ((), (), s32[]{:S(2)}) async-start(), calls=%async_computation.9 | async-start | bytes 5242880 | tf_op jit(solution)/shard_map/reduce_scatter | solution.py:80
  552.3 105.7 %copy-start.2 = (bf16[1024,512]{1,0:T(8,128)(2,1)S(1)}, bf16[1024,512]{1,0:T(8,128)(2,1)}, u32[]{:S(2)}) copy-start(bf16[1024,512]{1,0:T(8,128)(2,1)} %multiply_convert_fusion.1) | copy-start | bytes 3145732
  552.3 105.7 %all-gather.14.cloned.1.call-start = ((), (), s32[]{:S(2)}) async-start(), calls=%async_computation.10 | async-start | bytes 5242880 | tf_op jit(solution)/shard_map/all_gather | solution.py:72
Sparse Core Ops, SparseCore 0:
  15.3 55.9 reduce-scatter.3
  101.4 91.4 all-reduce.2
  196.4 34.1 all-gather.5
  251.2 82.0 all-gather.7
  343.5 51.0 reduce-scatter.5
  396.4 53.3 all-gather.9
  460.0 82.0 all-gather.11
  552.4 51.0 reduce-scatter.7
  605.4 52.5 all-gather.13

commit v7 on v6

--- a/solution.py
+++ b/solution.py
@@ -54,8 +54,11 @@
     )
     book = total_sums / jnp.maximum(total_counts, 1.0)[:, None, :]
     codebook = book.reshape(block_dims, K)
-    codebook_batch = lax.all_gather(book.astype(jnp.bfloat16), "rot", axis=0, tiled=True)
-    tile_book = lax.dynamic_slice_in_dim(codebook_batch, dp_index * tile_spaces, tile_spaces, 0)
+    blocks_per_rot = local_spaces // tile_spaces
+    offered = lax.dynamic_slice_in_dim(
+        book.astype(jnp.bfloat16), (dp_index % blocks_per_rot) * tile_spaces, tile_spaces, 0
+    )
+    tile_book = lax.all_gather(offered, "rot", axis=0)[dp_index // blocks_per_rot]
 
     tile_indicator = (tile_codes.T[:, :, None] == code_ids[None, None, :]).astype(jnp.bfloat16)
     rebuilt_t = jnp.einsum(

time: 675 us -> 669 us (level)
  waiting for transfers between devices: 489 us -> 478 us
  local copies, waits for them, and re-layouts: 13 us -> 20.1 us
    all_gather x1, waiting for transfers between devices: 34.3 us -> 25.6 us  [body(): lax.all_gather(offered, 'rot', axis=0)[dp_index // blocks_per_rot]]
  transfers between devices with their start and end apart: 16 -> 16, of which waited for: 10 -> 10; matrix products, arithmetic and copies ran while one was open for 4% -> 5% of each run, Pallas kernels for 0% -> 0%
where the time goes in v7:
time: 669 us; the launch traced here: 668 us
  waiting for transfers between devices  478 us (71%)
  matrix products  73 us (11%)
  blocking collectives  51.3 us (8%)
  local copies, waits for them, and re-layouts  20.1 us (3%)
  starting transfers between devices  19.4 us (3%)
  between operations  14.8 us (2%)
  other arithmetic  11.8 us (2%)
    all_gather x2, waiting for transfers between devices, body(): rows_b = lax.all_gather(columns, 'dp', axis=1, tiled=True)  164 us
    reduce_scatter x2, waiting for transfers between devices, body(): lax.psum_scatter(lax.dot_general(rows_b, columns, (((0,), (0,)), ((), ())...  102 us
    psum x1, waiting for transfers between devices, body(): total_sums, total_counts = lax.psum((shard_code_sums, local_counts), 'dp')  82.8 us
    all_gather x2, waiting for transfers between devices, apply_gram(): lax.all_gather(gram_b, 'rot', axis=0, tiled=True)  66 us
    psum x1, blocking collectives, body(): total = lax.psum(jnp.sum(gram_f * gram_f), ('dp', 'rot'))  40.3 us
    ppermute x7, waiting for transfers between devices, body(): lax.ppermute(tile_part((dp_index + shift) % dp_size), 'dp', pairs)  37.1 us
    all_gather x1, waiting for transfers between devices, body(): lax.all_gather(offered, 'rot', axis=0)[dp_index // blocks_per_rot]  25.6 us
    dot_general x2, matrix products, body(): lax.dot_general(rows_b, columns, (((0,), (0,)), ((), ())), preferred_elem...  20.3 us
  transfers between devices with their start and end apart: 16, of which 10 were waited for; matrix products, arithmetic and copies ran while one was open for 5% of the time, Pallas kernels for 0%

profile of v7, /device:TPU:0, one launch (start us, length us, event | category | flops | bytes accessed | tf_op | source)
XLA Modules:
  0.0 668.3 jit_solution(17642110602501884151)
XLA Ops:
  7.2 0.0 reduce-scatter.4.cloned.1.call-start
  7.2 7.9 %fusion.9 = f32[4096,256]{1,0:T(8,128)} fusion(bf16[1024,4096]{1,0:T(8,128)(2,1)} %param.4, bf16[256,1024]{1,0:T(8,128)(2,1)} %param.3), kind=kOutput, calls=%fused_computation.45 | convolution fusion | flops 2147483648 | bytes 13107200 | tf_op jit(solution)/shard_map/dot_general | solution.py:38
  15.1 0.0 reduce-scatter.4.cloned.1.call-update
  15.1 0.0 all-reduce.3.cloned.1.call-start
  15.3 0.9 copy-done.4
  16.2 0.2 copy.14
  16.4 11.0 %all_gather.21 = s32[256,256]{0,1:T(8,128)S(1)} all-gather(s32[256,64]{0,1:T(8,128)S(1)} %copy-done.5), channel_id=1, replica_groups=mesh['dp'=8,'rot'=4] {'rot'}, dimensions={1}, use_global_device_ids=true | all-gather | bytes 327680 | tf_op jit(solution)/shard_map/all_gather | solution.py:23
  27.5 1.5 pad_maximum_fusion.6
  29.0 1.8 collective-permute-start.1
  30.7 3.0 collective-permute-start.2
  33.7 0.9 collective-permute-start.3
  34.6 1.5 collective-permute-start.4
  36.1 3.4 convert_reduce_fusion
  39.5 5.5 collective-permute-done
  45.0 2.5 collective-permute-start.5
  47.4 1.9 constant_dynamic-update-slice_fusion.6
  49.4 9.1 %collective-permute-start.6 = (bf16[256,1056]{0,1:T(8,128)(2,1)S(1)}, bf16[256,1056]{0,1:T(8,128)(2,1)}, u32[]{:S(2)}, u32[]{:S(2)}) collective-permute-start(bf16[256,1056]{0,1:T(8,128)(2,1)S(1)} %get-tuple-element.12), channel_id=1, source_target_pairs={{0,28},{4,0},{8,4},{12,8},{16,12},{20,16},{24,20},{28,24},{1,29},{... | collective-permute-start | bytes 1622024 | tf_op jit(solution)/shard_map/ppermute | solution.py:32
  58.5 1.9 constant_dynamic-update-slice_fusion.5
  60.4 31.6 %collective-permute-done.2 = bf16[256,1056]{0,1:T(8,128)(2,1)} collective-permute-done((bf16[256,1056]{0,1:T(8,128)(2,1)S(1)}, bf16[256,1056]{0,1:T(8,128)(2,1)}, u32[]{:S(2)}, u32[]{:S(2)}) %collective-permute-start.2) | collective-permute-done | bytes 540704 | tf_op jit(solution)/shard_map/ppermute | solution.py:32
  92.0 1.9 constant_dynamic-update-slice_fusion.4
  93.9 1.9 constant_dynamic-update-slice_fusion.3
  95.8 1.9 constant_dynamic-update-slice_fusion.2
  97.7 0.9 constant_dynamic-update-slice_fusion.1
  98.6 1.3 convert_element_type.67
  99.9 5.1 fusion.3
  105.0 0.0 all-reduce.3.cloned.1.call-update
  105.0 0.0 all-gather.15.cloned.1.call-start
  105.1 1.9 constant_dynamic-update-slice_fusion
  107.0 4.8 slice.8
  111.8 0.9 slice_convert_fusion
  112.7 82.8 %all-reduce.3.cloned.1.call-done = (f32[64,16,256]{2,1,0:T(8,128)}, f32[64,256]{1,0:T(8,128)}) async-done(((f32[64,16,256]{2,1,0:T(8,128)}, f32[64,256]{1,0:T(8,128)}), (f32[64,16,256]{2,1,0:T(8,128)}, f32[64,256]{1,0:T(8,128)})) %all-reduce.3.cloned.1.call-update) | async-done | bytes 1114128 | tf_op jit(solution)/shard_map/psum | solution.py:51
  195.6 0.8 broadcast_maximum_fusion
  196.4 1.3 broadcast_divide_fusion
  197.8 0.0 copy-start.1
  197.8 0.8 dynamic-slice_convert_fusion
  198.6 0.0 all-gather.15.cloned.1.call-update
  198.6 0.0 all-gather.7.cloned.1.call-start
  198.7 25.6 %all-gather.15.cloned.1.call-done = bf16[128,16,256]{2,1,0:T(8,128)(2,1)} async-done(((bf16[32,16,256]{2,1,0:T(8,128)(2,1)}), bf16[128,16,256]{2,1,0:T(8,128)(2,1)}) %all-gather.15.cloned.1.call-update) | async-done | bytes 1048592 | tf_op jit(solution)/shard_map/all_gather | solution.py:61
  224.3 1.0 fusion.26
  225.3 16.1 %fusion.5 = bf16[32,16,2048]{2,1,0:T(8,128)(2,1)S(1)} fusion(s32[32,2048]{1,0:T(8,128)S(1)} %bitcast.31, bf16[32,16,256]{2,1,0:T(8,128)(2,1)S(1)} %fusion.26), kind=kOutput, calls=%fused_computation.10 | convolution fusion | flops 554696704 | bytes 2621440 | tf_op jit(solution)/shard_map/lyg,lxg->lyx/dot_general | solution.py:64
  241.4 3.3 convolution_convert_fusion.2
  244.7 0.0 all-gather.7.cloned.1.call-update
  244.7 0.2 reduce-scatter.6.cloned.1.call-start
  245.0 82.0 %all-gather.7.cloned.1.call-done = bf16[1024,4096]{1,0:T(8,128)(2,1)} async-done(((bf16[1024,512]{1,0:T(8,128)(2,1)}), bf16[1024,4096]{1,0:T(8,128)(2,1)}) %all-gather.7.cloned.1.call-update) | async-done | bytes 8388624 | tf_op jit(solution)/shard_map/all_gather | solution.py:82
  326.9 10.2 %convolution_convert_fusion.1 = bf16[4096,512]{1,0:T(8,128)(2,1)} fusion(bf16[1024,4096]{1,0:T(8,128)(2,1)} %all-gather.7.cloned.1.call-done, bf16[1024,512]{1,0:T(8,128)(2,1)} %convolution_convert_fusion.2), kind=kOutput, calls=%fused_computation.9 | convolution fusion | flops 4297064448 | bytes 13631488 | tf_op jit(solution)/shard_map/dot_general | solution.py:84
  337.1 0.0 reduce-scatter.6.cloned.1.call-update
  337.1 0.0 all-gather.9.cloned.1.call-start
  337.1 51.2 %reduce-scatter.6.cloned.1.call-done = bf16[1024,512]{1,0:T(8,128)(2,1)} async-done(((bf16[4096,512]{1,0:T(8,128)(2,1)}), bf16[1024,512]{1,0:T(8,128)(2,1)}) %reduce-scatter.6.cloned.1.call-update) | async-done | bytes 1048592 | tf_op jit(solution)/shard_map/reduce_scatter | solution.py:83
  388.3 0.0 all-gather.9.cloned.1.call-update
  388.4 0.0 all-gather.11.cloned.1.call-start
  388.4 2.4 multiply_reduce_fusion
  390.9 40.3 %psum.23 = f32[]{:T(128)} all-reduce(f32[]{:T(128)} %multiply_reduce_fusion), channel_id=1, replica_groups=mesh['dp'=8,'rot'=4] {'dp','rot'}, use_global_device_ids=true, to_apply=%region_6.7 | all-reduce | flops 1 | bytes 8 | tf_op jit(solution)/shard_map/psum | solution.py:96
  431.9 11.6 %all-gather.9.cloned.1.call-done = bf16[4096,512]{1,0:T(8,128)(2,1)} async-done(((bf16[1024,512]{1,0:T(8,128)(2,1)}), bf16[4096,512]{1,0:T(8,128)(2,1)}) %all-gather.9.cloned.1.call-update) | async-done | bytes 4194320 | tf_op jit(solution)/shard_map/all_gather | solution.py:75
  443.4 10.1 %multiply_convert_fusion.1 = bf16[1024,512]{1,0:T(8,128)(2,1)} fusion(bf16[1024,512]{1,0:T(8,128)(2,1)S(1)} %copy-done.2, bf16[1024,4096]{1,0:T(8,128)(2,1)} %all-gather.7.cloned.1.call-done, bf16[4096,512]{1,0:T(8,128)(2,1)} %all-gather.9.cloned.1.call-done, f32[]{:T(128)S(6)} %mul.79, f32[]{:T(128)S(6)} %div.24), kind=kOutput, calls=%fused_computation.12 | convolution fusion | flops 4298113024 | bytes 14680072 | tf_op jit(solution)/shard_map/dot_general | solution.py:73
  453.5 0.0 all-gather.11.cloned.1.call-update
  453.6 0.3 reduce-scatter.8.cloned.1.call-start
  453.8 81.9 %all-gather.11.cloned.1.call-done = bf16[1024,4096]{1,0:T(8,128)(2,1)} async-done(((bf16[1024,512]{1,0:T(8,128)(2,1)}), bf16[1024,4096]{1,0:T(8,128)(2,1)}) %all-gather.11.cloned.1.call-update) | async-done | bytes 8388624 | tf_op jit(solution)/shard_map/all_gather | solution.py:82
  535.8 10.2 %convolution_convert_fusion = bf16[4096,512]{1,0:T(8,128)(2,1)} fusion(bf16[1024,4096]{1,0:T(8,128)(2,1)} %all-gather.11.cloned.1.call-done, bf16[1024,512]{1,0:T(8,128)(2,1)} %multiply_convert_fusion.1), kind=kOutput, calls=%fused_computation.8 | convolution fusion | flops 4297064448 | bytes 13631488 | tf_op jit(solution)/shard_map/dot_general | solution.py:84
  545.9 0.0 reduce-scatter.8.cloned.1.call-update
  545.9 0.0 all-gather.13.cloned.1.call-start
  546.0 51.2 %reduce-scatter.8.cloned.1.call-done = bf16[1024,512]{1,0:T(8,128)(2,1)} async-done(((bf16[4096,512]{1,0:T(8,128)(2,1)}), bf16[1024,512]{1,0:T(8,128)(2,1)}) %reduce-scatter.8.cloned.1.call-update) | async-done | bytes 1048592 | tf_op jit(solution)/shard_map/reduce_scatter | solution.py:83
  597.2 0.0 all-gather.13.cloned.1.call-update
  597.2 54.4 %all-gather.13.cloned.1.call-done = bf16[4096,512]{1,0:T(8,128)(2,1)} async-done(((bf16[1024,512]{1,0:T(8,128)(2,1)}), bf16[4096,512]{1,0:T(8,128)(2,1)}) %all-gather.13.cloned.1.call-update) | async-done | bytes 4194320 | tf_op jit(solution)/shard_map/all_gather | solution.py:75
  651.7 10.1 %multiply_convert_fusion = bf16[1024,512]{1,0:T(8,128)(2,1)} fusion(bf16[1024,512]{1,0:T(8,128)(2,1)S(1)} %copy-done.3, bf16[1024,4096]{1,0:T(8,128)(2,1)} %all-gather.11.cloned.1.call-done, bf16[4096,512]{1,0:T(8,128)(2,1)} %all-gather.13.cloned.1.call-done), kind=kOutput, calls=%fused_computation.11 | convolution fusion | flops 4298113024 | bytes 14680064 | tf_op jit(solution)/shard_map/dot_general | solution.py:73
  (18 shorter events, 0.1 us)
Async XLA Ops:
  7.2 91.5 %reduce-scatter.4.cloned.1.call-start = ((), (), s32[]{:S(2)}) async-start(), calls=%async_computation.3 | async-start | bytes 5242880 | tf_op jit(solution)/shard_map/reduce_scatter | solution.py:37
  15.1 1.0 copy-start.4
  15.1 1.3 copy-start.5
  15.1 180.4 %all-reduce.3.cloned.1.call-start = ((), (), s32[]{:S(2)}) async-start(), calls=%async_computation.11 | async-start | bytes 2228224 | tf_op jit(solution)/shard_map/psum | solution.py:51
  29.0 16.0 %collective-permute-start = (bf16[256,1056]{0,1:T(8,128)(2,1)}, bf16[256,1056]{0,1:T(8,128)(2,1)}, u32[]{:S(2)}, u32[]{:S(2)}) collective-permute-start(bf16[256,1056]{0,1:T(8,128)(2,1)} %get-tuple-element.13), channel_id=1, source_target_pairs={{0,4},{4,8},{8,12},{12,16},{16,20},{20,24},{24,28},{28,0},{1,5},{5... | collective-permute-start | bytes 1622024 | tf_op jit(solution)/shard_map/ppermute | solution.py:32
  29.0 20.4 %collective-permute-start.1 = (bf16[256,1056]{0,1:T(8,128)(2,1)}, bf16[256,1056]{0,1:T(8,128)(2,1)}, u32[]{:S(2)}, u32[]{:S(2)}) collective-permute-start(bf16[256,1056]{0,1:T(8,128)(2,1)} %get-tuple-element.14), channel_id=1, source_target_pairs={{0,8},{4,12},{8,16},{12,20},{16,24},{20,28},{24,0},{28,4},{1,9},{5... | collective-permute-start | bytes 1622024 | tf_op jit(solution)/shard_map/ppermute | solution.py:32
  30.7 61.2 %collective-permute-start.2 = (bf16[256,1056]{0,1:T(8,128)(2,1)S(1)}, bf16[256,1056]{0,1:T(8,128)(2,1)}, u32[]{:S(2)}, u32[]{:S(2)}) collective-permute-start(bf16[256,1056]{0,1:T(8,128)(2,1)S(1)} %get-tuple-element.15), channel_id=1, source_target_pairs={{0,12},{4,16},{8,20},{12,24},{16,28},{20,0},{24,4},{28,8},{1,13},{... | collective-permute-start | bytes 1622024 | tf_op jit(solution)/shard_map/ppermute | solution.py:32
  33.7 60.2 %collective-permute-start.3 = (bf16[256,1056]{0,1:T(8,128)(2,1)S(1)}, bf16[256,1056]{0,1:T(8,128)(2,1)}, u32[]{:S(2)}, u32[]{:S(2)}) collective-permute-start(bf16[256,1056]{0,1:T(8,128)(2,1)S(1)} %get-tuple-element.16), channel_id=1, source_target_pairs={{0,16},{4,20},{8,24},{12,28},{16,0},{20,4},{24,8},{28,12},{1,17},{... | collective-permute-start | bytes 1622024 | tf_op jit(solution)/shard_map/ppermute | solution.py:32
  34.6 61.3 %collective-permute-start.4 = (bf16[256,1056]{0,1:T(8,128)(2,1)S(1)}, bf16[256,1056]{0,1:T(8,128)(2,1)}, u32[]{:S(2)}, u32[]{:S(2)}) collective-permute-start(bf16[256,1056]{0,1:T(8,128)(2,1)S(1)} %get-tuple-element.17), channel_id=1, source_target_pairs={{0,20},{4,24},{8,28},{12,0},{16,4},{20,8},{24,12},{28,16},{1,21},{... | collective-permute-start | bytes 1622024 | tf_op jit(solution)/shard_map/ppermute | solution.py:32
  45.0 52.8 %collective-permute-start.5 = (bf16[256,1056]{0,1:T(8,128)(2,1)S(1)}, bf16[256,1056]{0,1:T(8,128)(2,1)S(1)}, u32[]{:S(2)}, u32[]{:S(2)}) collective-permute-start(bf16[256,1056]{0,1:T(8,128)(2,1)S(1)} %get-tuple-element.18), channel_id=1, source_target_pairs={{0,24},{4,28},{8,0},{12,4},{16,8},{20,12},{24,16},{28,20},{1,25},{... | collective-permute-start | bytes 1622024 | tf_op jit(solution)/shard_map/ppermute | solution.py:32
  49.4 55.7 %collective-permute-start.6 = (bf16[256,1056]{0,1:T(8,128)(2,1)S(1)}, bf16[256,1056]{0,1:T(8,128)(2,1)}, u32[]{:S(2)}, u32[]{:S(2)}) collective-permute-start(bf16[256,1056]{0,1:T(8,128)(2,1)S(1)} %get-tuple-element.12), channel_id=1, source_target_pairs={{0,28},{4,0},{8,4},{12,8},{16,12},{20,16},{24,20},{28,24},{1,29},{... | collective-permute-start | bytes 1622024 | tf_op jit(solution)/shard_map/ppermute | solution.py:32
  105.0 119.2 %all-gather.15.cloned.1.call-start = ((), (), s32[]{:S(2)}) async-start(), calls=%async_computation.10 | async-start | bytes 1310720 | tf_op jit(solution)/shard_map/all_gather | solution.py:61
  197.8 43.6 %copy-start.1 = (f32[64,16,256]{2,1,0:T(8,128)}, f32[64,16,256]{2,1,0:T(8,128)S(1)}, u32[]{:S(2)}) copy-start(f32[64,16,256]{2,1,0:T(8,128)S(1)} %broadcast_divide_fusion) | copy-start | bytes 3145732
  198.6 128.3 %all-gather.7.cloned.1.call-start = ((), (), s32[]{:S(2)}) async-start(), calls=%async_computation.4 | async-start | bytes 9437184 | tf_op jit(solution)/shard_map/all_gather | solution.py:82
  225.2 16.1 %copy-start = (bf16[2048,1024]{0,1:T(8,128)(2,1)S(1)}, bf16[2048,1024]{0,1:T(8,128)(2,1)}, u32[]{:S(2)}) copy-start(bf16[2048,1024]{0,1:T(8,128)(2,1)} %slice.8) | copy-start | bytes 12582916
  244.7 143.6 %reduce-scatter.6.cloned.1.call-start = ((), (), s32[]{:S(2)}) async-start(), calls=%async_computation.5 | async-start | bytes 5242880 | tf_op jit(solution)/shard_map/reduce_scatter | solution.py:83
  337.1 106.4 %copy-start.2 = (bf16[1024,512]{1,0:T(8,128)(2,1)S(1)}, bf16[1024,512]{1,0:T(8,128)(2,1)}, u32[]{:S(2)}) copy-start(bf16[1024,512]{1,0:T(8,128)(2,1)} %convolution_convert_fusion.2) | copy-start | bytes 3145732
  337.1 106.3 %all-gather.9.cloned.1.call-start = ((), (), s32[]{:S(2)}) async-start(), calls=%async_computation.6 | async-start | bytes 5242880 | tf_op jit(solution)/shard_map/all_gather | solution.py:75
  388.4 147.4 %all-gather.11.cloned.1.call-start = ((), (), s32[]{:S(2)}) async-start(), calls=%async_computation.7 | async-start | bytes 9437184 | tf_op jit(solution)/shard_map/all_gather | solution.py:82
  453.6 143.6 %reduce-scatter.8.cloned.1.call-start = ((), (), s32[]{:S(2)}) async-start(), calls=%async_computation.8 | async-start | bytes 5242880 | tf_op jit(solution)/shard_map/reduce_scatter | solution.py:83
  545.9 105.7 %copy-start.3 = (bf16[1024,512]{1,0:T(8,128)(2,1)S(1)}, bf16[1024,512]{1,0:T(8,128)(2,1)}, u32[]{:S(2)}) copy-start(bf16[1024,512]{1,0:T(8,128)(2,1)} %multiply_convert_fusion.1) | copy-start | bytes 3145732
  545.9 105.7 %all-gather.13.cloned.1.call-start = ((), (), s32[]{:S(2)}) async-start(), calls=%async_computation.9 | async-start | bytes 5242880 | tf_op jit(solution)/shard_map/all_gather | solution.py:75
Sparse Core Ops, SparseCore 0:
  15.3 55.9 reduce-scatter.3
  105.2 90.3 all-reduce.2
  198.7 25.4 all-gather.14
  244.8 82.0 all-gather.6
  337.2 51.0 reduce-scatter.5
  390.0 53.3 all-gather.8
  453.7 82.0 all-gather.10
  546.1 51.0 reduce-scatter.7
  599.0 52.5 all-gather.12

commit v8 on v7

--- a/solution.py
+++ b/solution.py
@@ -78,8 +78,16 @@
 
     columns = cross_tile
     new_tile = None
+    def row_panel(tile):
+        if dp_size % 2:
+            return lax.all_gather(tile, "dp", axis=1, tiled=True)
+        groups = [list(range(parity, dp_size, 2)) for parity in range(2)]
+        own = lax.all_gather(tile, "dp", axis=1, tiled=True, axis_index_groups=groups)
+        mates = [(i, i ^ 1) for i in range(dp_size)]
+        return jnp.concatenate([own, lax.ppermute(own, "dp", mates)], axis=1)
+
     for iteration in range(ITERS):
-        rows_b = lax.all_gather(columns, "dp", axis=1, tiled=True)
+        rows_b = row_panel(columns)
         gram_part = lax.psum_scatter(
             lax.dot_general(
                 rows_b,

time: 669 us -> 679 us (1.015)
  waiting for transfers between devices: 478 us -> 490 us
  local copies, waits for them, and re-layouts: 20.1 us -> 31.7 us
  matrix products: 73 us -> 65.2 us
    ppermute x7, waiting for transfers between devices: 37.1 us -> 52.4 us  [body(): lax.ppermute(tile_part((dp_index + shift) % dp_size), 'dp', pairs)]
    psum x1, waiting for transfers between devices: 82.8 us -> 71.8 us  [body(): total_sums, total_counts = lax.psum((shard_code_sums, local_counts), 'dp')]
    unnamed x19 -> x25, local copies, waits for them, and re-layouts: 11.6 us -> 22.1 us
    ppermute x0 -> x2, waiting for transfers between devices: none -> 9.71 us  [row_panel(): return jnp.concatenate([own, lax.ppermute(own, 'dp', mates)], axis=1)]
    dot_general x2, matrix products: 20.3 us -> 12.6 us  [body(): lax.dot_general(rows_b, columns, (((0,), (0,)), ((), ())), preferred_elem...]
  transfers between devices with their start and end apart: 16 -> 18, of which waited for: 10 -> 14; matrix products, arithmetic and copies ran while one was open for 5% -> 5% of each run, Pallas kernels for 0% -> 0%
where the time goes in v8:
time: 679 us; the launch traced here: 678 us
  waiting for transfers between devices  490 us (72%)
  matrix products  65.2 us (10%)
  blocking collectives  51.3 us (8%)
  local copies, waits for them, and re-layouts  31.7 us (5%)
  between operations  14.9 us (2%)
  starting transfers between devices  13.5 us (2%)
  other arithmetic  11.7 us (2%)
    all_gather x2, waiting for transfers between devices, row_panel(): lax.all_gather(tile, 'dp', axis=1, tiled=True, axis_index_groups=groups)  162 us
    reduce_scatter x2, waiting for transfers between devices, body(): lax.psum_scatter(lax.dot_general(rows_b, columns, (((0,), (0,)), ((), ())...  102 us
    psum x1, waiting for transfers between devices, body(): total_sums, total_counts = lax.psum((shard_code_sums, local_counts), 'dp')  71.8 us
    all_gather x2, waiting for transfers between devices, apply_gram(): lax.all_gather(gram_b, 'rot', axis=0, tiled=True)  65.9 us
    ppermute x7, waiting for transfers between devices, body(): lax.ppermute(tile_part((dp_index + shift) % dp_size), 'dp', pairs)  52.4 us
    psum x1, blocking collectives, body(): total = lax.psum(jnp.sum(gram_f * gram_f), ('dp', 'rot'))  40.3 us
    all_gather x1, waiting for transfers between devices, body(): lax.all_gather(offered, 'rot', axis=0)[dp_index // blocks_per_rot]  25.6 us
    unnamed x25, local copies, waits for them, and re-layouts  22.1 us
  transfers between devices with their start and end apart: 18, of which 14 were waited for; matrix products, arithmetic and copies ran while one was open for 5% of the time, Pallas kernels for 0%

profile of v8, /device:TPU:0, one launch (start us, length us, event | category | flops | bytes accessed | tf_op | source)
XLA Modules:
  0.0 677.9 jit_solution(14149681000548639991)
XLA Ops:
  7.2 0.0 reduce-scatter.4.cloned.1.call-start
  7.2 7.9 %fusion.9 = f32[4096,256]{1,0:T(8,128)} fusion(bf16[1024,4096]{1,0:T(8,128)(2,1)} %param.4, bf16[256,1024]{1,0:T(8,128)(2,1)} %param.3), kind=kOutput, calls=%fused_computation.49 | convolution fusion | flops 2147483648 | bytes 13107200 | tf_op jit(solution)/shard_map/dot_general | solution.py:38
  15.1 0.0 reduce-scatter.4.cloned.1.call-update
  15.1 0.0 all-reduce.3.cloned.1.call-start
  15.3 0.9 copy-done.6
  16.2 0.2 copy.14
  16.4 11.0 %all_gather.21 = s32[256,256]{0,1:T(8,128)S(1)} all-gather(s32[256,64]{0,1:T(8,128)S(1)} %copy-done.7), channel_id=1, replica_groups=mesh['dp'=8,'rot'=4] {'rot'}, dimensions={1}, use_global_device_ids=true | all-gather | bytes 327680 | tf_op jit(solution)/shard_map/all_gather | solution.py:23
  27.5 1.5 pad_maximum_fusion.6
  29.0 3.5 collective-permute-start.6
  32.5 1.2 collective-permute-start.2
  33.7 1.7 collective-permute-start.3
  35.5 3.4 convert_reduce_fusion
  38.9 4.4 collective-permute-done
  43.2 6.4 collective-permute-start.4
  49.7 1.9 constant_dynamic-update-slice_fusion.6
  51.6 8.1 %collective-permute-done.1 = bf16[256,1056]{0,1:T(8,128)(2,1)} collective-permute-done((bf16[256,1056]{0,1:T(8,128)(2,1)}, bf16[256,1056]{0,1:T(8,128)(2,1)}, u32[]{:S(2)}, u32[]{:S(2)}) %collective-permute-start.1) | collective-permute-done | bytes 540704 | tf_op jit(solution)/shard_map/ppermute | solution.py:32
  59.7 1.9 constant_dynamic-update-slice_fusion.5
  61.6 28.1 %collective-permute-done.2 = bf16[256,1056]{0,1:T(8,128)(2,1)} collective-permute-done((bf16[256,1056]{0,1:T(8,128)(2,1)S(1)}, bf16[256,1056]{0,1:T(8,128)(2,1)}, u32[]{:S(2)}, u32[]{:S(2)}) %collective-permute-start.2) | collective-permute-done | bytes 540704 | tf_op jit(solution)/shard_map/ppermute | solution.py:32
  89.8 1.9 constant_dynamic-update-slice_fusion.4
  91.7 11.8 %collective-permute-done.3 = bf16[256,1056]{0,1:T(8,128)(2,1)} collective-permute-done((bf16[256,1056]{0,1:T(8,128)(2,1)S(1)}, bf16[256,1056]{0,1:T(8,128)(2,1)}, u32[]{:S(2)}, u32[]{:S(2)}) %collective-permute-start.3) | collective-permute-done | bytes 540704 | tf_op jit(solution)/shard_map/ppermute | solution.py:32
  103.5 1.9 constant_dynamic-update-slice_fusion.3
  105.4 0.9 constant_dynamic-update-slice_fusion.2
  106.3 0.9 constant_dynamic-update-slice_fusion.1
  107.2 1.3 convert_element_type.67
  108.5 5.1 fusion.3
  113.6 0.0 all-reduce.3.cloned.1.call-update
  113.6 0.0 all-gather.15.cloned.1.call-start
  113.6 1.9 constant_dynamic-update-slice_fusion
  115.6 4.8 slice.8
  120.4 0.9 slice_convert_fusion
  121.3 71.8 %all-reduce.3.cloned.1.call-done = (f32[64,16,256]{2,1,0:T(8,128)}, f32[64,256]{1,0:T(8,128)}) async-done(((f32[64,16,256]{2,1,0:T(8,128)}, f32[64,256]{1,0:T(8,128)}), (f32[64,16,256]{2,1,0:T(8,128)}, f32[64,256]{1,0:T(8,128)})) %all-reduce.3.cloned.1.call-update) | async-done | bytes 1114128 | tf_op jit(solution)/shard_map/psum | solution.py:51
  193.1 0.8 broadcast_maximum_fusion
  193.9 1.3 broadcast_divide_fusion
  195.3 0.8 dynamic-slice_convert_fusion
  196.1 0.0 all-gather.7.cloned.1.call-start
  196.2 25.6 %all-gather.15.cloned.1.call-done = bf16[128,16,256]{2,1,0:T(8,128)(2,1)} async-done(((bf16[32,16,256]{2,1,0:T(8,128)(2,1)}), bf16[128,16,256]{2,1,0:T(8,128)(2,1)}) %all-gather.15.cloned.1.call-update) | async-done | bytes 1048592 | tf_op jit(solution)/shard_map/all_gather | solution.py:61
  221.8 1.0 fusion.26
  222.8 16.1 %fusion.5 = bf16[32,16,2048]{2,1,0:T(8,128)(2,1)S(1)} fusion(s32[32,2048]{1,0:T(8,128)S(1)} %bitcast.31, bf16[32,16,256]{2,1,0:T(8,128)(2,1)S(1)} %fusion.26), kind=kOutput, calls=%fused_computation.10 | convolution fusion | flops 554696704 | bytes 2621440 | tf_op jit(solution)/shard_map/lyg,lxg->lyx/dot_general | solution.py:64
  238.9 3.3 convolution_convert_fusion.2
  242.2 0.0 reduce-scatter.6.cloned.1.call-start
  242.3 80.8 %all-gather.7.cloned.1.call-done = bf16[1024,2048]{1,0:T(8,128)(2,1)} async-done(((bf16[1024,512]{1,0:T(8,128)(2,1)}), bf16[1024,2048]{1,0:T(8,128)(2,1)}) %all-gather.7.cloned.1.call-update) | async-done | bytes 4194320 | tf_op jit(solution)/shard_map/all_gather | solution.py:85
  323.1 2.5 constant_dynamic-update-slice_fusion.8
  325.6 4.9 collective-permute-done.7
  330.5 0.6 constant_dynamic-update-slice_fusion.7
  331.1 3.3 copy-done.1
  334.3 6.3 convolution_convert_fusion.1
  340.6 0.0 all-gather.9.cloned.1.call-start
  340.7 51.2 %reduce-scatter.6.cloned.1.call-done = bf16[1024,512]{1,0:T(8,128)(2,1)} async-done(((bf16[4096,512]{1,0:T(8,128)(2,1)}), bf16[1024,512]{1,0:T(8,128)(2,1)}) %reduce-scatter.6.cloned.1.call-update) | async-done | bytes 1048592 | tf_op jit(solution)/shard_map/reduce_scatter | solution.py:91
  391.9 0.2 all-gather.11.cloned.1.call-start
  392.1 2.4 multiply_reduce_fusion
  394.5 40.3 %psum.23 = f32[]{:T(128)} all-reduce(f32[]{:T(128)} %multiply_reduce_fusion), channel_id=1, replica_groups=mesh['dp'=8,'rot'=4] {'dp','rot'}, use_global_device_ids=true, to_apply=%region_6.7 | all-reduce | flops 1 | bytes 8 | tf_op jit(solution)/shard_map/psum | solution.py:104
  435.6 11.4 %all-gather.9.cloned.1.call-done = bf16[4096,512]{1,0:T(8,128)(2,1)} async-done(((bf16[1024,512]{1,0:T(8,128)(2,1)}), bf16[4096,512]{1,0:T(8,128)(2,1)}) %all-gather.9.cloned.1.call-update) | async-done | bytes 4194320 | tf_op jit(solution)/shard_map/all_gather | solution.py:75
  447.0 10.1 %multiply_convert_fusion.1 = bf16[1024,512]{1,0:T(8,128)(2,1)} fusion(bf16[1024,512]{1,0:T(8,128)(2,1)S(1)} %copy-done.4, bf16[1024,4096]{1,0:T(8,128)(2,1)} %copy-done.1, bf16[4096,512]{1,0:T(8,128)(2,1)} %all-gather.9.cloned.1.call-done, f32[]{:T(128)S(6)} %mul.79, f32[]{:T(128)S(6)} %div.24), kind=kOutput, calls=%fused_computation.12 | convolution fusion | flops 4298113024 | bytes 14680072 | tf_op jit(solution)/shard_map/dot_general | solution.py:73
  457.1 0.0 reduce-scatter.8.cloned.1.call-start
  457.2 80.8 %all-gather.11.cloned.1.call-done = bf16[1024,2048]{1,0:T(8,128)(2,1)} async-done(((bf16[1024,512]{1,0:T(8,128)(2,1)}), bf16[1024,2048]{1,0:T(8,128)(2,1)}) %all-gather.11.cloned.1.call-update) | async-done | bytes 4194320 | tf_op jit(solution)/shard_map/all_gather | solution.py:85
  538.0 2.5 constant_dynamic-update-slice_fusion.10
  540.5 4.9 collective-permute-done.8
  545.4 0.6 constant_dynamic-update-slice_fusion.9
  546.0 3.3 copy-done.2
  549.2 6.3 convolution_convert_fusion
  555.5 0.0 all-gather.13.cloned.1.call-start
  555.6 51.2 %reduce-scatter.8.cloned.1.call-done = bf16[1024,512]{1,0:T(8,128)(2,1)} async-done(((bf16[4096,512]{1,0:T(8,128)(2,1)}), bf16[1024,512]{1,0:T(8,128)(2,1)}) %reduce-scatter.8.cloned.1.call-update) | async-done | bytes 1048592 | tf_op jit(solution)/shard_map/reduce_scatter | solution.py:91
  606.8 54.4 %all-gather.13.cloned.1.call-done = bf16[4096,512]{1,0:T(8,128)(2,1)} async-done(((bf16[1024,512]{1,0:T(8,128)(2,1)}), bf16[4096,512]{1,0:T(8,128)(2,1)}) %all-gather.13.cloned.1.call-update) | async-done | bytes 4194320 | tf_op jit(solution)/shard_map/all_gather | solution.py:75
  661.3 10.1 %multiply_convert_fusion = bf16[1024,512]{1,0:T(8,128)(2,1)} fusion(bf16[1024,512]{1,0:T(8,128)(2,1)S(1)} %copy-done.5, bf16[1024,4096]{1,0:T(8,128)(2,1)} %copy-done.2, bf16[4096,512]{1,0:T(8,128)(2,1)} %all-gather.13.cloned.1.call-done), kind=kOutput, calls=%fused_computation.11 | convolution fusion | flops 4298113024 | bytes 14680064 | tf_op jit(solution)/shard_map/dot_general | solution.py:73
  (30 shorter events, 0.2 us)
Async XLA Ops:
  7.2 100.0 %reduce-scatter.4.cloned.1.call-start = ((), (), s32[]{:S(2)}) async-start(), calls=%async_computation.3 | async-start | bytes 5242880 | tf_op jit(solution)/shard_map/reduce_scatter | solution.py:37
  15.1 1.0 copy-start.6
  15.1 1.3 copy-start.7
  15.1 177.9 %all-reduce.3.cloned.1.call-start = ((), (), s32[]{:S(2)}) async-start(), calls=%async_computation.11 | async-start | bytes 2228224 | tf_op jit(solution)/shard_map/psum | solution.py:51
  29.0 14.2 %collective-permute-start = (bf16[256,1056]{0,1:T(8,128)(2,1)}, bf16[256,1056]{0,1:T(8,128)(2,1)}, u32[]{:S(2)}, u32[]{:S(2)}) collective-permute-start(bf16[256,1056]{0,1:T(8,128)(2,1)} %get-tuple-element.13), channel_id=1, source_target_pairs={{0,4},{4,8},{8,12},{12,16},{16,20},{20,24},{24,28},{28,0},{1,5},{5... | collective-permute-start | bytes 1622024 | tf_op jit(solution)/shard_map/ppermute | solution.py:32
  29.0 84.6 %collective-permute-start.6 = (bf16[256,1056]{0,1:T(8,128)(2,1)S(1)}, bf16[256,1056]{0,1:T(8,128)(2,1)}, u32[]{:S(2)}, u32[]{:S(2)}) collective-permute-start(bf16[256,1056]{0,1:T(8,128)(2,1)S(1)} %get-tuple-element.12), channel_id=1, source_target_pairs={{0,28},{4,0},{8,4},{12,8},{16,12},{20,16},{24,20},{28,24},{1,29},{... | collective-permute-start | bytes 1622024 | tf_op jit(solution)/shard_map/ppermute | solution.py:32
  32.5 27.2 %collective-permute-start.1 = (bf16[256,1056]{0,1:T(8,128)(2,1)}, bf16[256,1056]{0,1:T(8,128)(2,1)}, u32[]{:S(2)}, u32[]{:S(2)}) collective-permute-start(bf16[256,1056]{0,1:T(8,128)(2,1)} %get-tuple-element.14), channel_id=1, source_target_pairs={{0,8},{4,12},{8,16},{12,20},{16,24},{20,28},{24,0},{28,4},{1,9},{5... | collective-permute-start | bytes 1622024 | tf_op jit(solution)/shard_map/ppermute | solution.py:32
  32.5 57.2 %collective-permute-start.2 = (bf16[256,1056]{0,1:T(8,128)(2,1)S(1)}, bf16[256,1056]{0,1:T(8,128)(2,1)}, u32[]{:S(2)}, u32[]{:S(2)}) collective-permute-start(bf16[256,1056]{0,1:T(8,128)(2,1)S(1)} %get-tuple-element.15), channel_id=1, source_target_pairs={{0,12},{4,16},{8,20},{12,24},{16,28},{20,0},{24,4},{28,8},{1,13},{... | collective-permute-start | bytes 1622024 | tf_op jit(solution)/shard_map/ppermute | solution.py:32
  33.7 69.8 %collective-permute-start.3 = (bf16[256,1056]{0,1:T(8,128)(2,1)S(1)}, bf16[256,1056]{0,1:T(8,128)(2,1)}, u32[]{:S(2)}, u32[]{:S(2)}) collective-permute-start(bf16[256,1056]{0,1:T(8,128)(2,1)S(1)} %get-tuple-element.16), channel_id=1, source_target_pairs={{0,16},{4,20},{8,24},{12,28},{16,0},{20,4},{24,8},{28,12},{1,17},{... | collective-permute-start | bytes 1622024 | tf_op jit(solution)/shard_map/ppermute | solution.py:32
  43.2 62.2 %collective-permute-start.4 = (bf16[256,1056]{0,1:T(8,128)(2,1)S(1)}, bf16[256,1056]{0,1:T(8,128)(2,1)S(1)}, u32[]{:S(2)}, u32[]{:S(2)}) collective-permute-start(bf16[256,1056]{0,1:T(8,128)(2,1)S(1)} %get-tuple-element.17), channel_id=1, source_target_pairs={{0,20},{4,24},{8,28},{12,0},{16,4},{20,8},{24,12},{28,16},{1,21},{... | collective-permute-start | bytes 1622024 | tf_op jit(solution)/shard_map/ppermute | solution.py:32
  59.7 46.6 %collective-permute-start.5 = (bf16[256,1056]{0,1:T(8,128)(2,1)S(1)}, bf16[256,1056]{0,1:T(8,128)(2,1)S(1)}, u32[]{:S(2)}, u32[]{:S(2)}) collective-permute-start(bf16[256,1056]{0,1:T(8,128)(2,1)S(1)} %get-tuple-element.18), channel_id=1, source_target_pairs={{0,24},{4,28},{8,0},{12,4},{16,8},{20,12},{24,16},{28,20},{1,25},{... | collective-permute-start | bytes 1622024 | tf_op jit(solution)/shard_map/ppermute | solution.py:32
  113.6 108.2 %all-gather.15.cloned.1.call-start = ((), (), s32[]{:S(2)}) async-start(), calls=%async_computation.10 | async-start | bytes 1310720 | tf_op jit(solution)/shard_map/all_gather | solution.py:61
  195.3 43.6 %copy-start.3 = (f32[64,16,256]{2,1,0:T(8,128)}, f32[64,16,256]{2,1,0:T(8,128)S(1)}, u32[]{:S(2)}) copy-start(f32[64,16,256]{2,1,0:T(8,128)S(1)} %broadcast_divide_fusion) | copy-start | bytes 3145732
  196.1 127.0 %all-gather.7.cloned.1.call-start = ((), (), s32[]{:S(2)}) async-start(), calls=%async_computation.4 | async-start | bytes 5242880 | tf_op jit(solution)/shard_map/all_gather | solution.py:85
  222.7 16.1 %copy-start = (bf16[2048,1024]{0,1:T(8,128)(2,1)S(1)}, bf16[2048,1024]{0,1:T(8,128)(2,1)}, u32[]{:S(2)}) copy-start(bf16[2048,1024]{0,1:T(8,128)(2,1)} %slice.8) | copy-start | bytes 12582916
  242.2 149.7 %reduce-scatter.6.cloned.1.call-start = ((), (), s32[]{:S(2)}) async-start(), calls=%async_computation.5 | async-start | bytes 5242880 | tf_op jit(solution)/shard_map/reduce_scatter | solution.py:91
  323.1 7.4 %collective-permute-start.7 = (bf16[1024,2048]{1,0:T(8,128)(2,1)}, bf16[1024,2048]{1,0:T(8,128)(2,1)S(1)}, u32[]{:S(2)}, u32[]{:S(2)}) collective-permute-start(bf16[1024,2048]{1,0:T(8,128)(2,1)} %all-gather.7.cloned.1.call-done), channel_id=1, source_target_pairs={{0,4},{4,0},{8,12},{12,8},{16,20},{20,16},{24,28},{28,24},{1,5},{5... | collective-permute-start | bytes 12582920 | tf_op jit(solution)/shard_map/ppermute | solution.py:87
  325.6 8.7 %copy-start.4 = (bf16[1024,512]{1,0:T(8,128)(2,1)S(1)}, bf16[1024,512]{1,0:T(8,128)(2,1)}, u32[]{:S(2)}) copy-start(bf16[1024,512]{1,0:T(8,128)(2,1)} %convolution_convert_fusion.2) | copy-start | bytes 3145732
  331.1 3.3 copy-start.1
  340.6 106.3 %all-gather.9.cloned.1.call-start = ((), (), s32[]{:S(2)}) async-start(), calls=%async_computation.6 | async-start | bytes 5242880 | tf_op jit(solution)/shard_map/all_gather | solution.py:75
  391.9 146.1 %all-gather.11.cloned.1.call-start = ((), (), s32[]{:S(2)}) async-start(), calls=%async_computation.7 | async-start | bytes 5242880 | tf_op jit(solution)/shard_map/all_gather | solution.py:85
  457.1 149.7 %reduce-scatter.8.cloned.1.call-start = ((), (), s32[]{:S(2)}) async-start(), calls=%async_computation.8 | async-start | bytes 5242880 | tf_op jit(solution)/shard_map/reduce_scatter | solution.py:91
  538.0 7.4 %collective-permute-start.8 = (bf16[1024,2048]{1,0:T(8,128)(2,1)}, bf16[1024,2048]{1,0:T(8,128)(2,1)S(1)}, u32[]{:S(2)}, u32[]{:S(2)}) collective-permute-start(bf16[1024,2048]{1,0:T(8,128)(2,1)} %all-gather.11.cloned.1.call-done), channel_id=1, source_target_pairs={{0,4},{4,0},{8,12},{12,8},{16,20},{20,16},{24,28},{28,24},{1,5},{5... | collective-permute-start | bytes 12582920 | tf_op jit(solution)/shard_map/ppermute | solution.py:87
  540.5 8.7 %copy-start.5 = (bf16[1024,512]{1,0:T(8,128)(2,1)S(1)}, bf16[1024,512]{1,0:T(8,128)(2,1)}, u32[]{:S(2)}) copy-start(bf16[1024,512]{1,0:T(8,128)(2,1)} %multiply_convert_fusion.1) | copy-start | bytes 3145732
  546.0 3.3 copy-start.2
  555.5 105.7 %all-gather.13.cloned.1.call-start = ((), (), s32[]{:S(2)}) async-start(), calls=%async_computation.9 | async-start | bytes 5242880 | tf_op jit(solution)/shard_map/all_gather | solution.py:75
Sparse Core Ops, SparseCore 0:
  15.3 55.9 reduce-scatter.3
  113.7 79.3 all-reduce.2
  196.2 25.4 all-gather.14
  242.3 80.7 all-gather.6
  340.8 51.0 reduce-scatter.5
  393.6 53.3 all-gather.8
  457.2 80.7 all-gather.10
  555.7 51.0 reduce-scatter.7
  608.6 52.5 all-gather.12

commit v9 on v7

--- a/solution.py
+++ b/solution.py
@@ -22,15 +22,37 @@
     dp_size = lax.axis_size("dp")
     row_codes = lax.all_gather(codes, "rot", axis=1, tiled=True)
 
-    def tile_part(block):
-        block_codes = lax.dynamic_slice_in_dim(row_codes, block * tile_spaces, tile_spaces, 1)
-        return jnp.concatenate([vectors, block_codes.astype(jnp.bfloat16)], axis=1)
+    def block_codes(block):
+        return lax.dynamic_slice_in_dim(
+            row_codes, block * tile_spaces, tile_spaces, 1
+        ).astype(jnp.bfloat16)
 
-    parts = [tile_part(dp_index)]
-    for shift in range(1, dp_size):
-        pairs = [(i, (i + shift) % dp_size) for i in range(dp_size)]
-        parts.append(lax.ppermute(tile_part((dp_index + shift) % dp_size), "dp", pairs))
-    joined = jnp.concatenate(parts, axis=0)
+    if dp_size % 2:
+        parts = [jnp.concatenate([vectors, block_codes(dp_index)], axis=1)]
+        for shift in range(1, dp_size):
+            pairs = [(i, (i + shift) % dp_size) for i in range(dp_size)]
+            target = (dp_index + shift) % dp_size
+            parts.append(
+                lax.ppermute(jnp.concatenate([vectors, block_codes(target)], axis=1), "dp", pairs)
+            )
+        joined = jnp.concatenate(parts, axis=0)
+    else:
+        def pair_part(block):
+            return jnp.concatenate(
+                [vectors, block_codes(block), block_codes(block ^ 1)], axis=1
+            )
+
+        parts = [pair_part(dp_index)]
+        for shift in range(2, dp_size, 2):
+            pairs = [(i, (i + shift) % dp_size) for i in range(dp_size)]
+            parts.append(lax.ppermute(pair_part((dp_index + shift) % dp_size), "dp", pairs))
+        group = jnp.concatenate(parts, axis=0)
+        mine = group[:, : block_dims + tile_spaces]
+        for_mate = jnp.concatenate(
+            [group[:, :block_dims], group[:, block_dims + tile_spaces :]], axis=1
+        )
+        mates = [(i, i ^ 1) for i in range(dp_size)]
+        joined = jnp.concatenate([mine, lax.ppermute(for_mate, "dp", mates)], axis=0)
     all_vectors = joined[:, :block_dims]
     tile_codes = joined[:, block_dims:].astype(jnp.int32)
 

time: 669 us -> 628 us (0.939)
  waiting for transfers between devices: 478 us -> 456 us
  local copies, waits for them, and re-layouts: 20.1 us -> 6.26 us
  starting transfers between devices: 19.4 us -> 5.8 us
  other arithmetic: 11.8 us -> 20.3 us
    psum x1, waiting for transfers between devices: 82.8 us -> 54.5 us  [body(): total_sums, total_counts = lax.psum((shard_code_sums, local_counts), 'dp')]
    ppermute x7 -> x4, starting transfers between devices: 18.6 us -> 5.03 us  [the longest x3 5.03 us: body(): lax.ppermute(pair_part((dp_index + shift) % dp_size), 'dp', pairs)]
    unnamed x19 -> x15, local copies, waits for them, and re-layouts: 11.6 us -> 2.52 us
    concatenate x1 -> x4, other arithmetic: 1.53 us -> 10.2 us  [the longest x1 4.12 us: body(): jnp.concatenate([group[:, :block_dims], group[:, block_dims + tile_spaces...]
    ppermute x7 -> x4, waiting for transfers between devices: 37.1 us -> 43.6 us  [the longest x3 43.6 us: body(): lax.ppermute(pair_part((dp_index + shift) % dp_size), 'dp', pairs)]
  transfers between devices with their start and end apart: 16 -> 13, of which waited for: 10 -> 10; matrix products, arithmetic and copies ran while one was open for 5% -> 4% of each run, Pallas kernels for 0% -> 0%
where the time goes in v9:
time: 628 us
  waiting for transfers between devices  456 us (73%)
  matrix products  72.9 us (12%)
  blocking collectives  51.4 us (8%)
  other arithmetic  20.3 us (3%)
  between operations  14.8 us (2%)
    all_gather x2, waiting for transfers between devices, body(): rows_b = lax.all_gather(columns, 'dp', axis=1, tiled=True)  164 us
    reduce_scatter x2, waiting for transfers between devices, body(): lax.psum_scatter(lax.dot_general(rows_b, columns, (((0,), (0,)), ((), ())...  102 us
    all_gather x2, waiting for transfers between devices, apply_gram(): lax.all_gather(gram_b, 'rot', axis=0, tiled=True)  66.1 us
    psum x1, waiting for transfers between devices, body(): total_sums, total_counts = lax.psum((shard_code_sums, local_counts), 'dp')  54.5 us
    ppermute x3, waiting for transfers between devices, body(): lax.ppermute(pair_part((dp_index + shift) % dp_size), 'dp', pairs)  43.6 us
    psum x1, blocking collectives, body(): total = lax.psum(jnp.sum(gram_f * gram_f), ('dp', 'rot'))  40.4 us
    all_gather x1, waiting for transfers between devices, body(): lax.all_gather(offered, 'rot', axis=0)[dp_index // blocks_per_rot]  25.6 us
    dot_general x2, matrix products, body(): lax.dot_general(rows_b, columns, (((0,), (0,)), ((), ())), preferred_elem...  20.3 us
  transfers between devices with their start and end apart: 13, of which 10 were waited for; matrix products, arithmetic and copies ran while one was open for 4% of the time, Pallas kernels for 0%

profile of v9, /device:TPU:0, one launch (start us, length us, event | category | flops | bytes accessed | tf_op | source)
XLA Modules:
  0.0 627.6 jit_solution(3124917151758471524)
XLA Ops:
  7.2 0.0 reduce-scatter.4.cloned.1.call-start
  7.2 7.8 %fusion.22 = f32[4096,256]{1,0:T(8,128)} fusion(bf16[1024,4096]{1,0:T(8,128)(2,1)} %param.4, bf16[256,1024]{1,0:T(8,128)(2,1)} %param.3), kind=kOutput, calls=%fused_computation.50 | convolution fusion | flops 2147483648 | bytes 13107200 | tf_op jit(solution)/shard_map/dot_general | solution.py:60
  15.1 0.0 reduce-scatter.4.cloned.1.call-update
  15.1 0.0 all-reduce.3.cloned.1.call-start
  15.2 0.9 copy-done.5
  16.1 0.2 copy.14
  16.3 11.0 %all_gather.21 = s32[256,256]{0,1:T(8,128)S(1)} all-gather(s32[256,64]{0,1:T(8,128)S(1)} %copy-done.6), channel_id=1, replica_groups=mesh['dp'=8,'rot'=4] {'rot'}, dimensions={1}, use_global_device_ids=true | all-gather | bytes 327680 | tf_op jit(solution)/shard_map/all_gather | solution.py:23
  27.4 0.1 pad_maximum_fusion.1
  27.5 4.2 collective-permute-start.2
  31.7 0.0 collective-permute-start.1
  31.7 0.8 collective-permute-start
  32.5 12.2 %collective-permute-done.2 = bf16[256,1088]{0,1:T(8,128)(2,1)S(1)} collective-permute-done((bf16[256,1088]{0,1:T(8,128)(2,1)S(1)}, bf16[256,1088]{0,1:T(8,128)(2,1)S(1)}, u32[]{:S(2)}, u32[]{:S(2)}) %collective-permute-start.2) | collective-permute-done | bytes 557088 | tf_op jit(solution)/shard_map/ppermute | solution.py:48
  44.7 31.4 %collective-permute-done.1 = bf16[256,1088]{0,1:T(8,128)(2,1)S(1)} collective-permute-done((bf16[256,1088]{0,1:T(8,128)(2,1)S(1)}, bf16[256,1088]{0,1:T(8,128)(2,1)S(1)}, u32[]{:S(2)}, u32[]{:S(2)}) %collective-permute-start.1) | collective-permute-done | bytes 557088 | tf_op jit(solution)/shard_map/ppermute | solution.py:48
  76.2 0.0 collective-permute-done
  76.2 2.5 pad_maximum_fusion
  78.7 1.4 copy-done
  80.1 0.2 slice.21
  80.3 4.1 fusion.17
  84.4 0.0 collective-permute-start.3
  84.4 3.4 convert_reduce_fusion
  87.9 1.8 slice.20
  89.6 0.0 reduce-scatter.4.cloned.1.call-done
  89.7 1.3 convert_element_type.67
  91.0 5.1 fusion.3
  96.1 0.0 all-reduce.3.cloned.1.call-update
  96.1 0.0 all-gather.15.cloned.1.call-start
  96.1 0.0 collective-permute-done.3
  96.1 0.9 fusion.20
  97.0 3.4 fusion.10
  100.4 54.5 %all-reduce.3.cloned.1.call-done = (f32[64,16,256]{2,1,0:T(8,128)}, f32[64,256]{1,0:T(8,128)}) async-done(((f32[64,16,256]{2,1,0:T(8,128)}, f32[64,256]{1,0:T(8,128)}), (f32[64,16,256]{2,1,0:T(8,128)}, f32[64,256]{1,0:T(8,128)})) %all-reduce.3.cloned.1.call-update) | async-done | bytes 1114128 | tf_op jit(solution)/shard_map/psum | solution.py:73
  154.9 0.8 broadcast_maximum_fusion
  155.8 1.3 broadcast_divide_fusion
  157.1 0.0 copy-start.2
  157.1 0.8 dynamic-slice_convert_fusion
  157.9 0.0 all-gather.15.cloned.1.call-update
  157.9 0.0 all-gather.7.cloned.1.call-start
  158.0 25.6 %all-gather.15.cloned.1.call-done = bf16[128,16,256]{2,1,0:T(8,128)(2,1)} async-done(((bf16[32,16,256]{2,1,0:T(8,128)(2,1)}), bf16[128,16,256]{2,1,0:T(8,128)(2,1)}) %all-gather.15.cloned.1.call-update) | async-done | bytes 1048592 | tf_op jit(solution)/shard_map/all_gather | solution.py:83
  183.6 1.0 fusion.39
  184.6 16.1 %fusion.11 = bf16[32,16,2048]{2,1,0:T(8,128)(2,1)S(1)} fusion(s32[32,2048]{1,0:T(8,128)S(1)} %bitcast.29, bf16[32,16,256]{2,1,0:T(8,128)(2,1)S(1)} %fusion.39), kind=kOutput, calls=%fused_computation.19 | convolution fusion | flops 554696704 | bytes 2621440 | tf_op jit(solution)/shard_map/lyg,lxg->lyx/dot_general | solution.py:86
  200.7 3.3 convolution_convert_fusion.2
  204.0 0.0 all-gather.7.cloned.1.call-update
  204.1 0.2 reduce-scatter.6.cloned.1.call-start
  204.3 82.0 %all-gather.7.cloned.1.call-done = bf16[1024,4096]{1,0:T(8,128)(2,1)} async-done(((bf16[1024,512]{1,0:T(8,128)(2,1)}), bf16[1024,4096]{1,0:T(8,128)(2,1)}) %all-gather.7.cloned.1.call-update) | async-done | bytes 8388624 | tf_op jit(solution)/shard_map/all_gather | solution.py:104
  286.2 10.2 %convolution_convert_fusion.1 = bf16[4096,512]{1,0:T(8,128)(2,1)} fusion(bf16[1024,4096]{1,0:T(8,128)(2,1)} %all-gather.7.cloned.1.call-done, bf16[1024,512]{1,0:T(8,128)(2,1)} %convolution_convert_fusion.2), kind=kOutput, calls=%fused_computation.9 | convolution fusion | flops 4297064448 | bytes 13631488 | tf_op jit(solution)/shard_map/dot_general | solution.py:106
  296.4 0.0 reduce-scatter.6.cloned.1.call-update
  296.4 0.0 all-gather.9.cloned.1.call-start
  296.5 51.2 %reduce-scatter.6.cloned.1.call-done = bf16[1024,512]{1,0:T(8,128)(2,1)} async-done(((bf16[4096,512]{1,0:T(8,128)(2,1)}), bf16[1024,512]{1,0:T(8,128)(2,1)}) %reduce-scatter.6.cloned.1.call-update) | async-done | bytes 1048592 | tf_op jit(solution)/shard_map/reduce_scatter | solution.py:105
  347.7 0.0 all-gather.9.cloned.1.call-update
  347.7 0.0 all-gather.11.cloned.1.call-start
  347.7 2.3 multiply_reduce_fusion
  350.1 40.4 %psum.23 = f32[]{:T(128)} all-reduce(f32[]{:T(128)} %multiply_reduce_fusion), channel_id=1, replica_groups=mesh['dp'=8,'rot'=4] {'dp','rot'}, use_global_device_ids=true, to_apply=%region_6.7 | all-reduce | flops 1 | bytes 8 | tf_op jit(solution)/shard_map/psum | solution.py:118
  391.1 11.6 %all-gather.9.cloned.1.call-done = bf16[4096,512]{1,0:T(8,128)(2,1)} async-done(((bf16[1024,512]{1,0:T(8,128)(2,1)}), bf16[4096,512]{1,0:T(8,128)(2,1)}) %all-gather.9.cloned.1.call-update) | async-done | bytes 4194320 | tf_op jit(solution)/shard_map/all_gather | solution.py:97
  402.8 10.1 %multiply_convert_fusion.1 = bf16[1024,512]{1,0:T(8,128)(2,1)} fusion(bf16[1024,512]{1,0:T(8,128)(2,1)S(1)} %copy-done.3, bf16[1024,4096]{1,0:T(8,128)(2,1)} %all-gather.7.cloned.1.call-done, bf16[4096,512]{1,0:T(8,128)(2,1)} %all-gather.9.cloned.1.call-done, f32[]{:T(128)S(6)} %mul.79, f32[]{:T(128)S(6)} %div.24), kind=kOutput, calls=%fused_computation.28 | convolution fusion | flops 4298113024 | bytes 14680072 | tf_op jit(solution)/shard_map/dot_general | solution.py:95
  412.9 0.0 all-gather.11.cloned.1.call-update
  412.9 0.3 reduce-scatter.8.cloned.1.call-start
  413.2 81.9 %all-gather.11.cloned.1.call-done = bf16[1024,4096]{1,0:T(8,128)(2,1)} async-done(((bf16[1024,512]{1,0:T(8,128)(2,1)}), bf16[1024,4096]{1,0:T(8,128)(2,1)}) %all-gather.11.cloned.1.call-update) | async-done | bytes 8388624 | tf_op jit(solution)/shard_map/all_gather | solution.py:104
  495.1 10.2 %convolution_convert_fusion = bf16[4096,512]{1,0:T(8,128)(2,1)} fusion(bf16[1024,4096]{1,0:T(8,128)(2,1)} %all-gather.11.cloned.1.call-done, bf16[1024,512]{1,0:T(8,128)(2,1)} %multiply_convert_fusion.1), kind=kOutput, calls=%fused_computation.8 | convolution fusion | flops 4297064448 | bytes 13631488 | tf_op jit(solution)/shard_map/dot_general | solution.py:106
  505.2 0.0 reduce-scatter.8.cloned.1.call-update
  505.2 0.0 all-gather.13.cloned.1.call-start
  505.3 51.2 %reduce-scatter.8.cloned.1.call-done = bf16[1024,512]{1,0:T(8,128)(2,1)} async-done(((bf16[4096,512]{1,0:T(8,128)(2,1)}), bf16[1024,512]{1,0:T(8,128)(2,1)}) %reduce-scatter.8.cloned.1.call-update) | async-done | bytes 1048592 | tf_op jit(solution)/shard_map/reduce_scatter | solution.py:105
  556.5 0.0 all-gather.13.cloned.1.call-update
  556.5 54.4 %all-gather.13.cloned.1.call-done = bf16[4096,512]{1,0:T(8,128)(2,1)} async-done(((bf16[1024,512]{1,0:T(8,128)(2,1)}), bf16[4096,512]{1,0:T(8,128)(2,1)}) %all-gather.13.cloned.1.call-update) | async-done | bytes 4194320 | tf_op jit(solution)/shard_map/all_gather | solution.py:97
  610.9 0.0 copy-done.4
  610.9 10.1 %multiply_convert_fusion = bf16[1024,512]{1,0:T(8,128)(2,1)} fusion(bf16[1024,512]{1,0:T(8,128)(2,1)S(1)} %copy-done.4, bf16[1024,4096]{1,0:T(8,128)(2,1)} %all-gather.11.cloned.1.call-done, bf16[4096,512]{1,0:T(8,128)(2,1)} %all-gather.13.cloned.1.call-done), kind=kOutput, calls=%fused_computation.27 | convolution fusion | flops 4298113024 | bytes 14680064 | tf_op jit(solution)/shard_map/dot_general | solution.py:95
  (11 shorter events, 0.0 us)
Async XLA Ops:
  7.2 82.5 %reduce-scatter.4.cloned.1.call-start = ((), (), s32[]{:S(2)}) async-start(), calls=%async_computation.3 | async-start | bytes 5242880 | tf_op jit(solution)/shard_map/reduce_scatter | solution.py:59
  15.0 1.0 copy-start.5
  15.0 1.3 copy-start.6
  15.1 139.8 %all-reduce.3.cloned.1.call-start = ((), (), s32[]{:S(2)}) async-start(), calls=%async_computation.11 | async-start | bytes 2228224 | tf_op jit(solution)/shard_map/psum | solution.py:73
  27.5 17.2 %collective-permute-start.2 = (bf16[256,1088]{0,1:T(8,128)(2,1)S(1)}, bf16[256,1088]{0,1:T(8,128)(2,1)S(1)}, u32[]{:S(2)}, u32[]{:S(2)}) collective-permute-start(bf16[256,1088]{0,1:T(8,128)(2,1)S(1)} %get-tuple-element.14), channel_id=1, source_target_pairs={{0,24},{4,28},{8,0},{12,4},{16,8},{20,12},{24,16},{28,20},{1,25},{... | collective-permute-start | bytes 1671176 | tf_op jit(solution)/shard_map/ppermute | solution.py:48
  31.7 44.5 %collective-permute-start.1 = (bf16[256,1088]{0,1:T(8,128)(2,1)S(1)}, bf16[256,1088]{0,1:T(8,128)(2,1)S(1)}, u32[]{:S(2)}, u32[]{:S(2)}) collective-permute-start(bf16[256,1088]{0,1:T(8,128)(2,1)S(1)} %get-tuple-element.13), channel_id=1, source_target_pairs={{0,16},{4,20},{8,24},{12,28},{16,0},{20,4},{24,8},{28,12},{1,17},{... | collective-permute-start | bytes 1671176 | tf_op jit(solution)/shard_map/ppermute | solution.py:48
  31.7 44.5 %collective-permute-start = (bf16[256,1088]{0,1:T(8,128)(2,1)S(1)}, bf16[256,1088]{0,1:T(8,128)(2,1)S(1)}, u32[]{:S(2)}, u32[]{:S(2)}) collective-permute-start(bf16[256,1088]{0,1:T(8,128)(2,1)S(1)} %get-tuple-element.12), channel_id=1, source_target_pairs={{0,8},{4,12},{8,16},{12,20},{16,24},{20,28},{24,0},{28,4},{1,9},{5... | collective-permute-start | bytes 1671176 | tf_op jit(solution)/shard_map/ppermute | solution.py:48
  78.7 1.4 copy-start
  84.4 11.7 %collective-permute-start.3 = (bf16[1024,1056]{0,1:T(8,128)(2,1)}, bf16[1024,1056]{0,1:T(8,128)(2,1)}, u32[]{:S(2)}, u32[]{:S(2)}) collective-permute-start(bf16[1024,1056]{0,1:T(8,128)(2,1)} %fusion.17), channel_id=1, source_target_pairs={{0,4},{4,0},{8,12},{12,8},{16,20},{20,16},{24,28},{28,24},{1,5},{5... | collective-permute-start | bytes 6488072 | tf_op jit(solution)/shard_map/ppermute | solution.py:55
  96.1 87.5 %all-gather.15.cloned.1.call-start = ((), (), s32[]{:S(2)}) async-start(), calls=%async_computation.10 | async-start | bytes 1310720 | tf_op jit(solution)/shard_map/all_gather | solution.py:83
  157.1 43.6 %copy-start.2 = (f32[64,16,256]{2,1,0:T(8,128)}, f32[64,16,256]{2,1,0:T(8,128)S(1)}, u32[]{:S(2)}) copy-start(f32[64,16,256]{2,1,0:T(8,128)S(1)} %broadcast_divide_fusion) | copy-start | bytes 3145732
  157.9 128.3 %all-gather.7.cloned.1.call-start = ((), (), s32[]{:S(2)}) async-start(), calls=%async_computation.4 | async-start | bytes 9437184 | tf_op jit(solution)/shard_map/all_gather | solution.py:104
  184.6 16.1 %copy-start.1 = (bf16[2048,1024]{0,1:T(8,128)(2,1)S(1)}, bf16[2048,1024]{0,1:T(8,128)(2,1)}, u32[]{:S(2)}) copy-start(bf16[2048,1024]{0,1:T(8,128)(2,1)} %fusion.10) | copy-start | bytes 12582916
  204.1 143.6 %reduce-scatter.6.cloned.1.call-start = ((), (), s32[]{:S(2)}) async-start(), calls=%async_computation.5 | async-start | bytes 5242880 | tf_op jit(solution)/shard_map/reduce_scatter | solution.py:105
  296.4 106.4 %copy-start.3 = (bf16[1024,512]{1,0:T(8,128)(2,1)S(1)}, bf16[1024,512]{1,0:T(8,128)(2,1)}, u32[]{:S(2)}) copy-start(bf16[1024,512]{1,0:T(8,128)(2,1)} %convolution_convert_fusion.2) | copy-start | bytes 3145732
  296.4 106.3 %all-gather.9.cloned.1.call-start = ((), (), s32[]{:S(2)}) async-start(), calls=%async_computation.6 | async-start | bytes 5242880 | tf_op jit(solution)/shard_map/all_gather | solution.py:97
  347.7 147.4 %all-gather.11.cloned.1.call-start = ((), (), s32[]{:S(2)}) async-start(), calls=%async_computation.7 | async-start | bytes 9437184 | tf_op jit(solution)/shard_map/all_gather | solution.py:104
  412.9 143.6 %reduce-scatter.8.cloned.1.call-start = ((), (), s32[]{:S(2)}) async-start(), calls=%async_computation.8 | async-start | bytes 5242880 | tf_op jit(solution)/shard_map/reduce_scatter | solution.py:105
  505.2 105.7 %copy-start.4 = (bf16[1024,512]{1,0:T(8,128)(2,1)S(1)}, bf16[1024,512]{1,0:T(8,128)(2,1)}, u32[]{:S(2)}) copy-start(bf16[1024,512]{1,0:T(8,128)(2,1)} %multiply_convert_fusion.1) | copy-start | bytes 3145732
  505.2 105.7 %all-gather.13.cloned.1.call-start = ((), (), s32[]{:S(2)}) async-start(), calls=%async_computation.9 | async-start | bytes 5242880 | tf_op jit(solution)/shard_map/all_gather | solution.py:97
Sparse Core Ops, SparseCore 0:
  15.2 55.9 reduce-scatter.3
  96.2 58.6 all-reduce.2
  158.1 25.4 all-gather.14
  204.2 82.0 all-gather.6
  296.5 51.0 reduce-scatter.5
  349.4 53.3 all-gather.8
  413.0 82.0 all-gather.10
  505.4 51.0 reduce-scatter.7
  558.3 52.5 all-gather.12

commit v10 on v9

--- a/solution.py
+++ b/solution.py
@@ -102,17 +102,16 @@
     new_tile = None
     for iteration in range(ITERS):
         rows_b = lax.all_gather(columns, "dp", axis=1, tiled=True)
-        gram_part = lax.psum_scatter(
-            lax.dot_general(
-                rows_b,
-                columns,
-                (((0,), (0,)), ((), ())),
-                preferred_element_type=jnp.float32,
-            ).astype(jnp.bfloat16),
-            "rot",
-            scatter_dimension=0,
-            tiled=True,
-        )
+        partial = lax.dot_general(
+            rows_b,
+            columns,
+            (((0,), (0,)), ((), ())),
+            preferred_element_type=jnp.float32,
+        ).astype(jnp.bfloat16)
+        if iteration == 0:
+            gram_part = lax.psum_scatter(partial, "rot", scatter_dimension=0, tiled=True)
+        else:
+            gram_part = lax.psum(partial, "rot")
         if iteration == 0:
             gram_f = gram_part.astype(jnp.float32)
             total = lax.psum(jnp.sum(gram_f * gram_f), ("dp", "rot"))
@@ -122,7 +121,7 @@
                 1.5 * columns.astype(jnp.float32) - 0.5 * (factor * factor) * product
             )
         else:
-            product = apply_gram(rows_b, gram_part)
+            product = jnp.dot(rows_b, gram_part, preferred_element_type=jnp.float32)
             new_tile = 1.5 * columns.astype(jnp.float32) - 0.5 * product
         columns = new_tile.astype(jnp.bfloat16)
     new_rotation = (math.sqrt(width) * new_tile).astype(jnp.bfloat16)

time: 628 us -> 625 us (level)
    psum x0 -> x1, waiting for transfers between devices: none -> 102 us  [body(): gram_part = lax.psum(partial, 'rot')]
    all_gather x2 -> x1, waiting for transfers between devices: 66.1 us -> 11.5 us  [apply_gram(): lax.all_gather(gram_b, 'rot', axis=0, tiled=True)]
    reduce_scatter x2 -> x1, waiting for transfers between devices: 102 us -> 51.2 us  [body(): lax.psum_scatter(partial, 'rot', scatter_dimension=0, tiled=True)]
    ppermute x3, waiting for transfers between devices: 43.6 us -> 31.8 us  [body(): lax.ppermute(pair_part((dp_index + shift) % dp_size), 'dp', pairs)]
    psum x1, waiting for transfers between devices: 54.5 us -> 65.7 us  [body(): total_sums, total_counts = lax.psum((shard_code_sums, local_counts), 'dp')]
    dot_general x0 -> x1, matrix products: none -> 10.1 us  [body(): product = jnp.dot(rows_b, gram_part, preferred_element_type=jnp.float32)]
    dot_general x2 -> x1, matrix products: 20.2 us -> 10.1 us  [apply_gram(): jnp.dot(rows_b, lax.all_gather(gram_b, 'rot', axis=0, tiled=True), prefer...]
  transfers between devices with their start and end apart: 13 -> 12, of which waited for: 10 -> 9; matrix products, arithmetic and copies ran while one was open for 4% -> 4% of each run, Pallas kernels for 0% -> 0%
where the time goes in v10:
time: 625 us
  waiting for transfers between devices  452 us (72%)
  matrix products  72.9 us (12%)
  blocking collectives  51.3 us (8%)
  other arithmetic  20.4 us (3%)
  between operations  15.2 us (2%)
  starting transfers between devices  6.66 us (1%)
  local copies, waits for them, and re-layouts  6.26 us (1%)
    all_gather x2, waiting for transfers between devices, body(): rows_b = lax.all_gather(columns, 'dp', axis=1, tiled=True)  164 us
    psum x1, waiting for transfers between devices, body(): gram_part = lax.psum(partial, 'rot')  102 us
    psum x1, waiting for transfers between devices, body(): total_sums, total_counts = lax.psum((shard_code_sums, local_counts), 'dp')  65.7 us
    reduce_scatter x1, waiting for transfers between devices, body(): lax.psum_scatter(partial, 'rot', scatter_dimension=0, tiled=True)  51.2 us
    psum x1, blocking collectives, body(): total = lax.psum(jnp.sum(gram_f * gram_f), ('dp', 'rot'))  40.3 us
    ppermute x3, waiting for transfers between devices, body(): lax.ppermute(pair_part((dp_index + shift) % dp_size), 'dp', pairs)  31.8 us
    all_gather x1, waiting for transfers between devices, body(): lax.all_gather(offered, 'rot', axis=0)[dp_index // blocks_per_rot]  25.6 us
    dot_general x2, matrix products, body(): lax.dot_general(rows_b, columns, (((0,), (0,)), ((), ())), preferred_elem...  20.2 us
  transfers between devices with their start and end apart: 12, of which 9 were waited for; matrix products, arithmetic and copies ran while one was open for 4% of the time, Pallas kernels for 0%

profile of v10, /device:TPU:0, one launch (start us, length us, event | category | flops | bytes accessed | tf_op | source)
XLA Modules:
  0.0 624.7 jit_solution(17052377595605976044)
XLA Ops:
  7.2 0.0 reduce-scatter.3.cloned.1.call-start
  7.2 7.9 %fusion.22 = f32[4096,256]{1,0:T(8,128)} fusion(bf16[1024,4096]{1,0:T(8,128)(2,1)} %param.4, bf16[256,1024]{1,0:T(8,128)(2,1)} %param.3), kind=kOutput, calls=%fused_computation.50 | convolution fusion | flops 2147483648 | bytes 13107200 | tf_op jit(solution)/shard_map/dot_general | solution.py:60
  15.1 0.0 reduce-scatter.3.cloned.1.call-update
  15.1 0.0 all-reduce.6.cloned.1.call-start
  15.2 0.9 copy-done.5
  16.1 0.2 copy.14
  16.4 0.0 copy-done.6
  16.4 11.0 %all_gather.18 = s32[256,256]{0,1:T(8,128)S(1)} all-gather(s32[256,64]{0,1:T(8,128)S(1)} %copy-done.6), channel_id=1, replica_groups=mesh['dp'=8,'rot'=4] {'rot'}, dimensions={1}, use_global_device_ids=true | all-gather | bytes 327680 | tf_op jit(solution)/shard_map/all_gather | solution.py:23
  27.4 0.1 pad_maximum_fusion.1
  27.5 1.8 collective-permute-start
  29.3 3.0 collective-permute-start.1
  32.3 1.2 collective-permute-start.2
  33.5 11.9 %collective-permute-done = bf16[256,1088]{0,1:T(8,128)(2,1)S(1)} collective-permute-done((bf16[256,1088]{0,1:T(8,128)(2,1)S(1)}, bf16[256,1088]{0,1:T(8,128)(2,1)S(1)}, u32[]{:S(2)}, u32[]{:S(2)}) %collective-permute-start) | collective-permute-done | bytes 557088 | tf_op jit(solution)/shard_map/ppermute | solution.py:48
  45.3 19.9 %collective-permute-done.1 = bf16[256,1088]{0,1:T(8,128)(2,1)S(1)} collective-permute-done((bf16[256,1088]{0,1:T(8,128)(2,1)S(1)}, bf16[256,1088]{0,1:T(8,128)(2,1)S(1)}, u32[]{:S(2)}, u32[]{:S(2)}) %collective-permute-start.1) | collective-permute-done | bytes 557088 | tf_op jit(solution)/shard_map/ppermute | solution.py:48
  65.2 0.0 collective-permute-done.2
  65.2 2.5 pad_maximum_fusion
  67.8 0.0 copy-start
  67.8 1.4 copy-done
  69.2 0.2 slice.21
  69.4 4.1 fusion.17
  73.5 0.0 collective-permute-start.3
  73.5 3.4 convert_reduce_fusion
  76.9 1.8 slice.20
  78.7 0.0 reduce-scatter.3.cloned.1.call-done
  78.8 1.3 convert_element_type.67
  80.0 5.1 fusion.3
  85.1 0.0 all-reduce.6.cloned.1.call-update
  85.2 0.0 all-gather.12.cloned.1.call-start
  85.2 0.0 collective-permute-done.3
  85.2 0.9 fusion.20
  86.1 3.4 fusion.10
  89.5 65.7 %all-reduce.6.cloned.1.call-done = (f32[64,16,256]{2,1,0:T(8,128)}, f32[64,256]{1,0:T(8,128)}) async-done(((f32[64,16,256]{2,1,0:T(8,128)}, f32[64,256]{1,0:T(8,128)}), (f32[64,16,256]{2,1,0:T(8,128)}, f32[64,256]{1,0:T(8,128)})) %all-reduce.6.cloned.1.call-update) | async-done | bytes 1114128 | tf_op jit(solution)/shard_map/psum | solution.py:73
  155.2 0.8 broadcast_maximum_fusion
  156.1 1.3 broadcast_divide_fusion
  157.4 0.0 copy-start.2
  157.4 0.8 dynamic-slice_convert_fusion
  158.2 0.0 all-gather.12.cloned.1.call-update
  158.2 0.0 all-gather.6.cloned.1.call-start
  158.3 25.6 %all-gather.12.cloned.1.call-done = bf16[128,16,256]{2,1,0:T(8,128)(2,1)} async-done(((bf16[32,16,256]{2,1,0:T(8,128)(2,1)}), bf16[128,16,256]{2,1,0:T(8,128)(2,1)}) %all-gather.12.cloned.1.call-update) | async-done | bytes 1048592 | tf_op jit(solution)/shard_map/all_gather | solution.py:83
  183.9 1.0 fusion.39
  184.9 0.0 copy-start.1
  184.9 16.1 %fusion.11 = bf16[32,16,2048]{2,1,0:T(8,128)(2,1)S(1)} fusion(s32[32,2048]{1,0:T(8,128)S(1)} %bitcast.29, bf16[32,16,256]{2,1,0:T(8,128)(2,1)S(1)} %fusion.39), kind=kOutput, calls=%fused_computation.19 | convolution fusion | flops 554696704 | bytes 2621440 | tf_op jit(solution)/shard_map/lyg,lxg->lyx/dot_general | solution.py:86
  201.0 3.3 convolution_convert_fusion.2
  204.3 0.0 all-gather.6.cloned.1.call-update
  204.3 0.2 reduce-scatter.5.cloned.1.call-start
  204.6 82.0 %all-gather.6.cloned.1.call-done = bf16[1024,4096]{1,0:T(8,128)(2,1)} async-done(((bf16[1024,512]{1,0:T(8,128)(2,1)}), bf16[1024,4096]{1,0:T(8,128)(2,1)}) %all-gather.6.cloned.1.call-update) | async-done | bytes 8388624 | tf_op jit(solution)/shard_map/all_gather | solution.py:104
  286.5 10.1 %convolution_convert_fusion.1 = bf16[4096,512]{1,0:T(8,128)(2,1)} fusion(bf16[1024,4096]{1,0:T(8,128)(2,1)} %all-gather.6.cloned.1.call-done, bf16[1024,512]{1,0:T(8,128)(2,1)} %convolution_convert_fusion.2), kind=kOutput, calls=%fused_computation.9 | convolution fusion | flops 4297064448 | bytes 13631488 | tf_op jit(solution)/shard_map/dot_general | solution.py:105
  296.7 0.0 reduce-scatter.5.cloned.1.call-update
  296.7 0.0 all-gather.8.cloned.1.call-start
  296.8 51.2 %reduce-scatter.5.cloned.1.call-done = bf16[1024,512]{1,0:T(8,128)(2,1)} async-done(((bf16[4096,512]{1,0:T(8,128)(2,1)}), bf16[1024,512]{1,0:T(8,128)(2,1)}) %reduce-scatter.5.cloned.1.call-update) | async-done | bytes 1048592 | tf_op jit(solution)/shard_map/reduce_scatter | solution.py:112
  348.0 0.0 all-gather.8.cloned.1.call-update
  348.0 0.0 all-gather.10.cloned.1.call-start
  348.0 2.4 multiply_reduce_fusion
  350.5 40.3 %psum.30 = f32[]{:T(128)} all-reduce(f32[]{:T(128)} %multiply_reduce_fusion), channel_id=1, replica_groups=mesh['dp'=8,'rot'=4] {'dp','rot'}, use_global_device_ids=true, to_apply=%region_6.7 | all-reduce | flops 1 | bytes 8 | tf_op jit(solution)/shard_map/psum | solution.py:117
  391.6 11.5 %all-gather.8.cloned.1.call-done = bf16[4096,512]{1,0:T(8,128)(2,1)} async-done(((bf16[1024,512]{1,0:T(8,128)(2,1)}), bf16[4096,512]{1,0:T(8,128)(2,1)}) %all-gather.8.cloned.1.call-update) | async-done | bytes 4194320 | tf_op jit(solution)/shard_map/all_gather | solution.py:97
  403.0 10.1 %multiply_convert_fusion.1 = bf16[1024,512]{1,0:T(8,128)(2,1)} fusion(bf16[1024,512]{1,0:T(8,128)(2,1)S(1)} %copy-done.3, bf16[1024,4096]{1,0:T(8,128)(2,1)} %all-gather.6.cloned.1.call-done, bf16[4096,512]{1,0:T(8,128)(2,1)} %all-gather.8.cloned.1.call-done, f32[]{:T(128)S(6)} %mul.79, f32[]{:T(128)S(6)} %div.24), kind=kOutput, calls=%fused_computation.28 | convolution fusion | flops 4298113024 | bytes 14680072 | tf_op jit(solution)/shard_map/dot_general | solution.py:95
  413.2 0.0 all-gather.10.cloned.1.call-update
  413.2 0.3 all-reduce.4.cloned.1.call-start
  413.4 81.9 %all-gather.10.cloned.1.call-done = bf16[1024,4096]{1,0:T(8,128)(2,1)} async-done(((bf16[1024,512]{1,0:T(8,128)(2,1)}), bf16[1024,4096]{1,0:T(8,128)(2,1)}) %all-gather.10.cloned.1.call-update) | async-done | bytes 8388624 | tf_op jit(solution)/shard_map/all_gather | solution.py:104
  495.4 10.1 %convolution_convert_fusion = bf16[4096,512]{1,0:T(8,128)(2,1)} fusion(bf16[1024,4096]{1,0:T(8,128)(2,1)} %all-gather.10.cloned.1.call-done, bf16[1024,512]{1,0:T(8,128)(2,1)} %multiply_convert_fusion.1), kind=kOutput, calls=%fused_computation.8 | convolution fusion | flops 4297064448 | bytes 13631488 | tf_op jit(solution)/shard_map/dot_general | solution.py:105
  505.5 0.0 all-reduce.4.cloned.1.call-update
  505.5 102.3 %all-reduce.4.cloned.1.call-done = bf16[4096,512]{1,0:T(8,128)(2,1)} async-done(((bf16[4096,512]{1,0:T(8,128)(2,1)}), bf16[4096,512]{1,0:T(8,128)(2,1)}) %all-reduce.4.cloned.1.call-update) | async-done | bytes 4194320 | tf_op jit(solution)/shard_map/psum | solution.py:114
  607.8 0.0 copy-done.4
  607.8 10.1 %multiply_convert_fusion = bf16[1024,512]{1,0:T(8,128)(2,1)} fusion(bf16[1024,512]{1,0:T(8,128)(2,1)S(1)} %copy-done.4, bf16[1024,4096]{1,0:T(8,128)(2,1)} %all-gather.10.cloned.1.call-done, bf16[4096,512]{1,0:T(8,128)(2,1)} %all-reduce.4.cloned.1.call-done), kind=kOutput, calls=%fused_computation.27 | convolution fusion | flops 4298113024 | bytes 14680064 | tf_op jit(solution)/shard_map/dot_general | solution.py:124
  (8 shorter events, 0.0 us)
Async XLA Ops:
  7.2 71.6 %reduce-scatter.3.cloned.1.call-start = ((), (), s32[]{:S(2)}) async-start(), calls=%async_computation.2 | async-start | bytes 5242880 | tf_op jit(solution)/shard_map/reduce_scatter | solution.py:59
  15.1 1.0 copy-start.5
  15.1 1.3 copy-start.6
  15.1 140.1 %all-reduce.6.cloned.1.call-start = ((), (), s32[]{:S(2)}) async-start(), calls=%async_computation.9 | async-start | bytes 2228224 | tf_op jit(solution)/shard_map/psum | solution.py:73
  27.5 17.8 %collective-permute-start = (bf16[256,1088]{0,1:T(8,128)(2,1)S(1)}, bf16[256,1088]{0,1:T(8,128)(2,1)S(1)}, u32[]{:S(2)}, u32[]{:S(2)}) collective-permute-start(bf16[256,1088]{0,1:T(8,128)(2,1)S(1)} %get-tuple-element.12), channel_id=1, source_target_pairs={{0,8},{4,12},{8,16},{12,20},{16,24},{20,28},{24,0},{28,4},{1,9},{5... | collective-permute-start | bytes 1671176 | tf_op jit(solution)/shard_map/ppermute | solution.py:48
  29.3 35.9 %collective-permute-start.1 = (bf16[256,1088]{0,1:T(8,128)(2,1)S(1)}, bf16[256,1088]{0,1:T(8,128)(2,1)S(1)}, u32[]{:S(2)}, u32[]{:S(2)}) collective-permute-start(bf16[256,1088]{0,1:T(8,128)(2,1)S(1)} %get-tuple-element.13), channel_id=1, source_target_pairs={{0,16},{4,20},{8,24},{12,28},{16,0},{20,4},{24,8},{28,12},{1,17},{... | collective-permute-start | bytes 1671176 | tf_op jit(solution)/shard_map/ppermute | solution.py:48
  32.3 33.0 %collective-permute-start.2 = (bf16[256,1088]{0,1:T(8,128)(2,1)S(1)}, bf16[256,1088]{0,1:T(8,128)(2,1)S(1)}, u32[]{:S(2)}, u32[]{:S(2)}) collective-permute-start(bf16[256,1088]{0,1:T(8,128)(2,1)S(1)} %get-tuple-element.14), channel_id=1, source_target_pairs={{0,24},{4,28},{8,0},{12,4},{16,8},{20,12},{24,16},{28,20},{1,25},{... | collective-permute-start | bytes 1671176 | tf_op jit(solution)/shard_map/ppermute | solution.py:48
  67.8 1.4 copy-start
  73.5 11.7 %collective-permute-start.3 = (bf16[1024,1056]{0,1:T(8,128)(2,1)}, bf16[1024,1056]{0,1:T(8,128)(2,1)}, u32[]{:S(2)}, u32[]{:S(2)}) collective-permute-start(bf16[1024,1056]{0,1:T(8,128)(2,1)} %fusion.17), channel_id=1, source_target_pairs={{0,4},{4,0},{8,12},{12,8},{16,20},{20,16},{24,28},{28,24},{1,5},{5... | collective-permute-start | bytes 6488072 | tf_op jit(solution)/shard_map/ppermute | solution.py:55
  85.2 98.7 %all-gather.12.cloned.1.call-start = ((), (), s32[]{:S(2)}) async-start(), calls=%async_computation.8 | async-start | bytes 1310720 | tf_op jit(solution)/shard_map/all_gather | solution.py:83
  157.4 43.6 %copy-start.2 = (f32[64,16,256]{2,1,0:T(8,128)}, f32[64,16,256]{2,1,0:T(8,128)S(1)}, u32[]{:S(2)}) copy-start(f32[64,16,256]{2,1,0:T(8,128)S(1)} %broadcast_divide_fusion) | copy-start | bytes 3145732
  158.2 128.3 %all-gather.6.cloned.1.call-start = ((), (), s32[]{:S(2)}) async-start(), calls=%async_computation.3 | async-start | bytes 9437184 | tf_op jit(solution)/shard_map/all_gather | solution.py:104
  184.9 16.1 %copy-start.1 = (bf16[2048,1024]{0,1:T(8,128)(2,1)S(1)}, bf16[2048,1024]{0,1:T(8,128)(2,1)}, u32[]{:S(2)}) copy-start(bf16[2048,1024]{0,1:T(8,128)(2,1)} %fusion.10) | copy-start | bytes 12582916
  204.3 143.6 %reduce-scatter.5.cloned.1.call-start = ((), (), s32[]{:S(2)}) async-start(), calls=%async_computation.4 | async-start | bytes 5242880 | tf_op jit(solution)/shard_map/reduce_scatter | solution.py:112
  296.7 106.4 %copy-start.3 = (bf16[1024,512]{1,0:T(8,128)(2,1)S(1)}, bf16[1024,512]{1,0:T(8,128)(2,1)}, u32[]{:S(2)}) copy-start(bf16[1024,512]{1,0:T(8,128)(2,1)} %convolution_convert_fusion.2) | copy-start | bytes 3145732
  296.7 106.3 %all-gather.8.cloned.1.call-start = ((), (), s32[]{:S(2)}) async-start(), calls=%async_computation.5 | async-start | bytes 5242880 | tf_op jit(solution)/shard_map/all_gather | solution.py:97
  348.0 147.4 %all-gather.10.cloned.1.call-start = ((), (), s32[]{:S(2)}) async-start(), calls=%async_computation.6 | async-start | bytes 9437184 | tf_op jit(solution)/shard_map/all_gather | solution.py:104
  413.2 194.6 %all-reduce.4.cloned.1.call-start = ((), (), s32[]{:S(2)}) async-start(), calls=%async_computation.7 | async-start | bytes 8388608 | tf_op jit(solution)/shard_map/psum | solution.py:114
  505.5 102.3 %copy-start.4 = (bf16[1024,512]{1,0:T(8,128)(2,1)S(1)}, bf16[1024,512]{1,0:T(8,128)(2,1)}, u32[]{:S(2)}) copy-start(bf16[1024,512]{1,0:T(8,128)(2,1)} %multiply_convert_fusion.1) | copy-start | bytes 3145732
Sparse Core Ops, SparseCore 0:
  15.2 55.9 reduce-scatter.2
  85.3 69.8 all-reduce.5
  158.4 25.4 all-gather.11
  204.5 82.0 all-gather.5
  296.8 51.0 reduce-scatter.4
  349.6 53.3 all-gather.7
  413.3 82.0 all-gather.9
  505.6 102.0 all-reduce.3

commit v11 on v10

--- a/solution.py
+++ b/solution.py
@@ -71,9 +71,6 @@
     )
     local_counts = jnp.sum(code_indicator, axis=1, dtype=jnp.float32)
     total_sums, total_counts = lax.psum((shard_code_sums, local_counts), "dp")
-    total_sums, total_counts, all_vectors, tile_codes = lax.optimization_barrier(
-        (total_sums, total_counts, all_vectors, tile_codes)
-    )
     book = total_sums / jnp.maximum(total_counts, 1.0)[:, None, :]
     codebook = book.reshape(block_dims, K)
     blocks_per_rot = local_spaces // tile_spaces
@@ -81,6 +78,9 @@
         book.astype(jnp.bfloat16), (dp_index % blocks_per_rot) * tile_spaces, tile_spaces, 0
     )
     tile_book = lax.all_gather(offered, "rot", axis=0)[dp_index // blocks_per_rot]
+    tile_book, all_vectors, tile_codes = lax.optimization_barrier(
+        (tile_book, all_vectors, tile_codes)
+    )
 
     tile_indicator = (tile_codes.T[:, :, None] == code_ids[None, None, :]).astype(jnp.bfloat16)
     rebuilt_t = jnp.einsum(

time: 625 us -> 616 us (0.986)
  waiting for transfers between devices: 452 us -> 444 us
  transfers between devices with their start and end apart: 12 -> 12, of which waited for: 9 -> 10; matrix products, arithmetic and copies ran while one was open for 4% -> 4% of each run, Pallas kernels for 0% -> 0%
where the time goes in v11:
time: 616 us
  waiting for transfers between devices  444 us (72%)
  matrix products  72.8 us (12%)
  blocking collectives  51.3 us (8%)
  other arithmetic  20.3 us (3%)
  between operations  15.1 us (2%)
  starting transfers between devices  6.66 us (1%)
    all_gather x2, waiting for transfers between devices, body(): rows_b = lax.all_gather(columns, 'dp', axis=1, tiled=True)  164 us
    psum x1, waiting for transfers between devices, body(): gram_part = lax.psum(partial, 'rot')  102 us
    psum x1, waiting for transfers between devices, body(): total_sums, total_counts = lax.psum((shard_code_sums, local_counts), 'dp')  64.6 us
    reduce_scatter x1, waiting for transfers between devices, body(): lax.psum_scatter(partial, 'rot', scatter_dimension=0, tiled=True)  51.2 us
    psum x1, blocking collectives, body(): total = lax.psum(jnp.sum(gram_f * gram_f), ('dp', 'rot'))  40.3 us
    ppermute x3, waiting for transfers between devices, body(): lax.ppermute(pair_part((dp_index + shift) % dp_size), 'dp', pairs)  28.4 us
    all_gather x1, waiting for transfers between devices, body(): lax.all_gather(offered, 'rot', axis=0)[dp_index // blocks_per_rot]  21.1 us
    dot_general x2, matrix products, body(): lax.dot_general(rows_b, columns, (((0,), (0,)), ((), ())), preferred_elem...  20.3 us
  transfers between devices with their start and end apart: 12, of which 10 were waited for; matrix products, arithmetic and copies ran while one was open for 4% of the time, Pallas kernels for 0%

profile of v11, /device:TPU:0, one launch (start us, length us, event | category | flops | bytes accessed | tf_op | source)
XLA Modules:
  0.0 616.0 jit_solution(11668680264245755234)
XLA Ops:
  7.2 0.0 reduce-scatter.3.cloned.1.call-start
  7.2 7.8 %fusion.19 = f32[4096,256]{1,0:T(8,128)} fusion(bf16[1024,4096]{1,0:T(8,128)(2,1)} %param.4, bf16[256,1024]{1,0:T(8,128)(2,1)} %param.3), kind=kOutput, calls=%fused_computation.48 | convolution fusion | flops 2147483648 | bytes 13107200 | tf_op jit(solution)/shard_map/dot_general | solution.py:60
  15.1 0.0 reduce-scatter.3.cloned.1.call-update
  15.1 0.0 all-reduce.6.cloned.1.call-start
  15.2 0.9 copy-done.6
  16.1 0.2 copy.14
  16.3 0.0 copy-done.7
  16.4 11.0 %all_gather.20 = s32[256,256]{0,1:T(8,128)S(1)} all-gather(s32[256,64]{0,1:T(8,128)S(1)} %copy-done.7), channel_id=1, replica_groups=mesh['dp'=8,'rot'=4] {'rot'}, dimensions={1}, use_global_device_ids=true | all-gather | bytes 327680 | tf_op jit(solution)/shard_map/all_gather | solution.py:23
  27.4 0.1 pad_maximum_fusion.1
  27.5 1.8 collective-permute-start
  29.3 3.0 collective-permute-start.1
  32.3 1.2 collective-permute-start.2
  33.4 3.4 convert_reduce_fusion
  36.9 8.4 %collective-permute-done = bf16[256,1088]{0,1:T(8,128)(2,1)S(1)} collective-permute-done((bf16[256,1088]{0,1:T(8,128)(2,1)S(1)}, bf16[256,1088]{0,1:T(8,128)(2,1)S(1)}, u32[]{:S(2)}, u32[]{:S(2)}) %collective-permute-start) | collective-permute-done | bytes 557088 | tf_op jit(solution)/shard_map/ppermute | solution.py:48
  45.3 19.9 %collective-permute-done.1 = bf16[256,1088]{0,1:T(8,128)(2,1)S(1)} collective-permute-done((bf16[256,1088]{0,1:T(8,128)(2,1)S(1)}, bf16[256,1088]{0,1:T(8,128)(2,1)S(1)}, u32[]{:S(2)}, u32[]{:S(2)}) %collective-permute-start.1) | collective-permute-done | bytes 557088 | tf_op jit(solution)/shard_map/ppermute | solution.py:48
  65.2 0.0 collective-permute-done.2
  65.2 0.8 copy-done.1
  66.0 0.2 copy-done.2
  66.2 2.4 pad_maximum_fusion
  68.7 1.5 slice.21
  70.2 1.0 reduce-scatter.3.cloned.1.call-done
  71.2 1.3 convert_element_type.67
  72.5 5.1 fusion.3
  77.6 0.0 all-reduce.6.cloned.1.call-update
  77.6 0.0 all-gather.12.cloned.1.call-start
  77.7 4.2 fusion.17
  81.9 0.0 collective-permute-start.3
  81.9 64.6 %all-reduce.6.cloned.1.call-done = (f32[64,16,256]{2,1,0:T(8,128)}, f32[64,256]{1,0:T(8,128)}) async-done(((f32[64,16,256]{2,1,0:T(8,128)}, f32[64,256]{1,0:T(8,128)}), (f32[64,16,256]{2,1,0:T(8,128)}, f32[64,256]{1,0:T(8,128)})) %all-reduce.6.cloned.1.call-update) | async-done | bytes 1114128 | tf_op jit(solution)/shard_map/psum | solution.py:73
  146.5 0.8 broadcast_maximum_fusion
  147.3 1.3 broadcast_divide_fusion
  148.7 0.0 copy-start.3
  148.7 0.8 dynamic-slice_convert_fusion
  149.5 0.0 all-gather.12.cloned.1.call-update
  149.5 0.0 all-gather.6.cloned.1.call-start
  149.6 0.2 slice.20
  149.8 0.0 collective-permute-done.3
  149.8 0.9 fusion.18
  150.7 0.0 copy-done.3
  150.7 3.4 fusion.10
  154.1 21.1 %all-gather.12.cloned.1.call-done = bf16[128,16,256]{2,1,0:T(8,128)(2,1)} async-done(((bf16[32,16,256]{2,1,0:T(8,128)(2,1)}), bf16[128,16,256]{2,1,0:T(8,128)(2,1)}) %all-gather.12.cloned.1.call-update) | async-done | bytes 1048592 | tf_op jit(solution)/shard_map/all_gather | solution.py:80
  175.2 1.0 dynamic-slice_bitcast_fusion
  176.2 16.1 %fusion.11 = bf16[32,16,2048]{2,1,0:T(8,128)(2,1)S(1)} fusion(bf16[32,16,256]{2,1,0:T(8,128)(2,1)S(1)} %dynamic-slice_bitcast_fusion, s32[32,2048]{1,0:T(8,128)S(1)} %bitcast.25), kind=kOutput, calls=%fused_computation.19 | convolution fusion | flops 554696704 | bytes 2621440 | tf_op jit(solution)/shard_map/lyg,lxg->lyx/dot_general | solution.py:86
  192.3 0.0 copy-done
  192.3 3.3 convolution_convert_fusion.2
  195.6 0.0 all-gather.6.cloned.1.call-update
  195.6 0.2 reduce-scatter.5.cloned.1.call-start
  195.9 82.0 %all-gather.6.cloned.1.call-done = bf16[1024,4096]{1,0:T(8,128)(2,1)} async-done(((bf16[1024,512]{1,0:T(8,128)(2,1)}), bf16[1024,4096]{1,0:T(8,128)(2,1)}) %all-gather.6.cloned.1.call-update) | async-done | bytes 8388624 | tf_op jit(solution)/shard_map/all_gather | solution.py:104
  277.8 10.2 %convolution_convert_fusion.1 = bf16[4096,512]{1,0:T(8,128)(2,1)} fusion(bf16[1024,4096]{1,0:T(8,128)(2,1)} %all-gather.6.cloned.1.call-done, bf16[1024,512]{1,0:T(8,128)(2,1)} %convolution_convert_fusion.2), kind=kOutput, calls=%fused_computation.9 | convolution fusion | flops 4297064448 | bytes 13631488 | tf_op jit(solution)/shard_map/dot_general | solution.py:105
  288.0 0.0 reduce-scatter.5.cloned.1.call-update
  288.0 0.0 all-gather.8.cloned.1.call-start
  288.0 51.2 %reduce-scatter.5.cloned.1.call-done = bf16[1024,512]{1,0:T(8,128)(2,1)} async-done(((bf16[4096,512]{1,0:T(8,128)(2,1)}), bf16[1024,512]{1,0:T(8,128)(2,1)}) %reduce-scatter.5.cloned.1.call-update) | async-done | bytes 1048592 | tf_op jit(solution)/shard_map/reduce_scatter | solution.py:112
  339.2 0.0 all-gather.8.cloned.1.call-update
  339.3 0.0 all-gather.10.cloned.1.call-start
  339.3 2.4 multiply_reduce_fusion
  341.7 40.3 %psum.30 = f32[]{:T(128)} all-reduce(f32[]{:T(128)} %multiply_reduce_fusion), channel_id=1, replica_groups=mesh['dp'=8,'rot'=4] {'dp','rot'}, use_global_device_ids=true, to_apply=%region_6.7 | all-reduce | flops 1 | bytes 8 | tf_op jit(solution)/shard_map/psum | solution.py:117
  382.7 11.6 %all-gather.8.cloned.1.call-done = bf16[4096,512]{1,0:T(8,128)(2,1)} async-done(((bf16[1024,512]{1,0:T(8,128)(2,1)}), bf16[4096,512]{1,0:T(8,128)(2,1)}) %all-gather.8.cloned.1.call-update) | async-done | bytes 4194320 | tf_op jit(solution)/shard_map/all_gather | solution.py:97
  394.4 10.1 %multiply_convert_fusion.1 = bf16[1024,512]{1,0:T(8,128)(2,1)} fusion(bf16[1024,512]{1,0:T(8,128)(2,1)S(1)} %copy-done.4, bf16[1024,4096]{1,0:T(8,128)(2,1)} %all-gather.6.cloned.1.call-done, bf16[4096,512]{1,0:T(8,128)(2,1)} %all-gather.8.cloned.1.call-done, f32[]{:T(128)S(6)} %mul.79, f32[]{:T(128)S(6)} %div.24), kind=kOutput, calls=%fused_computation.28 | convolution fusion | flops 4298113024 | bytes 14680072 | tf_op jit(solution)/shard_map/dot_general | solution.py:95
  404.5 0.0 all-gather.10.cloned.1.call-update
  404.5 0.3 all-reduce.4.cloned.1.call-start
  404.7 81.9 %all-gather.10.cloned.1.call-done = bf16[1024,4096]{1,0:T(8,128)(2,1)} async-done(((bf16[1024,512]{1,0:T(8,128)(2,1)}), bf16[1024,4096]{1,0:T(8,128)(2,1)}) %all-gather.10.cloned.1.call-update) | async-done | bytes 8388624 | tf_op jit(solution)/shard_map/all_gather | solution.py:104
  486.7 10.1 %convolution_convert_fusion = bf16[4096,512]{1,0:T(8,128)(2,1)} fusion(bf16[1024,4096]{1,0:T(8,128)(2,1)} %all-gather.10.cloned.1.call-done, bf16[1024,512]{1,0:T(8,128)(2,1)} %multiply_convert_fusion.1), kind=kOutput, calls=%fused_computation.8 | convolution fusion | flops 4297064448 | bytes 13631488 | tf_op jit(solution)/shard_map/dot_general | solution.py:105
  496.8 0.0 all-reduce.4.cloned.1.call-update
  496.8 102.3 %all-reduce.4.cloned.1.call-done = bf16[4096,512]{1,0:T(8,128)(2,1)} async-done(((bf16[4096,512]{1,0:T(8,128)(2,1)}), bf16[4096,512]{1,0:T(8,128)(2,1)}) %all-reduce.4.cloned.1.call-update) | async-done | bytes 4194320 | tf_op jit(solution)/shard_map/psum | solution.py:114
  599.1 10.1 %multiply_convert_fusion = bf16[1024,512]{1,0:T(8,128)(2,1)} fusion(bf16[1024,512]{1,0:T(8,128)(2,1)S(1)} %copy-done.5, bf16[1024,4096]{1,0:T(8,128)(2,1)} %all-gather.10.cloned.1.call-done, bf16[4096,512]{1,0:T(8,128)(2,1)} %all-reduce.4.cloned.1.call-done), kind=kOutput, calls=%fused_computation.27 | convolution fusion | flops 4298113024 | bytes 14680064 | tf_op jit(solution)/shard_map/dot_general | solution.py:124
  (10 shorter events, 0.0 us)
Async XLA Ops:
  7.2 64.0 %reduce-scatter.3.cloned.1.call-start = ((), (), s32[]{:S(2)}) async-start(), calls=%async_computation.2 | async-start | bytes 5242880 | tf_op jit(solution)/shard_map/reduce_scatter | solution.py:59
  15.1 1.0 copy-start.6
  15.1 1.3 copy-start.7
  15.1 131.4 %all-reduce.6.cloned.1.call-start = ((), (), s32[]{:S(2)}) async-start(), calls=%async_computation.9 | async-start | bytes 2228224 | tf_op jit(solution)/shard_map/psum | solution.py:73
  27.5 17.8 %collective-permute-start = (bf16[256,1088]{0,1:T(8,128)(2,1)S(1)}, bf16[256,1088]{0,1:T(8,128)(2,1)S(1)}, u32[]{:S(2)}, u32[]{:S(2)}) collective-permute-start(bf16[256,1088]{0,1:T(8,128)(2,1)S(1)} %get-tuple-element.10), channel_id=1, source_target_pairs={{0,8},{4,12},{8,16},{12,20},{16,24},{20,28},{24,0},{28,4},{1,9},{5... | collective-permute-start | bytes 1671176 | tf_op jit(solution)/shard_map/ppermute | solution.py:48
  29.3 35.9 %collective-permute-start.1 = (bf16[256,1088]{0,1:T(8,128)(2,1)S(1)}, bf16[256,1088]{0,1:T(8,128)(2,1)S(1)}, u32[]{:S(2)}, u32[]{:S(2)}) collective-permute-start(bf16[256,1088]{0,1:T(8,128)(2,1)S(1)} %get-tuple-element.11), channel_id=1, source_target_pairs={{0,16},{4,20},{8,24},{12,28},{16,0},{20,4},{24,8},{28,12},{1,17},{... | collective-permute-start | bytes 1671176 | tf_op jit(solution)/shard_map/ppermute | solution.py:48
  32.3 33.0 %collective-permute-start.2 = (bf16[256,1088]{0,1:T(8,128)(2,1)S(1)}, bf16[256,1088]{0,1:T(8,128)(2,1)S(1)}, u32[]{:S(2)}, u32[]{:S(2)}) collective-permute-start(bf16[256,1088]{0,1:T(8,128)(2,1)S(1)} %get-tuple-element.12), channel_id=1, source_target_pairs={{0,24},{4,28},{8,0},{12,4},{16,8},{20,12},{24,16},{28,20},{1,25},{... | collective-permute-start | bytes 1671176 | tf_op jit(solution)/shard_map/ppermute | solution.py:48
  65.2 0.8 copy-start.1
  65.2 1.0 copy-start.2
  77.6 97.6 %all-gather.12.cloned.1.call-start = ((), (), s32[]{:S(2)}) async-start(), calls=%async_computation.8 | async-start | bytes 1310720 | tf_op jit(solution)/shard_map/all_gather | solution.py:80
  81.9 67.9 %collective-permute-start.3 = (bf16[1024,1056]{0,1:T(8,128)(2,1)}, bf16[1024,1056]{0,1:T(8,128)(2,1)}, u32[]{:S(2)}, u32[]{:S(2)}) collective-permute-start(bf16[1024,1056]{0,1:T(8,128)(2,1)} %fusion.17), channel_id=1, source_target_pairs={{0,4},{4,0},{8,12},{12,8},{16,20},{20,16},{24,28},{28,24},{1,5},{5... | collective-permute-start | bytes 6488072 | tf_op jit(solution)/shard_map/ppermute | solution.py:55
  148.7 2.0 copy-start.3
  149.5 128.3 %all-gather.6.cloned.1.call-start = ((), (), s32[]{:S(2)}) async-start(), calls=%async_computation.3 | async-start | bytes 9437184 | tf_op jit(solution)/shard_map/all_gather | solution.py:104
  176.2 16.1 %copy-start = (bf16[2048,1024]{0,1:T(8,128)(2,1)S(1)}, bf16[2048,1024]{0,1:T(8,128)(2,1)}, u32[]{:S(2)}) copy-start(bf16[2048,1024]{0,1:T(8,128)(2,1)} %fusion.10) | copy-start | bytes 12582916
  195.6 143.6 %reduce-scatter.5.cloned.1.call-start = ((), (), s32[]{:S(2)}) async-start(), calls=%async_computation.4 | async-start | bytes 5242880 | tf_op jit(solution)/shard_map/reduce_scatter | solution.py:112
  288.0 106.4 %copy-start.4 = (bf16[1024,512]{1,0:T(8,128)(2,1)S(1)}, bf16[1024,512]{1,0:T(8,128)(2,1)}, u32[]{:S(2)}) copy-start(bf16[1024,512]{1,0:T(8,128)(2,1)} %convolution_convert_fusion.2) | copy-start | bytes 3145732
  288.0 106.4 %all-gather.8.cloned.1.call-start = ((), (), s32[]{:S(2)}) async-start(), calls=%async_computation.5 | async-start | bytes 5242880 | tf_op jit(solution)/shard_map/all_gather | solution.py:97
  339.3 147.4 %all-gather.10.cloned.1.call-start = ((), (), s32[]{:S(2)}) async-start(), calls=%async_computation.6 | async-start | bytes 9437184 | tf_op jit(solution)/shard_map/all_gather | solution.py:104
  404.5 194.6 %all-reduce.4.cloned.1.call-start = ((), (), s32[]{:S(2)}) async-start(), calls=%async_computation.7 | async-start | bytes 8388608 | tf_op jit(solution)/shard_map/psum | solution.py:114
  496.8 102.3 %copy-start.5 = (bf16[1024,512]{1,0:T(8,128)(2,1)S(1)}, bf16[1024,512]{1,0:T(8,128)(2,1)}, u32[]{:S(2)}) copy-start(bf16[1024,512]{1,0:T(8,128)(2,1)} %multiply_convert_fusion.1) | copy-start | bytes 3145732
Sparse Core Ops, SparseCore 0:
  15.2 55.9 reduce-scatter.2
  77.7 68.7 all-reduce.5
  149.7 25.4 all-gather.11
  195.7 82.0 all-gather.5
  288.1 51.0 reduce-scatter.4
  340.9 53.3 all-gather.7
  404.6 82.0 all-gather.9
  496.9 102.0 all-reduce.3

commit v12 on v11

--- a/solution.py
+++ b/solution.py
@@ -82,10 +82,7 @@
         (tile_book, all_vectors, tile_codes)
     )
 
-    tile_indicator = (tile_codes.T[:, :, None] == code_ids[None, None, :]).astype(jnp.bfloat16)
-    rebuilt_t = jnp.einsum(
-        "lyg,lxg->lyx", tile_book, tile_indicator, preferred_element_type=jnp.float32
-    )
+    rebuilt_t = jnp.take_along_axis(tile_book, tile_codes.T[:, None, :], axis=2)
     rebuilt_t = rebuilt_t.astype(jnp.bfloat16).reshape(tile_cols, all_vectors.shape[0])
     cross_tile = lax.dot_general(
         all_vectors, rebuilt_t, (((0,), (1,)), ((), ())), preferred_element_type=jnp.float32

time: 616 us -> 1250 us (2.03)
  local copies, waits for them, and re-layouts: 5.59 us -> 656 us
  matrix products: 72.8 us -> 56.8 us
    gather x0 -> x2, local copies, waits for them, and re-layouts: none -> 647 us  [body(): rebuilt_t = jnp.take_along_axis(tile_book, tile_codes.T[:, None, :], axis=2)]
    dot_general x1 -> x0, matrix products: 16.1 us -> none  [body(): jnp.einsum('lyg,lxg->lyx', tile_book, tile_indicator, preferred_element_t...]
  transfers between devices with their start and end apart: 12 -> 12, of which waited for: 10 -> 10; matrix products, arithmetic and copies ran while one was open for 4% -> 2% of each run, Pallas kernels for 0% -> 0%
where the time goes in v12:
time: 1250 us
  local copies, waits for them, and re-layouts  656 us (52%)
  waiting for transfers between devices  444 us (36%)
  matrix products  56.8 us (5%)
  blocking collectives  51.4 us (4%)
  other arithmetic  20.8 us (2%)
  between operations  15.1 us (1%)
    gather x2, local copies, waits for them, and re-layouts, body(): rebuilt_t = jnp.take_along_axis(tile_book, tile_codes.T[:, None, :], axis=2)  647 us
    all_gather x2, waiting for transfers between devices, body(): rows_b = lax.all_gather(columns, 'dp', axis=1, tiled=True)  164 us
    psum x1, waiting for transfers between devices, body(): gram_part = lax.psum(partial, 'rot')  102 us
    psum x1, waiting for transfers between devices, body(): total_sums, total_counts = lax.psum((shard_code_sums, local_counts), 'dp')  64.6 us
    reduce_scatter x1, waiting for transfers between devices, body(): lax.psum_scatter(partial, 'rot', scatter_dimension=0, tiled=True)  51.2 us
    psum x1, blocking collectives, body(): total = lax.psum(jnp.sum(gram_f * gram_f), ('dp', 'rot'))  40.4 us
    ppermute x3, waiting for transfers between devices, body(): lax.ppermute(pair_part((dp_index + shift) % dp_size), 'dp', pairs)  28.4 us
  transfers between devices with their start and end apart: 12, of which 10 were waited for; matrix products, arithmetic and copies ran while one was open for 2% of the time, Pallas kernels for 0%

profile of v12, /device:TPU:0, one launch (start us, length us, event | category | flops | bytes accessed | tf_op | source)
XLA Modules:
  0.0 1250.6 jit_solution(5058009144251274857)
XLA Ops:
  7.2 0.0 reduce-scatter.3.cloned.1.call-start
  7.2 7.8 fusion.17
  15.1 0.0 reduce-scatter.3.cloned.1.call-update
  15.1 0.0 all-reduce.6.cloned.1.call-start
  15.2 0.9 copy-done.6
  16.1 0.2 copy.28
  16.4 11.0 all_gather.20
  27.4 0.1 pad_maximum_fusion.1
  27.5 1.8 collective-permute-start
  29.3 3.0 collective-permute-start.1
  32.3 1.2 collective-permute-start.2
  33.4 3.4 convert_reduce_fusion
  36.9 8.4 collective-permute-done
  45.3 19.9 %collective-permute-done.1 = bf16[256,1088]{0,1:T(8,128)(2,1)S(1)} collective-permute-done((bf16[256,1088]{0,1:T(8,128)(2,1)S(1)}, bf16[256,1088]{0,1:T(8,128)(2,1)S(1)}, u32[]{:S(2)}, u32[]{:S(2)}) %collective-permute-start.1) | collective-permute-done | bytes 557088 | tf_op jit(solution)/shard_map/ppermute | solution.py:48
  65.2 0.8 copy-done.1
  66.0 0.2 copy-done.2
  66.2 2.4 pad_maximum_fusion
  68.7 1.5 slice.23
  70.2 1.0 reduce-scatter.3.cloned.1.call-done
  71.2 1.3 convert_element_type.63
  72.5 5.1 fusion.1
  77.6 0.0 all-reduce.6.cloned.1.call-update
  77.6 0.0 all-gather.12.cloned.1.call-start
  77.7 4.2 fusion.14
  81.9 64.6 %all-reduce.6.cloned.1.call-done = (f32[64,16,256]{2,1,0:T(8,128)}, f32[64,256]{1,0:T(8,128)}) async-done(((f32[64,16,256]{2,1,0:T(8,128)}, f32[64,256]{1,0:T(8,128)}), (f32[64,16,256]{2,1,0:T(8,128)}, f32[64,256]{1,0:T(8,128)})) %all-reduce.6.cloned.1.call-update) | async-done | bytes 1114128 | tf_op jit(solution)/shard_map/psum | solution.py:73
  146.5 0.8 broadcast_maximum_fusion
  147.3 1.3 broadcast_divide_fusion
  148.7 0.0 copy-start.3
  148.7 0.8 dynamic-slice_convert_fusion
  149.5 0.0 all-gather.12.cloned.1.call-update
  149.5 0.0 all-gather.6.cloned.1.call-start
  149.6 0.2 slice.22
  149.8 0.9 fusion.16
  150.7 3.4 fusion.8
  154.1 21.1 %all-gather.12.cloned.1.call-done = bf16[128,16,256]{2,1,0:T(8,128)(2,1)} async-done(((bf16[32,16,256]{2,1,0:T(8,128)(2,1)}), bf16[128,16,256]{2,1,0:T(8,128)(2,1)}) %all-gather.12.cloned.1.call-update) | async-done | bytes 1048592 | tf_op jit(solution)/shard_map/all_gather | solution.py:80
  175.2 1.0 constant_dynamic-slice_fusion
  176.2 1.0 copy.33
  177.2 0.1 compare_and_fusion
  177.3 0.1 fusion.15
  177.4 634.4 %gather_fusion = bf16[65536,16]{1,0:T(8,128)(2,1)} fusion(bf16[32,16,256]{1,2,0:T(8,128)(2,1)S(1)} %bitcast.37, s32[65536]{0:T(1024)S(1)} %bitcast.36), kind=kCustom, calls=%fused_computation | custom fusion | bytes 4718592 | tf_op jit(solution)/shard_map/jit(take_along_axis)/gather | solution.py:85
  811.8 12.8 %copy.32 = bf16[32,2048,16]{1,2,0:T(8,128)(2,1)S(1)} copy(bf16[32,2048,16]{2,1,0:T(8,128)(2,1)} %bitcast.38) | data formatting | bytes 4194304 | tf_op jit(solution)/shard_map/jit(take_along_axis)/gather | solution.py:85
  824.6 0.3 broadcast_select_fusion
  825.0 1.8 copy-done
  826.8 3.3 convolution_convert_fusion.2
  830.1 0.0 all-gather.6.cloned.1.call-update
  830.2 0.2 reduce-scatter.5.cloned.1.call-start
  830.4 82.0 %all-gather.6.cloned.1.call-done = bf16[1024,4096]{1,0:T(8,128)(2,1)} async-done(((bf16[1024,512]{1,0:T(8,128)(2,1)}), bf16[1024,4096]{1,0:T(8,128)(2,1)}) %all-gather.6.cloned.1.call-update) | async-done | bytes 8388624 | tf_op jit(solution)/shard_map/all_gather | solution.py:101
  912.4 10.2 convolution_convert_fusion.1
  922.5 0.0 reduce-scatter.5.cloned.1.call-update
  922.5 0.0 all-gather.8.cloned.1.call-start
  922.6 51.2 %reduce-scatter.5.cloned.1.call-done = bf16[1024,512]{1,0:T(8,128)(2,1)} async-done(((bf16[4096,512]{1,0:T(8,128)(2,1)}), bf16[1024,512]{1,0:T(8,128)(2,1)}) %reduce-scatter.5.cloned.1.call-update) | async-done | bytes 1048592 | tf_op jit(solution)/shard_map/reduce_scatter | solution.py:109
  973.8 0.0 all-gather.8.cloned.1.call-update
  973.8 0.0 all-gather.10.cloned.1.call-start
  973.9 2.4 multiply_reduce_fusion
  976.3 40.4 %psum.30 = f32[]{:T(128)} all-reduce(f32[]{:T(128)} %multiply_reduce_fusion), channel_id=1, replica_groups=mesh['dp'=8,'rot'=4] {'dp','rot'}, use_global_device_ids=true, to_apply=%region_6.7 | all-reduce | flops 1 | bytes 8 | tf_op jit(solution)/shard_map/psum | solution.py:114
  1017.3 11.5 all-gather.8.cloned.1.call-done
  1028.9 10.1 multiply_convert_fusion.1
  1039.0 0.0 all-gather.10.cloned.1.call-update
  1039.0 0.3 all-reduce.4.cloned.1.call-start
  1039.3 81.9 %all-gather.10.cloned.1.call-done = bf16[1024,4096]{1,0:T(8,128)(2,1)} async-done(((bf16[1024,512]{1,0:T(8,128)(2,1)}), bf16[1024,4096]{1,0:T(8,128)(2,1)}) %all-gather.10.cloned.1.call-update) | async-done | bytes 8388624 | tf_op jit(solution)/shard_map/all_gather | solution.py:101
  1121.2 10.1 convolution_convert_fusion
  1131.3 0.0 all-reduce.4.cloned.1.call-update
  1131.3 102.3 %all-reduce.4.cloned.1.call-done = bf16[4096,512]{1,0:T(8,128)(2,1)} async-done(((bf16[4096,512]{1,0:T(8,128)(2,1)}), bf16[4096,512]{1,0:T(8,128)(2,1)}) %all-reduce.4.cloned.1.call-update) | async-done | bytes 4194320 | tf_op jit(solution)/shard_map/psum | solution.py:111
  1233.6 10.1 multiply_convert_fusion
  (16 shorter events, 0.1 us)
Async XLA Ops:
  7.2 64.0 %reduce-scatter.3.cloned.1.call-start = ((), (), s32[]{:S(2)}) async-start(), calls=%async_computation.2 | async-start | bytes 5242880 | tf_op jit(solution)/shard_map/reduce_scatter | solution.py:59
  15.1 1.0 copy-start.6
  15.1 1.3 copy-start.7
  15.1 131.4 %all-reduce.6.cloned.1.call-start = ((), (), s32[]{:S(2)}) async-start(), calls=%async_computation.9 | async-start | bytes 2228224 | tf_op jit(solution)/shard_map/psum | solution.py:73
  27.5 17.8 %collective-permute-start = (bf16[256,1088]{0,1:T(8,128)(2,1)S(1)}, bf16[256,1088]{0,1:T(8,128)(2,1)S(1)}, u32[]{:S(2)}, u32[]{:S(2)}) collective-permute-start(bf16[256,1088]{0,1:T(8,128)(2,1)S(1)} %get-tuple-element.10), channel_id=1, source_target_pairs={{0,8},{4,12},{8,16},{12,20},{16,24},{20,28},{24,0},{28,4},{1,9},{5... | collective-permute-start | bytes 1671176 | tf_op jit(solution)/shard_map/ppermute | solution.py:48
  29.3 35.9 %collective-permute-start.1 = (bf16[256,1088]{0,1:T(8,128)(2,1)S(1)}, bf16[256,1088]{0,1:T(8,128)(2,1)S(1)}, u32[]{:S(2)}, u32[]{:S(2)}) collective-permute-start(bf16[256,1088]{0,1:T(8,128)(2,1)S(1)} %get-tuple-element.11), channel_id=1, source_target_pairs={{0,16},{4,20},{8,24},{12,28},{16,0},{20,4},{24,8},{28,12},{1,17},{... | collective-permute-start | bytes 1671176 | tf_op jit(solution)/shard_map/ppermute | solution.py:48
  32.3 33.0 %collective-permute-start.2 = (bf16[256,1088]{0,1:T(8,128)(2,1)S(1)}, bf16[256,1088]{0,1:T(8,128)(2,1)S(1)}, u32[]{:S(2)}, u32[]{:S(2)}) collective-permute-start(bf16[256,1088]{0,1:T(8,128)(2,1)S(1)} %get-tuple-element.12), channel_id=1, source_target_pairs={{0,24},{4,28},{8,0},{12,4},{16,8},{20,12},{24,16},{28,20},{1,25},{... | collective-permute-start | bytes 1671176 | tf_op jit(solution)/shard_map/ppermute | solution.py:48
  65.2 0.8 copy-start.1
  65.2 1.0 copy-start.2
  77.6 97.6 %all-gather.12.cloned.1.call-start = ((), (), s32[]{:S(2)}) async-start(), calls=%async_computation.8 | async-start | bytes 1310720 | tf_op jit(solution)/shard_map/all_gather | solution.py:80
  81.9 67.9 %collective-permute-start.3 = (bf16[1024,1056]{0,1:T(8,128)(2,1)}, bf16[1024,1056]{0,1:T(8,128)(2,1)}, u32[]{:S(2)}, u32[]{:S(2)}) collective-permute-start(bf16[1024,1056]{0,1:T(8,128)(2,1)} %fusion.14), channel_id=1, source_target_pairs={{0,4},{4,0},{8,12},{12,8},{16,20},{20,16},{24,28},{28,24},{1,5},{5... | collective-permute-start | bytes 6488072 | tf_op jit(solution)/shard_map/ppermute | solution.py:55
  148.7 2.0 copy-start.3
  149.5 762.8 %all-gather.6.cloned.1.call-start = ((), (), s32[]{:S(2)}) async-start(), calls=%async_computation.3 | async-start | bytes 9437184 | tf_op jit(solution)/shard_map/all_gather | solution.py:101
  824.6 2.2 copy-start
  830.2 143.6 %reduce-scatter.5.cloned.1.call-start = ((), (), s32[]{:S(2)}) async-start(), calls=%async_computation.4 | async-start | bytes 5242880 | tf_op jit(solution)/shard_map/reduce_scatter | solution.py:109
  922.5 106.4 %copy-start.4 = (bf16[1024,512]{1,0:T(8,128)(2,1)S(1)}, bf16[1024,512]{1,0:T(8,128)(2,1)}, u32[]{:S(2)}) copy-start(bf16[1024,512]{1,0:T(8,128)(2,1)} %convolution_convert_fusion.2) | copy-start | bytes 3145732
  922.5 106.3 %all-gather.8.cloned.1.call-start = ((), (), s32[]{:S(2)}) async-start(), calls=%async_computation.5 | async-start | bytes 5242880 | tf_op jit(solution)/shard_map/all_gather | solution.py:94
  973.8 147.4 %all-gather.10.cloned.1.call-start = ((), (), s32[]{:S(2)}) async-start(), calls=%async_computation.6 | async-start | bytes 9437184 | tf_op jit(solution)/shard_map/all_gather | solution.py:101
  1039.0 194.6 %all-reduce.4.cloned.1.call-start = ((), (), s32[]{:S(2)}) async-start(), calls=%async_computation.7 | async-start | bytes 8388608 | tf_op jit(solution)/shard_map/psum | solution.py:111
  1131.3 102.3 %copy-start.5 = (bf16[1024,512]{1,0:T(8,128)(2,1)S(1)}, bf16[1024,512]{1,0:T(8,128)(2,1)}, u32[]{:S(2)}) copy-start(bf16[1024,512]{1,0:T(8,128)(2,1)} %multiply_convert_fusion.1) | copy-start | bytes 3145732
Sparse Core Ops, SparseCore 0:
  15.2 55.9 reduce-scatter.2
  77.7 68.7 all-reduce.5
  149.7 25.4 all-gather.11
  830.3 82.0 all-gather.5
  922.7 51.0 reduce-scatter.4
  975.5 53.3 all-gather.7
  1039.1 82.0 all-gather.9
  1131.5 102.0 all-reduce.3

commit v13 on v12

--- a/solution.py
+++ b/solution.py
@@ -82,11 +82,13 @@
         (tile_book, all_vectors, tile_codes)
     )
 
-    rebuilt_t = jnp.take_along_axis(tile_book, tile_codes.T[:, None, :], axis=2)
-    rebuilt_t = rebuilt_t.astype(jnp.bfloat16).reshape(tile_cols, all_vectors.shape[0])
-    cross_tile = lax.dot_general(
-        all_vectors, rebuilt_t, (((0,), (1,)), ((), ())), preferred_element_type=jnp.float32
+    tile_indicator = (tile_codes.T[:, :, None] == code_ids[None, None, :]).astype(jnp.bfloat16)
+    rebuilt = jnp.einsum(
+        "lxg,lyg->lxy", tile_indicator, tile_book, preferred_element_type=jnp.float32
     ).astype(jnp.bfloat16)
+    cross_tile = jnp.einsum(
+        "xa,lxy->aly", all_vectors, rebuilt, preferred_element_type=jnp.float32
+    ).reshape(block_dims, tile_cols).astype(jnp.bfloat16)
 
     def apply_gram(rows_b, gram_b):
         return jnp.dot(

time: 1250 us -> 617 us (0.49)
  local copies, waits for them, and re-layouts: 656 us -> 7.68 us
  matrix products: 56.8 us -> 72.3 us
    gather x2 -> x0, local copies, waits for them, and re-layouts: 647 us -> none  [body(): rebuilt_t = jnp.take_along_axis(tile_book, tile_codes.T[:, None, :], axis=2)]
    dot_general x1 -> x2, matrix products: 3.33 us -> 18.8 us  [the longest x1 16.1 us: body(): jnp.einsum('lxg,lyg->lxy', tile_indicator, tile_book, preferred_element_t...]
  transfers between devices with their start and end apart: 12 -> 12, of which waited for: 10 -> 10; matrix products, arithmetic and copies ran while one was open for 2% -> 4% of each run, Pallas kernels for 0% -> 0%
where the time goes in v13:
time: 617 us
  waiting for transfers between devices  443 us (72%)
  matrix products  72.3 us (12%)
  blocking collectives  51.5 us (8%)
  other arithmetic  20.3 us (3%)
  between operations  15.1 us (2%)
  local copies, waits for them, and re-layouts  7.68 us (1%)
  starting transfers between devices  6.66 us (1%)
    all_gather x2, waiting for transfers between devices, body(): rows_b = lax.all_gather(columns, 'dp', axis=1, tiled=True)  164 us
    psum x1, waiting for transfers between devices, body(): gram_part = lax.psum(partial, 'rot')  102 us
    psum x1, waiting for transfers between devices, body(): total_sums, total_counts = lax.psum((shard_code_sums, local_counts), 'dp')  64.6 us
    reduce_scatter x1, waiting for transfers between devices, body(): lax.psum_scatter(partial, 'rot', scatter_dimension=0, tiled=True)  51.2 us
    psum x1, blocking collectives, body(): total = lax.psum(jnp.sum(gram_f * gram_f), ('dp', 'rot'))  40.5 us
    ppermute x3, waiting for transfers between devices, body(): lax.ppermute(pair_part((dp_index + shift) % dp_size), 'dp', pairs)  28.4 us
    all_gather x1, waiting for transfers between devices, body(): lax.all_gather(offered, 'rot', axis=0)[dp_index // blocks_per_rot]  21.1 us
    dot_general x2, matrix products, body(): lax.dot_general(rows_b, columns, (((0,), (0,)), ((), ())), preferred_elem...  20.3 us
  transfers between devices with their start and end apart: 12, of which 10 were waited for; matrix products, arithmetic and copies ran while one was open for 4% of the time, Pallas kernels for 0%

profile of v13, /device:TPU:0, one launch (start us, length us, event | category | flops | bytes accessed | tf_op | source)
XLA Modules:
  0.0 616.9 jit_solution(17006208243110445827)
XLA Ops:
  7.2 0.0 reduce-scatter.3.cloned.1.call-start
  7.2 7.8 %fusion.27 = f32[4096,256]{1,0:T(8,128)} fusion(bf16[1024,4096]{1,0:T(8,128)(2,1)} %param.4, bf16[256,1024]{1,0:T(8,128)(2,1)} %param.3), kind=kOutput, calls=%fused_computation.51 | convolution fusion | flops 2147483648 | bytes 13107200 | tf_op jit(solution)/shard_map/dot_general | solution.py:60
  15.1 0.0 reduce-scatter.3.cloned.1.call-update
  15.1 0.0 all-reduce.6.cloned.1.call-start
  15.2 0.9 copy-done.6
  16.1 0.2 copy.25
  16.4 11.0 %all_gather.20 = s32[256,256]{0,1:T(8,128)S(1)} all-gather(s32[256,64]{0,1:T(8,128)S(1)} %copy-done.7), channel_id=1, replica_groups=mesh['dp'=8,'rot'=4] {'rot'}, dimensions={1}, use_global_device_ids=true | all-gather | bytes 327680 | tf_op jit(solution)/shard_map/all_gather | solution.py:23
  27.4 0.1 pad_maximum_fusion.1
  27.5 1.8 collective-permute-start
  29.3 3.0 collective-permute-start.1
  32.3 1.2 collective-permute-start.2
  33.4 3.4 convert_reduce_fusion
  36.9 8.4 %collective-permute-done = bf16[256,1088]{0,1:T(8,128)(2,1)S(1)} collective-permute-done((bf16[256,1088]{0,1:T(8,128)(2,1)S(1)}, bf16[256,1088]{0,1:T(8,128)(2,1)S(1)}, u32[]{:S(2)}, u32[]{:S(2)}) %collective-permute-start) | collective-permute-done | bytes 557088 | tf_op jit(solution)/shard_map/ppermute | solution.py:48
  45.3 19.9 %collective-permute-done.1 = bf16[256,1088]{0,1:T(8,128)(2,1)S(1)} collective-permute-done((bf16[256,1088]{0,1:T(8,128)(2,1)S(1)}, bf16[256,1088]{0,1:T(8,128)(2,1)S(1)}, u32[]{:S(2)}, u32[]{:S(2)}) %collective-permute-start.1) | collective-permute-done | bytes 557088 | tf_op jit(solution)/shard_map/ppermute | solution.py:48
  65.2 0.0 collective-permute-done.2
  65.2 0.8 copy-done.2
  66.0 0.2 copy-done.3
  66.2 2.4 pad_maximum_fusion
  68.7 1.5 slice.21
  70.2 1.0 reduce-scatter.3.cloned.1.call-done
  71.2 1.3 convert_element_type.70
  72.5 5.1 fusion.3
  77.6 0.0 all-reduce.6.cloned.1.call-update
  77.6 0.0 all-gather.12.cloned.1.call-start
  77.7 4.2 fusion.19
  81.9 0.0 collective-permute-start.3
  81.9 64.6 %all-reduce.6.cloned.1.call-done = (f32[64,16,256]{2,1,0:T(8,128)}, f32[64,256]{1,0:T(8,128)}) async-done(((f32[64,16,256]{2,1,0:T(8,128)}, f32[64,256]{1,0:T(8,128)}), (f32[64,16,256]{2,1,0:T(8,128)}, f32[64,256]{1,0:T(8,128)})) %all-reduce.6.cloned.1.call-update) | async-done | bytes 1114128 | tf_op jit(solution)/shard_map/psum | solution.py:73
  146.5 0.8 broadcast_maximum_fusion
  147.3 1.3 broadcast_divide_fusion
  148.7 0.0 copy-start.4
  148.7 0.8 dynamic-slice_convert_fusion
  149.5 0.0 all-gather.12.cloned.1.call-update
  149.5 0.0 all-gather.6.cloned.1.call-start
  149.6 0.2 slice.20
  149.8 0.0 collective-permute-done.3
  149.8 0.9 fusion.26
  150.7 3.4 fusion.10
  154.1 21.1 %all-gather.12.cloned.1.call-done = bf16[128,16,256]{2,1,0:T(8,128)(2,1)} async-done(((bf16[32,16,256]{2,1,0:T(8,128)(2,1)}), bf16[128,16,256]{2,1,0:T(8,128)(2,1)}) %all-gather.12.cloned.1.call-update) | async-done | bytes 1048592 | tf_op jit(solution)/shard_map/all_gather | solution.py:80
  175.2 1.0 dynamic-slice_bitcast_fusion
  176.2 16.1 %fusion.13 = bf16[32,2048,16]{1,2,0:T(8,128)(2,1)S(1)} fusion(bf16[32,16,256]{2,1,0:T(8,128)(2,1)S(1)} %dynamic-slice_bitcast_fusion, s32[32,2048]{1,0:T(8,128)S(1)} %bitcast.31), kind=kOutput, calls=%fused_computation.21 | convolution fusion | flops 554696704 | bytes 2621440 | tf_op jit(solution)/shard_map/lxg,lyg->lxy/dot_general | solution.py:86
  192.3 0.0 copy-done.1
  192.3 2.7 fusion.21
  195.0 1.5 copy.31
  196.5 0.0 all-gather.6.cloned.1.call-update
  196.6 0.2 reduce-scatter.5.cloned.1.call-start
  196.8 81.9 %all-gather.6.cloned.1.call-done = bf16[1024,4096]{0,1:T(8,128)(2,1)} async-done(((bf16[1024,512]{0,1:T(8,128)(2,1)}), bf16[1024,4096]{0,1:T(8,128)(2,1)}) %all-gather.6.cloned.1.call-update) | async-done | bytes 8388624 | tf_op jit(solution)/shard_map/all_gather | solution.py:103
  278.7 10.2 %convolution_convert_fusion.1 = bf16[4096,512]{1,0:T(8,128)(2,1)} fusion(bf16[1024,4096]{0,1:T(8,128)(2,1)} %all-gather.6.cloned.1.call-done, bf16[1024,512]{0,1:T(8,128)(2,1)} %bitcast.27), kind=kOutput, calls=%fused_computation.9 | convolution fusion | flops 4297064448 | bytes 13631488 | tf_op jit(solution)/shard_map/dot_general | solution.py:104
  288.9 0.0 reduce-scatter.5.cloned.1.call-update
  288.9 0.0 all-gather.8.cloned.1.call-start
  289.0 51.2 %reduce-scatter.5.cloned.1.call-done = bf16[1024,512]{1,0:T(8,128)(2,1)} async-done(((bf16[4096,512]{1,0:T(8,128)(2,1)}), bf16[1024,512]{1,0:T(8,128)(2,1)}) %reduce-scatter.5.cloned.1.call-update) | async-done | bytes 1048592 | tf_op jit(solution)/shard_map/reduce_scatter | solution.py:111
  340.2 0.0 all-gather.8.cloned.1.call-update
  340.2 0.0 all-gather.10.cloned.1.call-start
  340.2 2.4 multiply_reduce_fusion
  342.6 0.5 copy.32
  343.2 40.5 %psum.30 = f32[]{:T(128)} all-reduce(f32[]{:T(128)} %multiply_reduce_fusion), channel_id=1, replica_groups=mesh['dp'=8,'rot'=4] {'dp','rot'}, use_global_device_ids=true, to_apply=%region_6.7 | all-reduce | flops 1 | bytes 8 | tf_op jit(solution)/shard_map/psum | solution.py:116
  384.4 10.8 %all-gather.8.cloned.1.call-done = bf16[4096,512]{1,0:T(8,128)(2,1)} async-done(((bf16[1024,512]{1,0:T(8,128)(2,1)}), bf16[4096,512]{1,0:T(8,128)(2,1)}) %all-gather.8.cloned.1.call-update) | async-done | bytes 4194320 | tf_op jit(solution)/shard_map/all_gather | solution.py:96
  395.3 10.1 %multiply_convert_fusion.1 = bf16[1024,512]{1,0:T(8,128)(2,1)} fusion(bf16[1024,512]{1,0:T(8,128)(2,1)S(1)} %copy.32, bf16[1024,4096]{0,1:T(8,128)(2,1)} %all-gather.6.cloned.1.call-done, bf16[4096,512]{1,0:T(8,128)(2,1)} %all-gather.8.cloned.1.call-done, f32[]{:T(128)S(6)} %mul.79, f32[]{:T(128)S(6)} %div.24), kind=kOutput, calls=%fused_computation.31 | convolution fusion | flops 4298113024 | bytes 14680072 | tf_op jit(solution)/shard_map/dot_general | solution.py:94
  405.4 0.0 all-gather.10.cloned.1.call-update
  405.4 0.3 all-reduce.4.cloned.1.call-start
  405.7 81.9 %all-gather.10.cloned.1.call-done = bf16[1024,4096]{1,0:T(8,128)(2,1)} async-done(((bf16[1024,512]{1,0:T(8,128)(2,1)}), bf16[1024,4096]{1,0:T(8,128)(2,1)}) %all-gather.10.cloned.1.call-update) | async-done | bytes 8388624 | tf_op jit(solution)/shard_map/all_gather | solution.py:103
  487.6 10.1 %convolution_convert_fusion = bf16[4096,512]{1,0:T(8,128)(2,1)} fusion(bf16[1024,4096]{1,0:T(8,128)(2,1)} %all-gather.10.cloned.1.call-done, bf16[1024,512]{1,0:T(8,128)(2,1)} %multiply_convert_fusion.1), kind=kOutput, calls=%fused_computation.8 | convolution fusion | flops 4297064448 | bytes 13631488 | tf_op jit(solution)/shard_map/dot_general | solution.py:104
  497.7 0.0 all-reduce.4.cloned.1.call-update
  497.7 102.3 %all-reduce.4.cloned.1.call-done = bf16[4096,512]{1,0:T(8,128)(2,1)} async-done(((bf16[4096,512]{1,0:T(8,128)(2,1)}), bf16[4096,512]{1,0:T(8,128)(2,1)}) %all-reduce.4.cloned.1.call-update) | async-done | bytes 4194320 | tf_op jit(solution)/shard_map/psum | solution.py:113
  600.0 10.1 %multiply_convert_fusion = bf16[1024,512]{1,0:T(8,128)(2,1)} fusion(bf16[1024,512]{1,0:T(8,128)(2,1)S(1)} %copy-done.5, bf16[1024,4096]{1,0:T(8,128)(2,1)} %all-gather.10.cloned.1.call-done, bf16[4096,512]{1,0:T(8,128)(2,1)} %all-reduce.4.cloned.1.call-done), kind=kOutput, calls=%fused_computation.30 | convolution fusion | flops 4298113024 | bytes 14680064 | tf_op jit(solution)/shard_map/dot_general | solution.py:123
  (12 shorter events, 0.0 us)
Async XLA Ops:
  7.2 64.0 %reduce-scatter.3.cloned.1.call-start = ((), (), s32[]{:S(2)}) async-start(), calls=%async_computation.2 | async-start | bytes 5242880 | tf_op jit(solution)/shard_map/reduce_scatter | solution.py:59
  15.1 1.0 copy-start.6
  15.1 1.3 copy-start.7
  15.1 131.4 %all-reduce.6.cloned.1.call-start = ((), (), s32[]{:S(2)}) async-start(), calls=%async_computation.9 | async-start | bytes 2228224 | tf_op jit(solution)/shard_map/psum | solution.py:73
  27.5 17.8 %collective-permute-start = (bf16[256,1088]{0,1:T(8,128)(2,1)S(1)}, bf16[256,1088]{0,1:T(8,128)(2,1)S(1)}, u32[]{:S(2)}, u32[]{:S(2)}) collective-permute-start(bf16[256,1088]{0,1:T(8,128)(2,1)S(1)} %get-tuple-element.10), channel_id=1, source_target_pairs={{0,8},{4,12},{8,16},{12,20},{16,24},{20,28},{24,0},{28,4},{1,9},{5... | collective-permute-start | bytes 1671176 | tf_op jit(solution)/shard_map/ppermute | solution.py:48
  29.3 35.9 %collective-permute-start.1 = (bf16[256,1088]{0,1:T(8,128)(2,1)S(1)}, bf16[256,1088]{0,1:T(8,128)(2,1)S(1)}, u32[]{:S(2)}, u32[]{:S(2)}) collective-permute-start(bf16[256,1088]{0,1:T(8,128)(2,1)S(1)} %get-tuple-element.11), channel_id=1, source_target_pairs={{0,16},{4,20},{8,24},{12,28},{16,0},{20,4},{24,8},{28,12},{1,17},{... | collective-permute-start | bytes 1671176 | tf_op jit(solution)/shard_map/ppermute | solution.py:48
  32.3 33.0 %collective-permute-start.2 = (bf16[256,1088]{0,1:T(8,128)(2,1)S(1)}, bf16[256,1088]{0,1:T(8,128)(2,1)S(1)}, u32[]{:S(2)}, u32[]{:S(2)}) collective-permute-start(bf16[256,1088]{0,1:T(8,128)(2,1)S(1)} %get-tuple-element.12), channel_id=1, source_target_pairs={{0,24},{4,28},{8,0},{12,4},{16,8},{20,12},{24,16},{28,20},{1,25},{... | collective-permute-start | bytes 1671176 | tf_op jit(solution)/shard_map/ppermute | solution.py:48
  65.2 0.8 copy-start.2
  65.2 1.0 copy-start.3
  77.6 97.6 %all-gather.12.cloned.1.call-start = ((), (), s32[]{:S(2)}) async-start(), calls=%async_computation.8 | async-start | bytes 1310720 | tf_op jit(solution)/shard_map/all_gather | solution.py:80
  81.9 67.9 %collective-permute-start.3 = (bf16[1024,1056]{0,1:T(8,128)(2,1)}, bf16[1024,1056]{0,1:T(8,128)(2,1)}, u32[]{:S(2)}, u32[]{:S(2)}) collective-permute-start(bf16[1024,1056]{0,1:T(8,128)(2,1)} %fusion.19), channel_id=1, source_target_pairs={{0,4},{4,0},{8,12},{12,8},{16,20},{20,16},{24,28},{28,24},{1,5},{5... | collective-permute-start | bytes 6488072 | tf_op jit(solution)/shard_map/ppermute | solution.py:55
  148.7 2.0 copy-start.4
  149.5 129.2 %all-gather.6.cloned.1.call-start = ((), (), s32[]{:S(2)}) async-start(), calls=%async_computation.3 | async-start | bytes 9437184 | tf_op jit(solution)/shard_map/all_gather | solution.py:103
  176.2 16.1 %copy-start.1 = (bf16[2048,1024]{0,1:T(8,128)(2,1)S(1)}, bf16[2048,1024]{0,1:T(8,128)(2,1)}, u32[]{:S(2)}) copy-start(bf16[2048,1024]{0,1:T(8,128)(2,1)} %fusion.10) | copy-start | bytes 12582916
  196.6 143.6 %reduce-scatter.5.cloned.1.call-start = ((), (), s32[]{:S(2)}) async-start(), calls=%async_computation.4 | async-start | bytes 5242880 | tf_op jit(solution)/shard_map/reduce_scatter | solution.py:111
  288.9 53.7 %copy-start = (bf16[1024,32,16]{0,2,1:T(8,128)(2,1)S(1)}, bf16[1024,32,16]{0,2,1:T(8,128)(2,1)}, u32[]{:S(2)}) copy-start(bf16[1024,32,16]{0,2,1:T(8,128)(2,1)} %copy.31) | copy-start | bytes 3145732
  288.9 106.3 %all-gather.8.cloned.1.call-start = ((), (), s32[]{:S(2)}) async-start(), calls=%async_computation.5 | async-start | bytes 5242880 | tf_op jit(solution)/shard_map/all_gather | solution.py:96
  340.2 147.4 %all-gather.10.cloned.1.call-start = ((), (), s32[]{:S(2)}) async-start(), calls=%async_computation.6 | async-start | bytes 9437184 | tf_op jit(solution)/shard_map/all_gather | solution.py:103
  405.4 194.6 %all-reduce.4.cloned.1.call-start = ((), (), s32[]{:S(2)}) async-start(), calls=%async_computation.7 | async-start | bytes 8388608 | tf_op jit(solution)/shard_map/psum | solution.py:113
  497.7 102.3 %copy-start.5 = (bf16[1024,512]{1,0:T(8,128)(2,1)S(1)}, bf16[1024,512]{1,0:T(8,128)(2,1)}, u32[]{:S(2)}) copy-start(bf16[1024,512]{1,0:T(8,128)(2,1)} %multiply_convert_fusion.1) | copy-start | bytes 3145732
Sparse Core Ops, SparseCore 0:
  15.2 55.9 reduce-scatter.2
  77.7 68.7 all-reduce.5
  149.7 25.4 all-gather.11
  196.7 81.9 all-gather.5
  289.0 51.0 reduce-scatter.4
  341.9 53.3 all-gather.7
  405.5 82.0 all-gather.9
  497.9 102.0 all-reduce.3
